TPU v7x, 512 devices: a whole 4x4x16 slice. The times are simulated.
512 devices in a mesh: band: 16 (over y, x), pix: 32 (over z, core).
Axes of the slice: x: 4, y: 4, z: 16, core: 2. Of those that a mesh axis runs over, the one named last changes fastest.
Arguments:
- pixels: bfloat16 [512, 32, 1024], P('pix', 'band'), may hold values from -6 to 6
- clear_count: int32 [32], P('pix'), may hold values from 3 to 10, as said below
- clear_index: int32 [320], P('pix'), may hold values from 0 to 15, as said below
- attn_gain: float32 [1024], replicated, may hold values from 0.1 to 1.9
- w_query: bfloat16 [1024, 1024], P(None, 'band')
- w_key: bfloat16 [1024, 1024], P(None, 'band')
- w_value: bfloat16 [1024, 1024], P(None, 'band'), may hold values from -0.1875 to 0.1875
- w_out: bfloat16 [1024, 1024], P('band'), may hold values from -0.1875 to 0.1875
- mlp_gain: float32 [1024], replicated, may hold values from 0.1 to 1.9
- w_gate: bfloat16 [1024, 4096], P(None, 'band'), may hold values from -0.1875 to 0.1875
- w_up: bfloat16 [1024, 4096], P(None, 'band'), may hold values from -0.1875 to 0.1875
- w_down: bfloat16 [4096, 1024], P('band'), may hold values from -0.09375 to 0.09375
Outputs:
- updated: bfloat16 [512, 32, 1024], P('pix', 'band')
Inputs may be any that keep to these rules, and one draw needn't show every extreme that they name: `clear_count`: some tile, drawn from the seed, keeps exactly 10 clear pixels. `clear_index`: for tile t, entries t*10 to t*10+clear_count[t]-1 are distinct local pixel indices in rising order; the tile's remaining entries are 0.
All inputs are finite; a program needn't handle non-finite values.
Results may differ from a plain program's by a relative error of at most 0.019.
Values may be sent and summed in bfloat16 or wider, within the bound.
No kernel may reach another device: no remote copies, remote signals or barrier semaphores. Data moves between devices by JAX's collectives and lax.ppermute only.
A program may use at most 64 MiB of HBM per device.

v0:
```python
import jax
import jax.numpy as jnp
from jax import lax
from jax.sharding import PartitionSpec as P

HD = 64


def normed(rows, gain):
    full = rows.astype(jnp.float32)
    scaled = full * lax.rsqrt(jnp.mean(full * full, axis=-1, keepdims=True) + 1e-05)
    return (scaled * gain).astype(jnp.bfloat16)


def slot_live(number, slots_per_tile, counts):
    slot = jnp.arange(number, dtype=jnp.int32)
    owner = slot // slots_per_tile
    owned = owner[:, None] == jnp.arange(counts.shape[0], dtype=jnp.int32)[None, :]
    owner_count = jnp.sum(jnp.where(owned, counts[None, :], 0), axis=1)
    return slot % slots_per_tile < owner_count


def shards(
    pixels,
    clear_count,
    clear_index,
    attn_gain,
    w_query,
    w_key,
    w_value,
    w_out,
    mlp_gain,
    w_gate,
    w_up,
    w_down,
):
    own_count = clear_count[0]
    kept = jnp.take(pixels, clear_index, axis=0)
    kept_rows = jnp.swapaxes(kept, 0, 1)
    all_rows = lax.all_gather(kept_rows, "band", axis=0, tiled=True)
    spec, slots_here, width = all_rows.shape
    heads_here = w_query.shape[1] // HD
    flat = normed(all_rows, attn_gain).reshape(spec * slots_here, width)

    def project(weight):
        out = jnp.dot(flat, weight, preferred_element_type=jnp.float32).astype(jnp.bfloat16)
        return out.reshape(spec, slots_here, heads_here, HD)

    query = project(w_query)
    key = project(w_key)
    value = project(w_value)
    counts = lax.all_gather(clear_count, "pix", axis=0, tiled=True)
    start_top = jnp.full((spec, heads_here, slots_here), -1e30, jnp.float32)
    top = start_top
    key_piece = lax.all_gather(key, "pix", axis=1, tiled=True)
    value_piece = lax.all_gather(value, "pix", axis=1, tiled=True)
    live = slot_live(key_piece.shape[1], slots_here, counts)
    scores = jnp.einsum(
        "sqhd,skhd->shqk", query, key_piece, preferred_element_type=jnp.float32
    ) * HD ** (-0.5)
    masked = jnp.where(live[None, None, None, :], scores, -1e30)
    new_top = jnp.maximum(top, jnp.max(masked, axis=-1))
    expo = jnp.where(live[None, None, None, :], jnp.exp(masked - new_top[..., None]), 0.0)
    totals = jnp.sum(expo, axis=-1)
    mixed = jnp.einsum(
        "shqk,skhd->sqhd",
        expo.astype(jnp.bfloat16),
        value_piece,
        preferred_element_type=jnp.float32,
    )
    acc = mixed
    top, totals, acc = (new_top, totals, acc)
    context = (acc / jnp.transpose(totals, (0, 2, 1))[..., None]).astype(jnp.bfloat16)
    context_rows = context.reshape(spec, slots_here, heads_here * HD)
    spec_here = spec // lax.axis_size("band")
    piece = context_rows
    out = jnp.dot(
        piece.reshape(spec_here * lax.axis_size("band") * slots_here, heads_here * HD),
        w_out,
        preferred_element_type=jnp.float32,
    )
    attn_out = lax.psum_scatter(
        out.reshape(spec_here * lax.axis_size("band"), slots_here, width).astype(jnp.bfloat16),
        "band",
        scatter_dimension=0,
        tiled=True,
    ).astype(jnp.float32)
    state = (kept_rows.astype(jnp.float32) + attn_out).astype(jnp.bfloat16)
    mlp_in = lax.all_gather(normed(state, mlp_gain), "band", axis=0, tiled=True)
    piece = mlp_in.reshape(spec_here * lax.axis_size("band") * slots_here, width)
    gate = jnp.dot(piece, w_gate, preferred_element_type=jnp.float32)
    upper = jnp.dot(piece, w_up, preferred_element_type=jnp.float32)
    hidden = (jax.nn.silu(gate) * upper).astype(jnp.bfloat16)
    out = jnp.dot(hidden, w_down, preferred_element_type=jnp.float32)
    mlp_out = lax.psum_scatter(
        out.reshape(spec_here * lax.axis_size("band"), slots_here, width).astype(jnp.bfloat16),
        "band",
        scatter_dimension=0,
        tiled=True,
    ).astype(jnp.float32)
    encoded = (state.astype(jnp.float32) + mlp_out).astype(jnp.bfloat16)
    live_here = jnp.arange(slots_here, dtype=jnp.int32) < own_count
    chosen = (
        jnp.arange(pixels.shape[0], dtype=jnp.int32)[:, None] == clear_index[None, :]
    ) & live_here[None, :]
    placed = jnp.einsum(
        "pc,scd->psd", chosen.astype(jnp.bfloat16), encoded, preferred_element_type=jnp.float32
    ).astype(jnp.bfloat16)
    taken = jnp.any(chosen, axis=1)
    return jnp.where(taken[:, None, None], placed, pixels)


def solution(mesh):
    return jax.shard_map(
        shards,
        mesh=mesh,
        in_specs=(
            P("pix", "band", None),
            P("pix"),
            P("pix"),
            P(),
            P(None, "band"),
            P(None, "band"),
            P(None, "band"),
            P("band", None),
            P(),
            P(None, "band"),
            P(None, "band"),
            P("band", None),
        ),
        out_specs=P("pix", "band", None),
        check_vma=False,
    )
```

profile of v0, /device:TPU:2, one launch (start us, length us, event | category | flops | bytes accessed | tf_op | source)
XLA Modules:
  0.0 454.2 jit_solution(5196698798898972980)
XLA Ops:
  6.5 0.7 compare_select_fusion
  7.3 0.7 compare_and_fusion
  7.9 1.5 gather_fusion
  9.6 27.7 %all_gather.15 = bf16[32,10,1024]{2,1,0:T(8,128)(2,1)S(1)} all-gather(bf16[2,10,1024]{2,1,0:T(8,128)(2,1)S(1)} %copy.59), channel_id=1, replica_groups=mesh['band'=16,'pix'=32] {'band'}, dimensions={0}, use_global_device_ids=true | all-gather | bytes 696320 | tf_op jit(solution)/shard_map/all_gather | solution.py:40
  39.0 0.7 copy.65
  40.3 0.7 copy.61
  42.2 1.3 dynamic-slice
  43.5 0.7 dynamic-update-slice
  44.2 24.1 %all-reduce = s32[32]{0:T(128)S(1)} all-reduce(s32[32]{0:T(128)S(1)} %dynamic-update-slice), channel_id=1, replica_groups=mesh['band'=16,'pix'=32] {'pix'}, use_global_device_ids=true, to_apply=%add | all-reduce | flops 32 | bytes 256
  68.4 43.2 %all-gather.5.cloned.1.call-done = bf16[32,320,1,64]{3,0,2,1:T(8,128)(2,1)} async-done(((bf16[32,10,1,64]{3,0,2,1:T(8,128)(2,1)}), bf16[32,320,1,64]{3,0,2,1:T(8,128)(2,1)}) %all-gather.5.cloned.1.call-update) | async-done | bytes 1310736 | tf_op jit(solution)/shard_map/all_gather | solution.py:55
  111.6 4.4 copy.66
  116.8 65.8 %all-gather.3.cloned.1.call-done = bf16[32,320,1,64]{3,0,2,1:T(8,128)(2,1)} async-done(((bf16[32,10,1,64]{3,0,2,1:T(8,128)(2,1)}), bf16[32,320,1,64]{3,0,2,1:T(8,128)(2,1)}) %all-gather.3.cloned.1.call-update) | async-done | bytes 1310736 | tf_op jit(solution)/shard_map/all_gather | solution.py:56
  182.7 4.4 copy.62
  187.1 0.7 fusion.24
  188.0 1.2 convolution_convert_fusion
  189.3 1.3 dynamic-slice.1
  191.2 110.8 %all-reduce.6.cloned.1.call-done = bf16[32,10,1024]{2,0,1:T(8,128)(2,1)} async-done(((bf16[32,10,1024]{2,0,1:T(8,128)(2,1)}), bf16[32,10,1024]{2,0,1:T(8,128)(2,1)}) %all-reduce.6.cloned.1.call-update) | async-done | bytes 655376
  302.0 1.1 fusion.40
  303.3 23.2 %all_gather.19 = bf16[32,10,1024]{2,1,0:T(8,128)(2,1)S(1)} all-gather(bf16[2,10,1024]{2,1,0:T(8,128)(2,1)S(1)} %copy.68), channel_id=1, replica_groups=mesh['band'=16,'pix'=32] {'band'}, dimensions={0}, use_global_device_ids=true | all-gather | bytes 696320 | tf_op jit(solution)/shard_map/all_gather | solution.py:89
  327.6 0.9 convolution_convert_fusion.1
  328.7 1.2 copy.69
  330.0 115.7 %all-reduce.8.cloned.1.call-done = bf16[32,10,1024]{2,0,1:T(8,128)(2,1)} async-done(((bf16[32,10,1024]{2,0,1:T(8,128)(2,1)}), bf16[32,10,1024]{2,0,1:T(8,128)(2,1)}) %all-reduce.8.cloned.1.call-update) | async-done | bytes 655376
  445.8 1.0 fusion.43
  446.9 0.7 copy.72
  (62 shorter events, 5.8 us)
Async XLA Ops:
  6.5 320.6 %copy-start = (bf16[256,1024]{1,0:T(8,128)(2,1)S(1)}, bf16[256,1024]{1,0:T(8,128)(2,1)}, u32[]{:S(2)}) copy-start(bf16[256,1024]{1,0:T(8,128)(2,1)} %param.23) | copy-start | bytes 1572868
  6.5 31.1 %copy-start.7 = (f32[1024]{0:T(1024)S(1)}, f32[1024]{0:T(1024)}, u32[]{:S(2)}) copy-start(f32[1024]{0:T(1024)} %param.15) | copy-start | bytes 12292
  6.5 105.1 %all-gather.5.cloned.1.call-start = ((), (), s32[]{:S(2)}) async-start(), calls=%async_computation.1 | async-start | bytes 2703360 | tf_op jit(solution)/shard_map/all_gather | solution.py:55
  37.6 0.9 copy-start.2
  37.9 1.8 copy-start.3
  38.5 2.5 copy-start.4
  39.7 142.9 %all-gather.3.cloned.1.call-start = ((), (), s32[]{:S(2)}) async-start(), calls=%async_computation | async-start | bytes 2703360 | tf_op jit(solution)/shard_map/all_gather | solution.py:56
  41.0 261.0 %all-reduce.6.cloned.1.call-start = ((), (), s32[]{:S(2)}) async-start(), calls=%async_computation.2 | async-start | bytes 1310720
  187.1 0.9 copy-start.5
  188.0 115.2 %copy-start.8 = (f32[1024]{0:T(1024)S(1)}, f32[1024]{0:T(1024)}, u32[]{:S(2)}) copy-start(f32[1024]{0:T(1024)} %param.20) | copy-start | bytes 12292
  189.2 256.6 %all-reduce.8.cloned.1.call-start = ((), (), s32[]{:S(2)}) async-start(), calls=%async_computation.3 | async-start | bytes 1310720
  191.2 135.5 %copy-start.1 = (bf16[1024,256]{1,0:T(8,128)(2,1)S(1)}, bf16[1024,256]{1,0:T(8,128)(2,1)}, u32[]{:S(2)}) copy-start(bf16[1024,256]{1,0:T(8,128)(2,1)} %param.21) | copy-start | bytes 1572868
  326.5 1.0 copy-start.9
  328.6 1.3 copy-start.10
  328.6 118.1 %copy-start.6 = (bf16[16,2,1024]{2,1,0:T(2,128)(2,1)S(1)}, bf16[16,2,1024]{2,1,0:T(2,128)(2,1)}, u32[]{:S(2)}) copy-start(bf16[16,2,1024]{2,1,0:T(2,128)(2,1)} %param.12) | copy-start | bytes 196612
Sparse Core Ops, SparseCore 0:
  39.8 71.7 all-gather.4
  113.7 68.9 all-gather.2
  189.3 112.6 all-reduce.5
  330.0 115.7 all-reduce.7
where the time goes:
time: 455 us; the launch traced here: 454 us
  waiting for transfers between devices  336 us (74%)
  blocking collectives  75 us (16%)
  local copies, waits for them, and re-layouts  19 us (4%)
  between operations  14.7 us (3%)
  other arithmetic  4.92 us (1%)
  matrix products  4.72 us (1%)
    unnamed x6, waiting for transfers between devices  227 us
    all_gather x1, waiting for transfers between devices, shards(): value_piece = lax.all_gather(value, 'pix', axis=1, tiled=True)  65.8 us
    all_gather x1, waiting for transfers between devices, shards(): key_piece = lax.all_gather(key, 'pix', axis=1, tiled=True)  43.2 us
    all_gather x1, blocking collectives, shards(): all_rows = lax.all_gather(kept_rows, 'band', axis=0, tiled=True)  27.7 us
    unnamed x1, blocking collectives  24.1 us
    all_gather x1, blocking collectives, shards(): mlp_in = lax.all_gather(normed(state, mlp_gain), 'band', axis=0, tiled=True)  23.2 us
  transfers between devices with their start and end apart: 4, of which 4 were waited for; matrix products, arithmetic and copies ran while one was open for 2% of the time, Pallas kernels for 0%

commit v1 on v0

v1 whole, which is shorter than its diff:
```python
import jax
import jax.numpy as jnp
from jax import lax
from jax.sharding import PartitionSpec as P

HD = 64


def normed(rows, gain):
    full = rows.astype(jnp.float32)
    scaled = full * lax.rsqrt(jnp.mean(full * full, axis=-1, keepdims=True) + 1e-05)
    return (scaled * gain).astype(jnp.bfloat16)


def band_gather(rows):
    n = lax.axis_size("band")
    sent = jnp.broadcast_to(rows[None], (n,) + rows.shape)
    got = lax.all_to_all(sent, "band", 0, 0, tiled=True)
    return got.reshape((n * rows.shape[0],) + rows.shape[1:])


def band_reduce(part):
    n = lax.axis_size("band")
    split = part.reshape((n, part.shape[0] // n) + part.shape[1:])
    got = lax.all_to_all(split, "band", 0, 0, tiled=True)
    return jnp.sum(got.astype(jnp.float32), axis=0)


def shards(
    pixels,
    clear_count,
    clear_index,
    attn_gain,
    w_query,
    w_key,
    w_value,
    w_out,
    mlp_gain,
    w_gate,
    w_up,
    w_down,
):
    own_count = clear_count[0]
    n_pix = lax.axis_size("pix")
    kept = jnp.take(pixels, clear_index, axis=0)
    kept_rows = jnp.swapaxes(kept, 0, 1)
    spec_here, slots_here, width = kept_rows.shape
    attn_in = band_gather(normed(kept_rows, attn_gain))
    spec = attn_in.shape[0]
    flat = attn_in.reshape(spec * slots_here, width)
    heads_here = w_query.shape[1] // HD

    def project(weight):
        out = jnp.dot(flat, weight, preferred_element_type=jnp.float32).astype(jnp.bfloat16)
        return out.reshape(spec, slots_here, heads_here * HD)

    live_here = jnp.arange(slots_here, dtype=jnp.int32) < own_count
    flag = jnp.broadcast_to(
        live_here.astype(jnp.bfloat16)[None, :, None], (spec, slots_here, heads_here * HD)
    )
    payload = jnp.concatenate([project(w_query), project(w_key), project(w_value), flag], axis=-1)
    mine = lax.all_to_all(payload, "pix", 0, 1, tiled=True)
    spec_mine = mine.shape[0]
    slots = mine.shape[1]
    q = mine[..., 0 * HD : heads_here * HD].reshape(spec_mine, slots, heads_here, HD)
    k = mine[..., heads_here * HD : 2 * heads_here * HD].reshape(spec_mine, slots, heads_here, HD)
    v = mine[..., 2 * heads_here * HD : 3 * heads_here * HD].reshape(spec_mine, slots, heads_here, HD)
    live = mine[0, :, 3 * heads_here * HD] > 0.5
    scores = jnp.einsum("sqhd,skhd->shqk", q, k, preferred_element_type=jnp.float32) * HD ** (-0.5)
    masked = jnp.where(live[None, None, None, :], scores, -1e30)
    top = jnp.max(masked, axis=-1)
    expo = jnp.where(live[None, None, None, :], jnp.exp(masked - top[..., None]), 0.0)
    totals = jnp.sum(expo, axis=-1)
    mixed = jnp.einsum(
        "shqk,skhd->sqhd", expo.astype(jnp.bfloat16), v, preferred_element_type=jnp.float32
    )
    context = (mixed / jnp.transpose(totals, (0, 2, 1))[..., None]).astype(jnp.bfloat16)
    context = context.reshape(spec_mine, slots, heads_here * HD)
    context_rows = lax.all_to_all(context, "pix", 1, 0, tiled=True)
    out = jnp.dot(
        context_rows.reshape(spec * slots_here, heads_here * HD),
        w_out,
        preferred_element_type=jnp.float32,
    ).astype(jnp.bfloat16)
    attn_out = band_reduce(out.reshape(spec, slots_here, width))
    state = (kept_rows.astype(jnp.float32) + attn_out).astype(jnp.bfloat16)
    mlp_in = band_gather(normed(state, mlp_gain))
    piece = mlp_in.reshape(spec * slots_here, width)
    gate = jnp.dot(piece, w_gate, preferred_element_type=jnp.float32)
    upper = jnp.dot(piece, w_up, preferred_element_type=jnp.float32)
    hidden = (jax.nn.silu(gate) * upper).astype(jnp.bfloat16)
    out = jnp.dot(hidden, w_down, preferred_element_type=jnp.float32).astype(jnp.bfloat16)
    mlp_out = band_reduce(out.reshape(spec, slots_here, width))
    encoded = (state.astype(jnp.float32) + mlp_out).astype(jnp.bfloat16)
    chosen = (
        jnp.arange(pixels.shape[0], dtype=jnp.int32)[:, None] == clear_index[None, :]
    ) & live_here[None, :]
    placed = jnp.einsum(
        "pc,scd->psd", chosen.astype(jnp.bfloat16), encoded, preferred_element_type=jnp.float32
    ).astype(jnp.bfloat16)
    taken = jnp.any(chosen, axis=1)
    return jnp.where(taken[:, None, None], placed, pixels)


def solution(mesh):
    return jax.shard_map(
        shards,
        mesh=mesh,
        in_specs=(
            P("pix", "band", None),
            P("pix"),
            P("pix"),
            P(),
            P(None, "band"),
            P(None, "band"),
            P(None, "band"),
            P("band", None),
            P(),
            P(None, "band"),
            P(None, "band"),
            P("band", None),
        ),
        out_specs=P("pix", "band", None),
        check_vma=False,
    )
```

time: 455 us -> 139 us (0.31)
  the two profiles are of different devices: /device:TPU:2 before, /device:TPU:64 now
where the time goes in v1:
time: 139 us; the launch traced here: 138 us
  blocking collectives  83.2 us (60%)
  waiting for transfers between devices  23.6 us (17%)
  local copies, waits for them, and re-layouts  11.1 us (8%)
  starting transfers between devices  10.8 us (8%)
  other arithmetic  5.35 us (4%)
  matrix products  3.29 us (2%)
    all_to_all x1, blocking collectives, shards(): mine = lax.all_to_all(payload, 'pix', 0, 1, tiled=True)  33.5 us
    all_to_all x1, blocking collectives, shards(): context_rows = lax.all_to_all(context, 'pix', 1, 0, tiled=True)  18 us
    all_to_all x1, blocking collectives, band_reduce(): got = lax.all_to_all(split, 'band', 0, 0, tiled=True)  16.2 us
    all_to_all x1, blocking collectives, band_gather(): got = lax.all_to_all(sent, 'band', 0, 0, tiled=True)  15.6 us
    all_to_all x1, waiting for transfers between devices, band_gather(): got = lax.all_to_all(sent, 'band', 0, 0, tiled=True)  12.3 us
    all_to_all x1, waiting for transfers between devices, band_reduce(): got = lax.all_to_all(split, 'band', 0, 0, tiled=True)  11.3 us
    all_to_all x1, starting transfers between devices, band_gather(): got = lax.all_to_all(sent, 'band', 0, 0, tiled=True)  7.03 us
    all_to_all x1, starting transfers between devices, band_reduce(): got = lax.all_to_all(split, 'band', 0, 0, tiled=True)  3.72 us
  transfers between devices with their start and end apart: 2, of which 2 were waited for; matrix products, arithmetic and copies ran while one was open for 0% of the time, Pallas kernels for 0%

profile of v1, /device:TPU:64, one launch (start us, length us, event | category | flops | bytes accessed | tf_op | source)
XLA Modules:
  0.0 138.3 jit_solution(6909444645363471676)
XLA Ops:
  0.0 0.7 compare_select_fusion
  0.7 0.7 compare_and_fusion
  1.4 1.5 %gather_fusion = bf16[10,2,1024]{2,1,0:T(2,128)(2,1)S(1)} fusion(bf16[16,2,1024]{2,1,0:T(2,128)(2,1)} %param.12, s32[1024]{0:T(1024)S(1)} %pad_clamp_fusion), kind=kCustom, calls=%fused_computation | custom fusion | bytes 81960 | tf_op jit(solution)/shard_map/jit(_take)/gather | solution.py:45
  3.1 0.8 fusion.24
  3.9 1.2 broadcast_in_dim.71
  5.1 7.0 %all-to-all-start = ((bf16[16,2,10,1024]{3,1,2,0:T(2,128)(2,1)}), bf16[16,2,10,1024]{3,1,2,0:T(2,128)(2,1)S(1)}, u32[]{:S(2)}, u32[]{:S(2)}) async-start(bf16[16,2,10,1024]{3,1,2,0:T(2,128)(2,1)} %broadcast_in_dim.71), calls=%async_computation | async-start | bytes 1310720 | tf_op jit(solution)/shard_map/all_to_all | solution.py:18
  12.8 12.3 %all-to-all-done = bf16[16,2,10,1024]{3,1,2,0:T(2,128)(2,1)S(1)} async-done(((bf16[16,2,10,1024]{3,1,2,0:T(2,128)(2,1)}), bf16[16,2,10,1024]{3,1,2,0:T(2,128)(2,1)S(1)}, u32[]{:S(2)}, u32[]{:S(2)}) %all-to-all-start) | async-done | bytes 655392 | tf_op jit(solution)/shard_map/all_to_all | solution.py:18
  25.5 0.6 copy-done.2
  28.0 33.5 %all_to_all.41 = bf16[32,10,256]{2,1,0:T(8,128)(2,1)S(1)} all-to-all(bf16[32,10,256]{2,1,0:T(8,128)(2,1)S(1)} %pad_maximum_fusion), channel_id=1, replica_groups=mesh['band'=16,'pix'=32] {'pix'}, dimensions={0} | all-to-all | bytes 327680 | tf_op jit(solution)/shard_map/all_to_all | solution.py:62
  62.7 0.6 broadcast.89
  63.3 1.2 reduce.6
  64.6 18.0 %all_to_all.42 = bf16[32,2,320]{2,1,0:T(2,128)(2,1)S(1)} all-to-all(bf16[32,2,320]{2,1,0:T(2,128)(2,1)S(1)} %reshape.121), channel_id=1, replica_groups=mesh['band'=16,'pix'=32] {'pix'}, dimensions={0} | all-to-all | bytes 81920 | tf_op jit(solution)/shard_map/all_to_all | solution.py:79
  83.4 0.7 copy.70
  84.1 16.2 %all_to_all.43 = bf16[16,2,10,1024]{3,1,2,0:T(2,128)(2,1)S(1)} all-to-all(bf16[16,2,10,1024]{3,1,2,0:T(2,128)(2,1)S(1)} %copy.70), channel_id=1, replica_groups=mesh['band'=16,'pix'=32] {'band'}, dimensions={0} | all-to-all | bytes 1310720 | tf_op jit(solution)/shard_map/all_to_all | solution.py:25
  100.3 0.4 convert_reduce_fusion.1
  101.3 15.6 %all_to_all.44 = bf16[16,2,10,1024]{3,1,2,0:T(2,128)(2,1)S(1)} all-to-all(bf16[16,2,10,1024]{3,1,2,0:T(2,128)(2,1)S(1)} %broadcast_in_dim.76), channel_id=1, replica_groups=mesh['band'=16,'pix'=32] {'band'}, dimensions={0} | all-to-all | bytes 1310720 | tf_op jit(solution)/shard_map/all_to_all | solution.py:18
  117.4 0.8 copy-done.1
  118.5 0.7 copy-done.8
  119.2 0.9 convolution_convert_fusion.1
  120.3 1.5 %copy.75 = bf16[16,2,10,1024]{3,1,2,0:T(2,128)(2,1)} copy(bf16[16,2,10,1024]{3,2,1,0:T(8,128)(2,1)S(1)} %reshape_reshape.15) | data formatting | bytes 1310720 | tf_op jit(solution)/shard_map/reshape;reshape | solution.py:24
  121.8 3.7 %all-to-all-start.5 = ((bf16[16,2,10,1024]{3,1,2,0:T(2,128)(2,1)}), bf16[16,2,10,1024]{3,1,2,0:T(2,128)(2,1)S(1)}, u32[]{:S(2)}, u32[]{:S(2)}) async-start(bf16[16,2,10,1024]{3,1,2,0:T(2,128)(2,1)} %copy.75), calls=%async_computation.5 | async-start | bytes 1310720 | tf_op jit(solution)/shard_map/all_to_all | solution.py:25
  125.7 11.3 %all-to-all-done.5 = bf16[16,2,10,1024]{3,1,2,0:T(2,128)(2,1)S(1)} async-done(((bf16[16,2,10,1024]{3,1,2,0:T(2,128)(2,1)}), bf16[16,2,10,1024]{3,1,2,0:T(2,128)(2,1)S(1)}, u32[]{:S(2)}, u32[]{:S(2)}) %all-to-all-start.5) | async-done | bytes 655392 | tf_op jit(solution)/shard_map/all_to_all | solution.py:25
  137.0 0.4 convert_reduce_fusion
  137.6 0.7 copy.81
  (57 shorter events, 6.5 us)
Async XLA Ops:
  0.0 118.5 %copy-start = (bf16[256,1024]{1,0:T(8,128)(2,1)S(1)}, bf16[256,1024]{1,0:T(8,128)(2,1)}, u32[]{:S(2)}) copy-start(bf16[256,1024]{1,0:T(8,128)(2,1)} %param.23) | copy-start | bytes 1572868
  5.1 20.0 %all-to-all-start = ((bf16[16,2,10,1024]{3,1,2,0:T(2,128)(2,1)}), bf16[16,2,10,1024]{3,1,2,0:T(2,128)(2,1)S(1)}, u32[]{:S(2)}, u32[]{:S(2)}) async-start(bf16[16,2,10,1024]{3,1,2,0:T(2,128)(2,1)} %broadcast_in_dim.71), calls=%async_computation | async-start | bytes 1310720 | tf_op jit(solution)/shard_map/all_to_all | solution.py:18
  25.3 0.9 copy-start.2
  25.3 1.4 %copy-start.3 = (bf16[1024,64]{0,1:T(8,128)(2,1)S(1)}, bf16[1024,64]{0,1:T(8,128)(2,1)}, u32[]{:S(2)}) copy-start(bf16[1024,64]{0,1:T(8,128)(2,1)} %param.17) | copy-start | bytes 393220
  26.2 1.1 copy-start.4
  62.2 20.6 %copy-start.5 = (bf16[64,1024]{1,0:T(8,128)(2,1)S(1)}, bf16[64,1024]{1,0:T(8,128)(2,1)}, u32[]{:S(2)}) copy-start(bf16[64,1024]{1,0:T(8,128)(2,1)} %param.19) | copy-start | bytes 393220
  84.1 16.8 %copy-start.7 = (f32[1024]{0:T(1024)S(1)}, f32[1024]{0:T(1024)}, u32[]{:S(2)}) copy-start(f32[1024]{0:T(1024)} %param.20) | copy-start | bytes 12292
  117.1 1.0 copy-start.1
  118.2 1.0 copy-start.8
  121.8 3.8 %copy-start.9 = (s32[10]{0:T(128)S(1)}, s32[10]{0:T(128)}, u32[]{:S(2)}) copy-start(s32[10]{0:T(128)} %param.14) | copy-start | bytes 124
  121.8 15.6 %copy-start.6 = (bf16[16,2,1024]{2,1,0:T(2,128)(2,1)S(1)}, bf16[16,2,1024]{2,1,0:T(2,128)(2,1)}, u32[]{:S(2)}) copy-start(bf16[16,2,1024]{2,1,0:T(2,128)(2,1)} %param.12) | copy-start | bytes 196612
  121.8 15.2 %all-to-all-start.5 = ((bf16[16,2,10,1024]{3,1,2,0:T(2,128)(2,1)}), bf16[16,2,10,1024]{3,1,2,0:T(2,128)(2,1)S(1)}, u32[]{:S(2)}, u32[]{:S(2)}) async-start(bf16[16,2,10,1024]{3,1,2,0:T(2,128)(2,1)} %copy.75), calls=%async_computation.5 | async-start | bytes 1310720 | tf_op jit(solution)/shard_map/all_to_all | solution.py:25

commit v2 on v1

--- a/solution.py
+++ b/solution.py
@@ -1,7 +1,7 @@
 import jax
 import jax.numpy as jnp
 from jax import lax
-from jax.sharding import PartitionSpec as P
+from jax.sharding import Mesh, PartitionSpec as P
 
 HD = 64
 
@@ -41,7 +41,6 @@
     w_down,
 ):
     own_count = clear_count[0]
-    n_pix = lax.axis_size("pix")
     kept = jnp.take(pixels, clear_index, axis=0)
     kept_rows = jnp.swapaxes(kept, 0, 1)
     spec_here, slots_here, width = kept_rows.shape
@@ -55,17 +54,22 @@
         return out.reshape(spec, slots_here, heads_here * HD)
 
     live_here = jnp.arange(slots_here, dtype=jnp.int32) < own_count
-    flag = jnp.broadcast_to(
-        live_here.astype(jnp.bfloat16)[None, :, None], (spec, slots_here, heads_here * HD)
-    )
-    payload = jnp.concatenate([project(w_query), project(w_key), project(w_value), flag], axis=-1)
-    mine = lax.all_to_all(payload, "pix", 0, 1, tiled=True)
+    qkv = jnp.concatenate([project(w_query), project(w_key), project(w_value)], axis=-1)
+    width_qkv = qkv.shape[-1]
+    flag_row = jnp.zeros((spec, 1, width_qkv), jnp.bfloat16)
+    flag_row = flag_row.at[:, 0, :slots_here].set(live_here.astype(jnp.bfloat16)[None, :])
+    payload = jnp.concatenate([qkv, flag_row], axis=1)
+    mine = lax.all_to_all(payload, "z", 0, 1, tiled=True)
+    mine = lax.all_to_all(mine, "c", 0, 1, tiled=True)
+    n_z, n_c = lax.axis_size("z"), lax.axis_size("c")
     spec_mine = mine.shape[0]
-    slots = mine.shape[1]
-    q = mine[..., 0 * HD : heads_here * HD].reshape(spec_mine, slots, heads_here, HD)
-    k = mine[..., heads_here * HD : 2 * heads_here * HD].reshape(spec_mine, slots, heads_here, HD)
-    v = mine[..., 2 * heads_here * HD : 3 * heads_here * HD].reshape(spec_mine, slots, heads_here, HD)
-    live = mine[0, :, 3 * heads_here * HD] > 0.5
+    mine = mine.reshape(spec_mine, n_c * n_z, slots_here + 1, width_qkv)
+    live = (mine[0, :, slots_here, :slots_here] > 0.5).reshape(-1)
+    rows = mine[:, :, :slots_here].reshape(spec_mine, n_c * n_z * slots_here, width_qkv)
+    slots = rows.shape[1]
+    q = rows[..., 0 * HD : heads_here * HD].reshape(spec_mine, slots, heads_here, HD)
+    k = rows[..., heads_here * HD : 2 * heads_here * HD].reshape(spec_mine, slots, heads_here, HD)
+    v = rows[..., 2 * heads_here * HD : 3 * heads_here * HD].reshape(spec_mine, slots, heads_here, HD)
     scores = jnp.einsum("sqhd,skhd->shqk", q, k, preferred_element_type=jnp.float32) * HD ** (-0.5)
     masked = jnp.where(live[None, None, None, :], scores, -1e30)
     top = jnp.max(masked, axis=-1)
@@ -75,8 +79,9 @@
         "shqk,skhd->sqhd", expo.astype(jnp.bfloat16), v, preferred_element_type=jnp.float32
     )
     context = (mixed / jnp.transpose(totals, (0, 2, 1))[..., None]).astype(jnp.bfloat16)
-    context = context.reshape(spec_mine, slots, heads_here * HD)
-    context_rows = lax.all_to_all(context, "pix", 1, 0, tiled=True)
+    context = context.reshape(spec_mine, n_c, n_z, slots_here, heads_here * HD)
+    context = jnp.swapaxes(context, 1, 2).reshape(spec_mine, slots, heads_here * HD)
+    context_rows = lax.all_to_all(context, ("z", "c"), 1, 0, tiled=True)
     out = jnp.dot(
         context_rows.reshape(spec * slots_here, heads_here * HD),
         w_out,
@@ -103,13 +108,16 @@
 
 
 def solution(mesh):
+    n_band, n_pix = mesh.devices.shape
+    split = Mesh(mesh.devices.reshape(n_band, n_pix // 2, 2), ("band", "z", "c"))
+    pix = ("z", "c")
     return jax.shard_map(
         shards,
-        mesh=mesh,
+        mesh=split,
         in_specs=(
-            P("pix", "band", None),
-            P("pix"),
-            P("pix"),
+            P(pix, "band", None),
+            P(pix),
+            P(pix),
             P(),
             P(None, "band"),
             P(None, "band"),
@@ -120,6 +128,6 @@
             P(None, "band"),
             P("band", None),
         ),
-        out_specs=P("pix", "band", None),
+        out_specs=P(pix, "band", None),
         check_vma=False,
     )

time: 139 us -> 141 us (1.014)
  blocking collectives: 83.2 us -> 85.1 us
    all_to_all x2 -> x3, blocking collectives: 51.4 us -> 52.3 us  [the longest x1 31.5 us: shards(): mine = lax.all_to_all(payload, 'z', 0, 1, tiled=True)]
where the time goes in v2:
time: 141 us; the launch traced here: 140 us
  blocking collectives  85.1 us (60%)
  waiting for transfers between devices  23.6 us (17%)
  local copies, waits for them, and re-layouts  11.4 us (8%)
  starting transfers between devices  10.8 us (8%)
  other arithmetic  5.16 us (4%)
  matrix products  3.28 us (2%)
    all_to_all x1, blocking collectives, shards(): mine = lax.all_to_all(payload, 'z', 0, 1, tiled=True)  31.5 us
    all_to_all x1, blocking collectives, band_reduce(): got = lax.all_to_all(split, 'band', 0, 0, tiled=True)  17.2 us
    all_to_all x1, blocking collectives, shards(): context_rows = lax.all_to_all(context, ('z', 'c'), 1, 0, tiled=True)  16.9 us
    all_to_all x1, blocking collectives, band_gather(): got = lax.all_to_all(sent, 'band', 0, 0, tiled=True)  15.6 us
    all_to_all x1, waiting for transfers between devices, band_gather(): got = lax.all_to_all(sent, 'band', 0, 0, tiled=True)  12.3 us
    all_to_all x1, waiting for transfers between devices, band_reduce(): got = lax.all_to_all(split, 'band', 0, 0, tiled=True)  11.3 us
    all_to_all x1, starting transfers between devices, band_gather(): got = lax.all_to_all(sent, 'band', 0, 0, tiled=True)  7.03 us
    all_to_all x1, blocking collectives, shards(): mine = lax.all_to_all(mine, 'c', 0, 1, tiled=True)  3.87 us
  transfers between devices with their start and end apart: 2, of which 2 were waited for; matrix products, arithmetic and copies ran while one was open for 0% of the time, Pallas kernels for 0%

profile of v2, /device:TPU:64, one launch (start us, length us, event | category | flops | bytes accessed | tf_op | source)
XLA Modules:
  0.0 140.3 jit_solution(6600643705289486313)
XLA Ops:
  0.0 0.7 compare_select_fusion
  0.7 0.7 compare_and_fusion
  1.4 1.5 %gather_fusion = bf16[10,2,1024]{2,1,0:T(2,128)(2,1)S(1)} fusion(bf16[16,2,1024]{2,1,0:T(2,128)(2,1)} %param.14, s32[1024]{0:T(1024)S(1)} %pad_clamp_fusion), kind=kCustom, calls=%fused_computation | custom fusion | bytes 81960 | tf_op jit(solution)/shard_map/jit(_take)/gather | solution.py:44
  3.1 0.8 fusion.24
  3.9 1.2 broadcast_in_dim.68
  5.1 7.0 %all-to-all-start = ((bf16[16,2,10,1024]{3,1,2,0:T(2,128)(2,1)}), bf16[16,2,10,1024]{3,1,2,0:T(2,128)(2,1)S(1)}, u32[]{:S(2)}, u32[]{:S(2)}) async-start(bf16[16,2,10,1024]{3,1,2,0:T(2,128)(2,1)} %broadcast_in_dim.68), calls=%async_computation | async-start | bytes 1310720 | tf_op jit(solution)/shard_map/all_to_all | solution.py:18
  12.8 12.3 %all-to-all-done = bf16[16,2,10,1024]{3,1,2,0:T(2,128)(2,1)S(1)} async-done(((bf16[16,2,10,1024]{3,1,2,0:T(2,128)(2,1)}), bf16[16,2,10,1024]{3,1,2,0:T(2,128)(2,1)S(1)}, u32[]{:S(2)}, u32[]{:S(2)}) %all-to-all-start) | async-done | bytes 655392 | tf_op jit(solution)/shard_map/all_to_all | solution.py:18
  25.5 0.6 copy-done.2
  28.0 31.5 %all_to_all.56 = bf16[32,11,192]{2,1,0:T(8,128)(2,1)S(1)} all-to-all(bf16[32,11,192]{2,1,0:T(8,128)(2,1)S(1)} %pad_maximum_fusion), channel_id=1, replica_groups=mesh['band'=16,'z'=16,'c'=2] {'z'}, dimensions={0} | all-to-all | bytes 270336 | tf_op jit(solution)/shard_map/all_to_all | solution.py:62
  59.7 3.9 %all_to_all.57 = bf16[2,176,192]{2,1,0:T(8,128)(2,1)S(1)} all-to-all(bf16[2,176,192]{2,1,0:T(8,128)(2,1)S(1)} %copy.73), channel_id=1, replica_groups=mesh['band'=16,'z'=16,'c'=2] {'c'}, dimensions={0} | all-to-all | bytes 270336 | tf_op jit(solution)/shard_map/all_to_all | solution.py:63
  64.9 0.5 broadcast.134
  65.4 1.1 reduce.8
  66.7 16.9 %all_to_all.58 = bf16[32,2,320]{2,1,0:T(2,128)(2,1)S(1)} all-to-all(bf16[32,2,320]{2,1,0:T(2,128)(2,1)S(1)} %reshape.173), channel_id=1, replica_groups=mesh['band'=16,'z'=16,'c'=2] {'z','c'}, dimensions={0} | all-to-all | bytes 81920 | tf_op jit(solution)/shard_map/all_to_all | solution.py:84
  84.4 0.7 copy.78
  85.1 17.2 %all_to_all.59 = bf16[16,2,10,1024]{3,1,2,0:T(2,128)(2,1)S(1)} all-to-all(bf16[16,2,10,1024]{3,1,2,0:T(2,128)(2,1)S(1)} %copy.78), channel_id=1, replica_groups=mesh['band'=16,'z'=16,'c'=2] {'band'}, dimensions={0} | all-to-all | bytes 1310720 | tf_op jit(solution)/shard_map/all_to_all | solution.py:25
  103.3 15.6 %all_to_all.60 = bf16[16,2,10,1024]{3,1,2,0:T(2,128)(2,1)S(1)} all-to-all(bf16[16,2,10,1024]{3,1,2,0:T(2,128)(2,1)S(1)} %broadcast_in_dim.72), channel_id=1, replica_groups=mesh['band'=16,'z'=16,'c'=2] {'band'}, dimensions={0} | all-to-all | bytes 1310720 | tf_op jit(solution)/shard_map/all_to_all | solution.py:18
  119.4 0.8 copy-done.1
  120.5 0.7 copy-done.8
  121.2 0.9 convolution_convert_fusion.1
  122.3 1.5 %copy.83 = bf16[16,2,10,1024]{3,1,2,0:T(2,128)(2,1)} copy(bf16[16,2,10,1024]{3,2,1,0:T(8,128)(2,1)S(1)} %reshape_reshape.15) | data formatting | bytes 1310720 | tf_op jit(solution)/shard_map/reshape;reshape | solution.py:24
  123.8 3.7 %all-to-all-start.6 = ((bf16[16,2,10,1024]{3,1,2,0:T(2,128)(2,1)}), bf16[16,2,10,1024]{3,1,2,0:T(2,128)(2,1)S(1)}, u32[]{:S(2)}, u32[]{:S(2)}) async-start(bf16[16,2,10,1024]{3,1,2,0:T(2,128)(2,1)} %copy.83), calls=%async_computation.6 | async-start | bytes 1310720 | tf_op jit(solution)/shard_map/all_to_all | solution.py:25
  127.7 11.3 %all-to-all-done.6 = bf16[16,2,10,1024]{3,1,2,0:T(2,128)(2,1)S(1)} async-done(((bf16[16,2,10,1024]{3,1,2,0:T(2,128)(2,1)}), bf16[16,2,10,1024]{3,1,2,0:T(2,128)(2,1)S(1)}, u32[]{:S(2)}, u32[]{:S(2)}) %all-to-all-start.6) | async-done | bytes 655392 | tf_op jit(solution)/shard_map/all_to_all | solution.py:25
  139.0 0.4 convert_reduce_fusion
  139.6 0.7 copy.89
  (65 shorter events, 7.1 us)
Async XLA Ops:
  0.0 120.5 %copy-start = (bf16[256,1024]{1,0:T(8,128)(2,1)S(1)}, bf16[256,1024]{1,0:T(8,128)(2,1)}, u32[]{:S(2)}) copy-start(bf16[256,1024]{1,0:T(8,128)(2,1)} %param.25) | copy-start | bytes 1572868
  5.1 20.0 %all-to-all-start = ((bf16[16,2,10,1024]{3,1,2,0:T(2,128)(2,1)}), bf16[16,2,10,1024]{3,1,2,0:T(2,128)(2,1)S(1)}, u32[]{:S(2)}, u32[]{:S(2)}) async-start(bf16[16,2,10,1024]{3,1,2,0:T(2,128)(2,1)} %broadcast_in_dim.68), calls=%async_computation | async-start | bytes 1310720 | tf_op jit(solution)/shard_map/all_to_all | solution.py:18
  25.3 0.9 copy-start.2
  25.3 1.4 %copy-start.3 = (bf16[1024,64]{0,1:T(8,128)(2,1)S(1)}, bf16[1024,64]{0,1:T(8,128)(2,1)}, u32[]{:S(2)}) copy-start(bf16[1024,64]{0,1:T(8,128)(2,1)} %param.19) | copy-start | bytes 393220
  26.2 1.1 copy-start.4
  64.7 19.2 %copy-start.5 = (bf16[64,1024]{1,0:T(8,128)(2,1)S(1)}, bf16[64,1024]{1,0:T(8,128)(2,1)}, u32[]{:S(2)}) copy-start(bf16[64,1024]{1,0:T(8,128)(2,1)} %param.21) | copy-start | bytes 393220
  85.1 17.7 %copy-start.7 = (f32[1024]{0:T(1024)S(1)}, f32[1024]{0:T(1024)}, u32[]{:S(2)}) copy-start(f32[1024]{0:T(1024)} %param.22) | copy-start | bytes 12292
  119.1 1.0 copy-start.1
  120.2 1.0 copy-start.8
  123.8 3.7 %copy-start.9 = (s32[10]{0:T(128)S(1)}, s32[10]{0:T(128)}, u32[]{:S(2)}) copy-start(s32[10]{0:T(128)} %param.16) | copy-start | bytes 124
  123.8 15.6 %copy-start.6 = (bf16[16,2,1024]{2,1,0:T(2,128)(2,1)S(1)}, bf16[16,2,1024]{2,1,0:T(2,128)(2,1)}, u32[]{:S(2)}) copy-start(bf16[16,2,1024]{2,1,0:T(2,128)(2,1)} %param.14) | copy-start | bytes 196612
  123.8 15.2 %all-to-all-start.6 = ((bf16[16,2,10,1024]{3,1,2,0:T(2,128)(2,1)}), bf16[16,2,10,1024]{3,1,2,0:T(2,128)(2,1)S(1)}, u32[]{:S(2)}, u32[]{:S(2)}) async-start(bf16[16,2,10,1024]{3,1,2,0:T(2,128)(2,1)} %copy.83), calls=%async_computation.6 | async-start | bytes 1310720 | tf_op jit(solution)/shard_map/all_to_all | solution.py:25

commit v3 on v2

--- a/solution.py
+++ b/solution.py
@@ -44,7 +44,9 @@
     kept = jnp.take(pixels, clear_index, axis=0)
     kept_rows = jnp.swapaxes(kept, 0, 1)
     spec_here, slots_here, width = kept_rows.shape
-    attn_in = band_gather(normed(kept_rows, attn_gain))
+    w_out_all = lax.all_gather(w_out, "band", axis=0, tiled=True)
+    kept_all = band_gather(kept_rows)
+    attn_in = normed(kept_all, attn_gain)
     spec = attn_in.shape[0]
     flat = attn_in.reshape(spec * slots_here, width)
     heads_here = w_query.shape[1] // HD
@@ -82,14 +84,15 @@
     context = context.reshape(spec_mine, n_c, n_z, slots_here, heads_here * HD)
     context = jnp.swapaxes(context, 1, 2).reshape(spec_mine, slots, heads_here * HD)
     context_rows = lax.all_to_all(context, ("z", "c"), 1, 0, tiled=True)
-    out = jnp.dot(
-        context_rows.reshape(spec * slots_here, heads_here * HD),
-        w_out,
-        preferred_element_type=jnp.float32,
-    ).astype(jnp.bfloat16)
-    attn_out = band_reduce(out.reshape(spec, slots_here, width))
-    state = (kept_rows.astype(jnp.float32) + attn_out).astype(jnp.bfloat16)
-    mlp_in = band_gather(normed(state, mlp_gain))
+    n_band = lax.axis_size("band")
+    sent = jnp.broadcast_to(context_rows[None], (n_band,) + context_rows.shape)
+    context_all = lax.all_to_all(sent, "band", 0, 0, tiled=True)
+    context_all = jnp.transpose(context_all, (1, 2, 0, 3)).reshape(spec * slots_here, width)
+    attn_out = jnp.dot(context_all, w_out_all, preferred_element_type=jnp.float32)
+    state_all = (kept_all.reshape(spec * slots_here, width).astype(jnp.float32) + attn_out).astype(jnp.bfloat16)
+    mlp_in = normed(state_all, mlp_gain)
+    band = lax.axis_index("band")
+    state = lax.dynamic_slice_in_dim(state_all.reshape(spec, slots_here, width), band * spec_here, spec_here, 0)
     piece = mlp_in.reshape(spec * slots_here, width)
     gate = jnp.dot(piece, w_gate, preferred_element_type=jnp.float32)
     upper = jnp.dot(piece, w_up, preferred_element_type=jnp.float32)

time: 141 us -> 147 us (1.043)
  the two profiles are of different devices: /device:TPU:64 before, /device:TPU:2 now
where the time goes in v3:
time: 147 us; the launch traced here: 146 us
  blocking collectives  71.4 us (49%)
  waiting for transfers between devices  18.8 us (13%)
  local copies, waits for them, and re-layouts  15.4 us (10%)
  between operations  14.5 us (10%)
  starting transfers between devices  14.1 us (10%)
  other arithmetic  5.94 us (4%)
  matrix products  5.84 us (4%)
    all_to_all x1, blocking collectives, shards(): mine = lax.all_to_all(payload, 'z', 0, 1, tiled=True)  32.3 us
    all_to_all x1, blocking collectives, shards(): context_rows = lax.all_to_all(context, ('z', 'c'), 1, 0, tiled=True)  19.2 us
    all_to_all x1, blocking collectives, shards(): context_all = lax.all_to_all(sent, 'band', 0, 0, tiled=True)  16.1 us
    all_to_all x1, waiting for transfers between devices, band_reduce(): got = lax.all_to_all(split, 'band', 0, 0, tiled=True)  9.68 us
    all_to_all x1, starting transfers between devices, band_gather(): got = lax.all_to_all(sent, 'band', 0, 0, tiled=True)  9.26 us
    all_to_all x1, waiting for transfers between devices, band_gather(): got = lax.all_to_all(sent, 'band', 0, 0, tiled=True)  8.43 us
    all_to_all x1, starting transfers between devices, band_reduce(): got = lax.all_to_all(split, 'band', 0, 0, tiled=True)  4.84 us
    all_to_all x1, blocking collectives, shards(): mine = lax.all_to_all(mine, 'c', 0, 1, tiled=True)  3.87 us
  transfers between devices with their start and end apart: 3, of which 2 were waited for; matrix products, arithmetic and copies ran while one was open for 10% of the time, Pallas kernels for 0%

profile of v3, /device:TPU:2, one launch (start us, length us, event | category | flops | bytes accessed | tf_op | source)
XLA Modules:
  0.0 146.0 jit_solution(12047221145801747848)
XLA Ops:
  6.5 0.7 compare_select_fusion
  7.9 1.5 %gather_fusion = bf16[10,2,1024]{2,1,0:T(2,128)(2,1)S(1)} fusion(bf16[16,2,1024]{2,1,0:T(2,128)(2,1)} %param.14, s32[1024]{0:T(1024)S(1)} %pad_clamp_fusion), kind=kCustom, calls=%fused_computation | custom fusion | bytes 81960 | tf_op jit(solution)/shard_map/jit(_take)/gather | solution.py:44
  9.5 1.2 broadcast_in_dim.70
  10.7 9.3 %all-to-all-start = ((bf16[16,2,10,1024]{3,1,2,0:T(2,128)(2,1)}), bf16[16,2,10,1024]{3,1,2,0:T(2,128)(2,1)S(1)}, u32[]{:S(2)}, u32[]{:S(2)}) async-start(bf16[16,2,10,1024]{3,1,2,0:T(2,128)(2,1)} %broadcast_in_dim.70), calls=%async_computation | async-start | bytes 1310720 | tf_op jit(solution)/shard_map/all_to_all | solution.py:18
  20.0 0.7 all-gather.2.cloned.1.call-update
  21.4 8.4 %all-to-all-done = bf16[16,2,10,1024]{3,1,2,0:T(2,128)(2,1)S(1)} async-done(((bf16[16,2,10,1024]{3,1,2,0:T(2,128)(2,1)}), bf16[16,2,10,1024]{3,1,2,0:T(2,128)(2,1)S(1)}, u32[]{:S(2)}, u32[]{:S(2)}) %all-to-all-start) | async-done | bytes 655392 | tf_op jit(solution)/shard_map/all_to_all | solution.py:18
  30.5 0.8 copy.57
  31.3 1.2 reshape.180
  32.8 1.5 %multiply_convert_fusion = bf16[320,1024]{1,0:T(8,128)(2,1)S(1)} fusion(f32[320,1024]{1,0:T(8,128)} %reshape.180, f32[1024]{0:T(1024)S(1)} %copy-done.6, f32[320]{0:T(512)S(1)} %rsqrt.20), kind=kLoop, calls=%fused_computation.10 | loop fusion | flops 983040 | bytes 1971456 | tf_op jit(solution)/shard_map/convert_element_type | solution.py:12
  36.1 32.3 %all_to_all.51 = bf16[32,11,192]{2,1,0:T(8,128)(2,1)S(1)} all-to-all(bf16[32,11,192]{2,1,0:T(8,128)(2,1)S(1)} %pad_maximum_fusion), channel_id=1, replica_groups=mesh['band'=16,'z'=16,'c'=2] {'z'}, dimensions={0} | all-to-all | bytes 270336 | tf_op jit(solution)/shard_map/all_to_all | solution.py:64
  68.6 3.9 %all_to_all.52 = bf16[2,176,192]{2,1,0:T(8,128)(2,1)S(1)} all-to-all(bf16[2,176,192]{2,1,0:T(8,128)(2,1)S(1)} %copy.65), channel_id=1, replica_groups=mesh['band'=16,'z'=16,'c'=2] {'c'}, dimensions={0} | all-to-all | bytes 270336 | tf_op jit(solution)/shard_map/all_to_all | solution.py:65
  74.3 1.1 reduce.11
  75.5 19.2 %all_to_all.53 = bf16[32,2,320]{2,1,0:T(2,128)(2,1)S(1)} all-to-all(bf16[32,2,320]{2,1,0:T(2,128)(2,1)S(1)} %reshape.194), channel_id=1, replica_groups=mesh['band'=16,'z'=16,'c'=2] {'z','c'}, dimensions={0} | all-to-all | bytes 81920 | tf_op jit(solution)/shard_map/all_to_all | solution.py:86
  95.7 0.8 reshape.196
  96.5 16.1 %all_to_all.54 = bf16[16,2,10240]{2,1,0:T(2,128)(2,1)S(1)} all-to-all(bf16[16,2,10240]{2,1,0:T(2,128)(2,1)S(1)} %reshape.196), channel_id=1, replica_groups=mesh['band'=16,'z'=16,'c'=2] {'band'}, dimensions={0} | all-to-all | bytes 1310720 | tf_op jit(solution)/shard_map/all_to_all | solution.py:89
  112.6 0.8 reshape.197
  113.7 0.8 copy.70
  114.6 1.7 %reshape.178 = bf16[320,1024]{1,0:T(8,128)(2,1)} reshape(bf16[32,10,16,64]{3,2,1,0:T(8,128)(2,1)S(1)} %copy.70) | data formatting | bytes 1310720 | tf_op jit(solution)/shard_map/reshape | solution.py:90
  116.3 2.8 %fusion.1 = (f32[320]{0:T(512)S(1)}, bf16[320,1024]{1,0:T(8,128)(2,1)S(1)}) fusion(f32[320,1024]{1,0:T(8,128)S(1)} %copy-done.1, bf16[320,1024]{1,0:T(8,128)(2,1)} %reshape.178, bf16[1024,1024]{1,0:T(8,128)(2,1)} %all-gather.2.cloned.1.call-done), kind=kOutput, calls=%fused_computation.6 | convolution fusion | flops 672726720 | bytes 4719872 | tf_op jit(solution)/shard_map/dot_general | solution.py:91
  120.1 0.9 convolution_convert_fusion
  121.3 1.5 %copy.72 = bf16[16,2,10,1024]{3,1,2,0:T(2,128)(2,1)} copy(bf16[16,2,10,1024]{3,2,1,0:T(8,128)(2,1)S(1)} %reshape_reshape.4) | data formatting | bytes 1310720 | tf_op jit(solution)/shard_map/reshape;reshape | solution.py:24
  122.8 4.8 %all-to-all-start.5 = ((bf16[16,2,10,1024]{3,1,2,0:T(2,128)(2,1)}), bf16[16,2,10,1024]{3,1,2,0:T(2,128)(2,1)S(1)}, u32[]{:S(2)}, u32[]{:S(2)}) async-start(bf16[16,2,10,1024]{3,1,2,0:T(2,128)(2,1)} %copy.72), calls=%async_computation.5 | async-start | bytes 1310720 | tf_op jit(solution)/shard_map/all_to_all | solution.py:25
  128.0 9.7 %all-to-all-done.5 = bf16[16,2,10,1024]{3,1,2,0:T(2,128)(2,1)S(1)} async-done(((bf16[16,2,10,1024]{3,1,2,0:T(2,128)(2,1)}), bf16[16,2,10,1024]{3,1,2,0:T(2,128)(2,1)S(1)}, u32[]{:S(2)}, u32[]{:S(2)}) %all-to-all-start.5) | async-done | bytes 655392 | tf_op jit(solution)/shard_map/all_to_all | solution.py:25
  138.5 0.7 copy.75
  (75 shorter events, 9.0 us)
Async XLA Ops:
  6.5 113.0 %copy-start = (bf16[256,1024]{1,0:T(8,128)(2,1)S(1)}, bf16[256,1024]{1,0:T(8,128)(2,1)}, u32[]{:S(2)}) copy-start(bf16[256,1024]{1,0:T(8,128)(2,1)} %param.25) | copy-start | bytes 1572868
  10.7 19.1 %all-to-all-start = ((bf16[16,2,10,1024]{3,1,2,0:T(2,128)(2,1)}), bf16[16,2,10,1024]{3,1,2,0:T(2,128)(2,1)S(1)}, u32[]{:S(2)}, u32[]{:S(2)}) async-start(bf16[16,2,10,1024]{3,1,2,0:T(2,128)(2,1)} %broadcast_in_dim.70), calls=%async_computation | async-start | bytes 1310720 | tf_op jit(solution)/shard_map/all_to_all | solution.py:18
  20.0 96.3 %all-gather.2.cloned.1.call-start = ((), (), s32[]{:S(2)}) async-start(), calls=%async_computation.6 | async-start | bytes 2228224 | tf_op jit(solution)/shard_map/all_gather | solution.py:47
  31.3 1.5 %copy-start.6 = (f32[1024]{0:T(1024)S(1)}, f32[1024]{0:T(1024)}, u32[]{:S(2)}) copy-start(f32[1024]{0:T(1024)} %param.17) | copy-start | bytes 12292
  32.5 1.8 %copy-start.2 = (bf16[1024,64]{0,1:T(8,128)(2,1)S(1)}, bf16[1024,64]{0,1:T(8,128)(2,1)}, u32[]{:S(2)}) copy-start(bf16[1024,64]{0,1:T(8,128)(2,1)} %param.18) | copy-start | bytes 393220
  32.7 2.1 %copy-start.3 = (bf16[1024,64]{0,1:T(8,128)(2,1)S(1)}, bf16[1024,64]{0,1:T(8,128)(2,1)}, u32[]{:S(2)}) copy-start(bf16[1024,64]{0,1:T(8,128)(2,1)} %param.19) | copy-start | bytes 393220
  34.3 1.1 copy-start.4
  114.6 1.7 %copy-start.1 = (f32[320,1024]{1,0:T(8,128)S(1)}, f32[320,1024]{1,0:T(8,128)}, u32[]{:S(2)}) copy-start(f32[320,1024]{1,0:T(8,128)} %reshape.180) | copy-start | bytes 3932164
  116.3 2.8 %copy-start.7 = (bf16[1024,256]{1,0:T(8,128)(2,1)S(1)}, bf16[1024,256]{1,0:T(8,128)(2,1)}, u32[]{:S(2)}) copy-start(bf16[1024,256]{1,0:T(8,128)(2,1)} %param.23) | copy-start | bytes 1572868
  116.3 2.8 %copy-start.9 = (f32[1024]{0:T(1024)S(1)}, f32[1024]{0:T(1024)}, u32[]{:S(2)}) copy-start(f32[1024]{0:T(1024)} %param.22) | copy-start | bytes 12292
  119.1 1.0 copy-start.8
  121.3 6.4 %copy-start.10 = (s32[10]{0:T(128)S(1)}, s32[10]{0:T(128)}, u32[]{:S(2)}) copy-start(s32[10]{0:T(128)} %param.16) | copy-start | bytes 124
  122.8 14.9 %all-to-all-start.5 = ((bf16[16,2,10,1024]{3,1,2,0:T(2,128)(2,1)}), bf16[16,2,10,1024]{3,1,2,0:T(2,128)(2,1)S(1)}, u32[]{:S(2)}, u32[]{:S(2)}) async-start(bf16[16,2,10,1024]{3,1,2,0:T(2,128)(2,1)} %copy.72), calls=%async_computation.5 | async-start | bytes 1310720 | tf_op jit(solution)/shard_map/all_to_all | solution.py:25
  127.8 10.6 %copy-start.5 = (bf16[16,2,1024]{2,1,0:T(2,128)(2,1)S(1)}, bf16[16,2,1024]{2,1,0:T(2,128)(2,1)}, u32[]{:S(2)}) copy-start(bf16[16,2,1024]{2,1,0:T(2,128)(2,1)} %param.14) | copy-start | bytes 196612
Sparse Core Ops, SparseCore 0:
  23.8 62.3 all-gather.1

commit v4 on v3

--- a/solution.py
+++ b/solution.py
@@ -44,8 +44,11 @@
     kept = jnp.take(pixels, clear_index, axis=0)
     kept_rows = jnp.swapaxes(kept, 0, 1)
     spec_here, slots_here, width = kept_rows.shape
-    w_out_all = lax.all_gather(w_out, "band", axis=0, tiled=True)
-    kept_all = band_gather(kept_rows)
+    n_band = lax.axis_size("band")
+    both = jnp.concatenate([kept_rows.reshape(spec_here * slots_here, width), w_out], axis=0)
+    both = lax.all_to_all(jnp.broadcast_to(both[None], (n_band,) + both.shape), "band", 0, 0, tiled=True)
+    kept_all = both[:, : spec_here * slots_here].reshape(n_band * spec_here, slots_here, width)
+    w_out_all = both[:, spec_here * slots_here :].reshape(n_band * w_out.shape[0], width)
     attn_in = normed(kept_all, attn_gain)
     spec = attn_in.shape[0]
     flat = attn_in.reshape(spec * slots_here, width)
@@ -84,7 +87,6 @@
     context = context.reshape(spec_mine, n_c, n_z, slots_here, heads_here * HD)
     context = jnp.swapaxes(context, 1, 2).reshape(spec_mine, slots, heads_here * HD)
     context_rows = lax.all_to_all(context, ("z", "c"), 1, 0, tiled=True)
-    n_band = lax.axis_size("band")
     sent = jnp.broadcast_to(context_rows[None], (n_band,) + context_rows.shape)
     context_all = lax.all_to_all(sent, "band", 0, 0, tiled=True)
     context_all = jnp.transpose(context_all, (1, 2, 0, 3)).reshape(spec * slots_here, width)

time: 147 us -> 201 us (1.37)
  waiting for transfers between devices: 18.8 us -> 52.7 us
  local copies, waits for them, and re-layouts: 15.4 us -> 42.3 us
  between operations: 14.5 us -> 0.94 us
  blocking collectives: 71.4 us -> 59.1 us
  starting transfers between devices: 14.1 us -> 22.9 us
  matrix products: 5.84 us -> 11.1 us
  other arithmetic: 5.94 us -> 10.5 us
    all_to_all x1 -> x2, waiting for transfers between devices: 8.43 us -> 42.7 us  [the longest x1 33.8 us: shards(): lax.all_to_all(jnp.broadcast_to(both[None], (n_band,) + both.shape), 'ban...]
    all_to_all x1 -> x0, blocking collectives: 16.1 us -> none  [shards(): context_all = lax.all_to_all(sent, 'band', 0, 0, tiled=True)]
    all_to_all x1 -> x2, starting transfers between devices: 9.26 us -> 18.1 us  [the longest x1 9.4 us: shards(): lax.all_to_all(jnp.broadcast_to(both[None], (n_band,) + both.shape), 'ban...]
    unnamed x28 -> x26, local copies, waits for them, and re-layouts: 3.32 us -> 10.2 us
    reshape x3, local copies, waits for them, and re-layouts: 0.12 us -> 4.06 us  [project(): return out.reshape(spec, slots_here, heads_here * HD)]
    dot_general x3, matrix products: 1.03 us -> 4.47 us  [project(): jnp.dot(flat, weight, preferred_element_type=jnp.float32)]
    convert_element_type x3, local copies, waits for them, and re-layouts: 0.37 us -> 3.79 us  [project(): jnp.dot(flat, weight, preferred_element_type=jnp.float32)]
    all_to_all x1, blocking collectives: 32.3 us -> 35.1 us  [shards(): mine = lax.all_to_all(payload, 'z', 0, 1, tiled=True)]
  transfers between devices with their start and end apart: 3 -> 3, of which waited for: 2 -> 3; matrix products, arithmetic and copies ran while one was open for 10% -> 1% of each run, Pallas kernels for 0% -> 0%
where the time goes in v4:
time: 201 us; the launch traced here: 200 us
  blocking collectives  59.1 us (29%)
  waiting for transfers between devices  52.7 us (26%)
  local copies, waits for them, and re-layouts  42.3 us (21%)
  starting transfers between devices  22.9 us (11%)
  matrix products  11.1 us (6%)
  other arithmetic  10.5 us (5%)
    all_to_all x1, blocking collectives, shards(): mine = lax.all_to_all(payload, 'z', 0, 1, tiled=True)  35.1 us
    all_to_all x1, waiting for transfers between devices, shards(): lax.all_to_all(jnp.broadcast_to(both[None], (n_band,) + both.shape), 'ban...  33.8 us
    all_to_all x1, blocking collectives, shards(): context_rows = lax.all_to_all(context, ('z', 'c'), 1, 0, tiled=True)  19.4 us
    unnamed x26, local copies, waits for them, and re-layouts  10.2 us
    all_to_all x1, waiting for transfers between devices, band_reduce(): got = lax.all_to_all(split, 'band', 0, 0, tiled=True)  9.96 us
    all_to_all x1, starting transfers between devices, shards(): lax.all_to_all(jnp.broadcast_to(both[None], (n_band,) + both.shape), 'ban...  9.4 us
    all_to_all x1, waiting for transfers between devices, shards(): context_all = lax.all_to_all(sent, 'band', 0, 0, tiled=True)  8.96 us
    all_to_all x1, starting transfers between devices, shards(): context_all = lax.all_to_all(sent, 'band', 0, 0, tiled=True)  8.69 us
  transfers between devices with their start and end apart: 3, of which 3 were waited for; matrix products, arithmetic and copies ran while one was open for 1% of the time, Pallas kernels for 0%

profile of v4, /device:TPU:2, one launch (start us, length us, event | category | flops | bytes accessed | tf_op | source)
XLA Modules:
  0.0 199.6 jit_solution(17584292986275596950)
XLA Ops:
  4.0 1.9 broadcast_in_dim.70
  5.9 9.4 %all-to-all-start = ((bf16[16,84,1024]{2,1,0:T(8,128)(2,1)}), bf16[16,84,1024]{2,1,0:T(8,128)(2,1)S(1)}, u32[]{:S(2)}, u32[]{:S(2)}) async-start(bf16[16,84,1024]{2,1,0:T(8,128)(2,1)} %broadcast_in_dim.70), calls=%async_computation | async-start | bytes 5767168 | tf_op jit(solution)/shard_map/all_to_all | solution.py:49
  16.0 33.8 %all-to-all-done = bf16[16,84,1024]{2,1,0:T(8,128)(2,1)S(1)} async-done(((bf16[16,84,1024]{2,1,0:T(8,128)(2,1)}), bf16[16,84,1024]{2,1,0:T(8,128)(2,1)S(1)}, u32[]{:S(2)}, u32[]{:S(2)}) %all-to-all-start) | async-done | bytes 2752544 | tf_op jit(solution)/shard_map/all_to_all | solution.py:49
  51.5 2.4 %reshape.188 = f32[320,1024]{1,0:T(8,128)} reshape(f32[16,20,1024]{2,1,0:T(8,128)} %slice_convert_fusion) | data formatting | bytes 2621440 | tf_op jit(solution)/shard_map/convert_element_type | solution.py:94
  58.3 2.1 %convolution_convert_fusion.3 = bf16[320,64]{0,1:T(8,128)(2,1)} fusion(bf16[320,1024]{1,0:T(8,128)(2,1)} %copy-done.1, bf16[1024,64]{0,1:T(8,128)(2,1)} %param.19), kind=kOutput, calls=%fused_computation.19 | convolution fusion | flops 41963520 | bytes 827392 | tf_op jit(solution)/shard_map/dot_general | solution.py:58
  60.4 2.1 %convolution_convert_fusion.4 = bf16[320,64]{0,1:T(8,128)(2,1)} fusion(bf16[320,1024]{1,0:T(8,128)(2,1)} %copy-done.1, bf16[1024,64]{0,1:T(8,128)(2,1)} %param.18), kind=kOutput, calls=%fused_computation.20 | convolution fusion | flops 41963520 | bytes 827392 | tf_op jit(solution)/shard_map/dot_general | solution.py:58
  67.0 1.6 reshape.175
  69.8 35.1 %all_to_all.51 = bf16[32,11,192]{2,1,0:T(8,128)(2,1)S(1)} all-to-all(bf16[32,11,192]{2,1,0:T(8,128)(2,1)S(1)} %pad_maximum_fusion), channel_id=1, replica_groups=mesh['band'=16,'z'=16,'c'=2] {'z'}, dimensions={0} | all-to-all | bytes 270336 | tf_op jit(solution)/shard_map/all_to_all | solution.py:67
  105.1 4.6 %all_to_all.52 = bf16[2,176,192]{2,1,0:T(8,128)(2,1)} all-to-all(bf16[2,176,192]{2,1,0:T(8,128)(2,1)S(1)} %copy.44), channel_id=1, replica_groups=mesh['band'=16,'z'=16,'c'=2] {'c'}, dimensions={0} | all-to-all | bytes 270336 | tf_op jit(solution)/shard_map/all_to_all | solution.py:68
  109.7 1.7 reshape.178
  112.4 1.7 reshape.179
  119.0 1.6 reshape.199
  121.1 2.0 %reduce.11 = bf16[320,64]{1,0:T(8,128)(2,1)S(1)} reduce(bf16[320,1,64]{2,1,0:T(2,128)(2,1)} %bitcast.67, bf16[]{:T(256)} %broadcast.128), dimensions={1}, to_apply=%bitcast.38.reduce_sub_computation | reduce | bytes 81922
  123.2 19.4 %all_to_all.53 = bf16[32,2,320]{2,1,0:T(2,128)(2,1)S(1)} all-to-all(bf16[32,2,320]{2,1,0:T(2,128)(2,1)S(1)} %reshape.202), channel_id=1, replica_groups=mesh['band'=16,'z'=16,'c'=2] {'z','c'}, dimensions={0} | all-to-all | bytes 81920 | tf_op jit(solution)/shard_map/all_to_all | solution.py:89
  143.4 2.0 %bitcast_reduce_fusion = bf16[320,64]{1,0:T(8,128)(2,1)} fusion(bf16[320,1,64]{2,1,0:T(2,128)(2,1)} %reshape.203), kind=kLoop, calls=%fused_computation.68 | loop fusion | bytes 81920 | tf_op jit(solution)/shard_map/all_to_all | solution.py:89
  147.7 3.3 %reshape.204 = bf16[16,2,10240]{2,1,0:T(2,128)(2,1)} reshape(bf16[16,10,32,64]{3,2,1,0:T(8,128)(2,1)} %broadcast_bitcast_fusion) | data formatting | bytes 1310720
  151.1 8.7 %all-to-all-start.4 = ((bf16[16,2,10240]{2,1,0:T(2,128)(2,1)}), bf16[16,2,10240]{2,1,0:T(2,128)(2,1)}, u32[]{:S(2)}, u32[]{:S(2)}) async-start(bf16[16,2,10240]{2,1,0:T(2,128)(2,1)} %reshape.204), calls=%async_computation.4 | async-start | bytes 1310720 | tf_op jit(solution)/shard_map/all_to_all | solution.py:91
  159.8 2.2 %slice.59 = bf16[16,64,1024]{2,1,0:T(8,128)(2,1)} slice(bf16[16,84,1024]{2,1,0:T(8,128)(2,1)S(1)} %all-to-all-done), slice={[0:16], [20:84], [0:1024]} | slice | bytes 4194304 | tf_op jit(solution)/shard_map/slice | solution.py:51
  162.0 9.0 %all-to-all-done.4 = bf16[16,2,10240]{2,1,0:T(2,128)(2,1)} async-done(((bf16[16,2,10240]{2,1,0:T(2,128)(2,1)}), bf16[16,2,10240]{2,1,0:T(2,128)(2,1)}, u32[]{:S(2)}, u32[]{:S(2)}) %all-to-all-start.4) | async-done | bytes 655392 | tf_op jit(solution)/shard_map/all_to_all | solution.py:91
  171.0 2.6 %reshape.205 = bf16[16,10,32,64]{3,2,1,0:T(8,128)(2,1)S(1)} reshape(bf16[16,2,10240]{2,1,0:T(2,128)(2,1)} %all-to-all-done.4) | data formatting | bytes 1310720
  174.7 1.7 reshape.185
  176.4 2.8 %fusion.1 = (f32[320]{0:T(512)S(1)}, bf16[320,1024]{1,0:T(8,128)(2,1)S(1)}) fusion(f32[320,1024]{1,0:T(8,128)S(1)} %copy-done.2, bf16[320,1024]{1,0:T(8,128)(2,1)} %reshape.185, bf16[1024,1024]{1,0:T(8,128)(2,1)} %bitcast.63), kind=kOutput, calls=%fused_computation.7 | convolution fusion | flops 672726720 | bytes 4719872 | tf_op jit(solution)/shard_map/dot_general | solution.py:93
  182.9 4.8 %all-to-all-start.5 = ((bf16[16,2,10,1024]{3,1,2,0:T(2,128)(2,1)}), bf16[16,2,10,1024]{3,1,2,0:T(2,128)(2,1)S(1)}, u32[]{:S(2)}, u32[]{:S(2)}) async-start(bf16[16,2,10,1024]{3,1,2,0:T(2,128)(2,1)} %copy.51), calls=%async_computation.5 | async-start | bytes 1310720 | tf_op jit(solution)/shard_map/all_to_all | solution.py:25
  188.1 10.0 %all-to-all-done.5 = bf16[16,2,10,1024]{3,1,2,0:T(2,128)(2,1)S(1)} async-done(((bf16[16,2,10,1024]{3,1,2,0:T(2,128)(2,1)}), bf16[16,2,10,1024]{3,1,2,0:T(2,128)(2,1)S(1)}, u32[]{:S(2)}, u32[]{:S(2)}) %all-to-all-start.5) | async-done | bytes 655392 | tf_op jit(solution)/shard_map/all_to_all | solution.py:25
  (73 shorter events, 32.0 us)
Async XLA Ops:
  0.0 179.7 %copy-start = (bf16[256,1024]{1,0:T(8,128)(2,1)S(1)}, bf16[256,1024]{1,0:T(8,128)(2,1)}, u32[]{:S(2)}) copy-start(bf16[256,1024]{1,0:T(8,128)(2,1)} %param.25) | copy-start | bytes 1572868
  5.9 43.9 %all-to-all-start = ((bf16[16,84,1024]{2,1,0:T(8,128)(2,1)}), bf16[16,84,1024]{2,1,0:T(8,128)(2,1)S(1)}, u32[]{:S(2)}, u32[]{:S(2)}) async-start(bf16[16,84,1024]{2,1,0:T(8,128)(2,1)} %broadcast_in_dim.70), calls=%async_computation | async-start | bytes 5767168 | tf_op jit(solution)/shard_map/all_to_all | solution.py:49
  51.5 2.5 %copy-start.5 = (f32[1024]{0:T(1024)S(1)}, f32[1024]{0:T(1024)}, u32[]{:S(2)}) copy-start(f32[1024]{0:T(1024)} %param.17) | copy-start | bytes 12292
  53.9 2.4 %copy-start.3 = (bf16[1024,64]{0,1:T(8,128)(2,1)S(1)}, bf16[1024,64]{0,1:T(8,128)(2,1)}, u32[]{:S(2)}) copy-start(bf16[1024,64]{0,1:T(8,128)(2,1)} %param.20) | copy-start | bytes 393220
  55.5 0.8 copy-start.1
  151.1 19.9 %all-to-all-start.4 = ((bf16[16,2,10240]{2,1,0:T(2,128)(2,1)}), bf16[16,2,10240]{2,1,0:T(2,128)(2,1)}, u32[]{:S(2)}, u32[]{:S(2)}) async-start(bf16[16,2,10240]{2,1,0:T(2,128)(2,1)} %reshape.204), calls=%async_computation.4 | async-start | bytes 1310720 | tf_op jit(solution)/shard_map/all_to_all | solution.py:91
  174.7 1.7 copy-start.2
  176.4 2.8 %copy-start.6 = (bf16[1024,256]{1,0:T(8,128)(2,1)S(1)}, bf16[1024,256]{1,0:T(8,128)(2,1)}, u32[]{:S(2)}) copy-start(bf16[1024,256]{1,0:T(8,128)(2,1)} %param.23) | copy-start | bytes 1572868
  176.4 2.8 %copy-start.8 = (f32[1024]{0:T(1024)S(1)}, f32[1024]{0:T(1024)}, u32[]{:S(2)}) copy-start(f32[1024]{0:T(1024)} %param.22) | copy-start | bytes 12292
  179.2 1.0 copy-start.7
  181.4 6.4 %copy-start.9 = (s32[10]{0:T(128)S(1)}, s32[10]{0:T(128)}, u32[]{:S(2)}) copy-start(s32[10]{0:T(128)} %param.16) | copy-start | bytes 124
  182.9 15.2 %all-to-all-start.5 = ((bf16[16,2,10,1024]{3,1,2,0:T(2,128)(2,1)}), bf16[16,2,10,1024]{3,1,2,0:T(2,128)(2,1)S(1)}, u32[]{:S(2)}, u32[]{:S(2)}) async-start(bf16[16,2,10,1024]{3,1,2,0:T(2,128)(2,1)} %copy.51), calls=%async_computation.5 | async-start | bytes 1310720 | tf_op jit(solution)/shard_map/all_to_all | solution.py:25
  187.9 10.8 %copy-start.4 = (bf16[16,2,1024]{2,1,0:T(2,128)(2,1)S(1)}, bf16[16,2,1024]{2,1,0:T(2,128)(2,1)}, u32[]{:S(2)}) copy-start(bf16[16,2,1024]{2,1,0:T(2,128)(2,1)} %param.14) | copy-start | bytes 196612

commit v5 on v2

--- a/solution.py
+++ b/solution.py
@@ -57,19 +57,22 @@
     qkv = jnp.concatenate([project(w_query), project(w_key), project(w_value)], axis=-1)
     width_qkv = qkv.shape[-1]
     flag_row = jnp.zeros((spec, 1, width_qkv), jnp.bfloat16)
-    flag_row = flag_row.at[:, 0, :slots_here].set(live_here.astype(jnp.bfloat16)[None, :])
+    at = heads_here * HD
+    flag_row = flag_row.at[:, 0, at : at + slots_here].set(live_here.astype(jnp.bfloat16)[None, :])
     payload = jnp.concatenate([qkv, flag_row], axis=1)
     mine = lax.all_to_all(payload, "z", 0, 1, tiled=True)
-    mine = lax.all_to_all(mine, "c", 0, 1, tiled=True)
-    n_z, n_c = lax.axis_size("z"), lax.axis_size("c")
+    n_z = lax.axis_size("z")
     spec_mine = mine.shape[0]
-    mine = mine.reshape(spec_mine, n_c * n_z, slots_here + 1, width_qkv)
-    live = (mine[0, :, slots_here, :slots_here] > 0.5).reshape(-1)
-    rows = mine[:, :, :slots_here].reshape(spec_mine, n_c * n_z * slots_here, width_qkv)
-    slots = rows.shape[1]
-    q = rows[..., 0 * HD : heads_here * HD].reshape(spec_mine, slots, heads_here, HD)
-    k = rows[..., heads_here * HD : 2 * heads_here * HD].reshape(spec_mine, slots, heads_here, HD)
-    v = rows[..., 2 * heads_here * HD : 3 * heads_here * HD].reshape(spec_mine, slots, heads_here, HD)
+    mine = mine.reshape(spec_mine, n_z, slots_here + 1, width_qkv)
+    kv_flag = mine[..., heads_here * HD :]
+    other = lax.ppermute(kv_flag, "c", [(0, 1), (1, 0)])
+    kv_flag = jnp.concatenate([kv_flag, other], axis=1)
+    live = (kv_flag[0, :, slots_here, :slots_here] > 0.5).reshape(-1)
+    kv = kv_flag[:, :, :slots_here].reshape(spec_mine, -1, 2 * heads_here * HD)
+    q_slots = n_z * slots_here
+    q = mine[:, :, :slots_here, : heads_here * HD].reshape(spec_mine, q_slots, heads_here, HD)
+    k = kv[..., : heads_here * HD].reshape(spec_mine, -1, heads_here, HD)
+    v = kv[..., heads_here * HD :].reshape(spec_mine, -1, heads_here, HD)
     scores = jnp.einsum("sqhd,skhd->shqk", q, k, preferred_element_type=jnp.float32) * HD ** (-0.5)
     masked = jnp.where(live[None, None, None, :], scores, -1e30)
     top = jnp.max(masked, axis=-1)
@@ -79,9 +82,8 @@
         "shqk,skhd->sqhd", expo.astype(jnp.bfloat16), v, preferred_element_type=jnp.float32
     )
     context = (mixed / jnp.transpose(totals, (0, 2, 1))[..., None]).astype(jnp.bfloat16)
-    context = context.reshape(spec_mine, n_c, n_z, slots_here, heads_here * HD)
-    context = jnp.swapaxes(context, 1, 2).reshape(spec_mine, slots, heads_here * HD)
-    context_rows = lax.all_to_all(context, ("z", "c"), 1, 0, tiled=True)
+    context = context.reshape(spec_mine, q_slots, heads_here * HD)
+    context_rows = lax.all_to_all(context, "z", 1, 0, tiled=True)
     out = jnp.dot(
         context_rows.reshape(spec * slots_here, heads_here * HD),
         w_out,

time: 141 us -> 136 us (0.965)
  the two profiles are of different devices: /device:TPU:64 before, /device:TPU:2 now
where the time goes in v5:
time: 136 us
  blocking collectives  80.2 us (59%)
  local copies, waits for them, and re-layouts  17.2 us (13%)
  starting transfers between devices  16.2 us (12%)
  waiting for transfers between devices  12.2 us (9%)
  other arithmetic  5.47 us (4%)
  matrix products  3.36 us (2%)
    all_to_all x1, blocking collectives, shards(): mine = lax.all_to_all(payload, 'z', 0, 1, tiled=True)  32.3 us
    all_to_all x1, blocking collectives, shards(): context_rows = lax.all_to_all(context, 'z', 1, 0, tiled=True)  17.8 us
    all_to_all x1, blocking collectives, band_reduce(): got = lax.all_to_all(split, 'band', 0, 0, tiled=True)  15.9 us
    all_to_all x1, blocking collectives, band_gather(): got = lax.all_to_all(sent, 'band', 0, 0, tiled=True)  14.2 us
    all_to_all x1, waiting for transfers between devices, band_reduce(): got = lax.all_to_all(split, 'band', 0, 0, tiled=True)  9.44 us
    all_to_all x1, starting transfers between devices, band_gather(): got = lax.all_to_all(sent, 'band', 0, 0, tiled=True)  9.26 us
    scatter x1, local copies, waits for them, and re-layouts, shards(): flag_row.at[:, 0, at:at + slots_here]  5.51 us
    all_to_all x1, starting transfers between devices, band_reduce(): got = lax.all_to_all(split, 'band', 0, 0, tiled=True)  4.97 us
  transfers between devices with their start and end apart: 3, of which 3 were waited for; matrix products, arithmetic and copies ran while one was open for 6% of the time, Pallas kernels for 0%

profile of v5, /device:TPU:2, one launch (start us, length us, event | category | flops | bytes accessed | tf_op | source)
XLA Modules:
  0.0 135.7 jit_solution(7053922894093468162)
XLA Ops:
  0.0 0.7 compare_select_fusion
  0.7 0.7 compare_and_fusion
  1.4 1.5 %gather_fusion = bf16[10,2,1024]{2,1,0:T(2,128)(2,1)S(1)} fusion(bf16[16,2,1024]{2,1,0:T(2,128)(2,1)} %param.14, s32[1024]{0:T(1024)S(1)} %pad_clamp_fusion), kind=kCustom, calls=%fused_computation | custom fusion | bytes 81960 | tf_op jit(solution)/shard_map/jit(_take)/gather | solution.py:44
  3.1 0.8 fusion.26
  3.9 1.2 broadcast_in_dim.70
  5.1 9.3 %all-to-all-start = ((bf16[16,2,10,1024]{3,1,2,0:T(2,128)(2,1)}), bf16[16,2,10,1024]{3,1,2,0:T(2,128)(2,1)S(1)}, u32[]{:S(2)}, u32[]{:S(2)}) async-start(bf16[16,2,10,1024]{3,1,2,0:T(2,128)(2,1)} %broadcast_in_dim.70), calls=%async_computation | async-start | bytes 1310720 | tf_op jit(solution)/shard_map/all_to_all | solution.py:18
  15.6 0.7 and_reduce_fusion
  16.3 0.6 broadcast_select_fusion.1
  17.1 5.5 %scatter.4 = bf16[32,1,192]{2,1,0:T(2,128)(2,1)S(1)} dynamic-update-slice(bf16[32,1,192]{2,1,0:T(2,128)(2,1)S(1)} %broadcast_in_dim.71, bf16[32,1,10]{2,1,0:T(2,128)(2,1)S(1)} %broadcast.134, s32[]{:T(128)} %constant.48.clone.1, s32[]{:T(128)} %constant.48.clone.1, s32[]{:T(128)} %bitcast.3) | dynamic-update-slice | bytes 1284 | tf_op jit(solution)/shard_map/scatter | solution.py:61
  22.6 1.6 %all-to-all-done = bf16[16,2,10,1024]{3,1,2,0:T(2,128)(2,1)S(1)} async-done(((bf16[16,2,10,1024]{3,1,2,0:T(2,128)(2,1)}), bf16[16,2,10,1024]{3,1,2,0:T(2,128)(2,1)S(1)}, u32[]{:S(2)}, u32[]{:S(2)}) %all-to-all-start) | async-done | bytes 655392 | tf_op jit(solution)/shard_map/all_to_all | solution.py:18
  27.1 32.3 %all_to_all.50 = bf16[32,11,192]{2,1,0:T(8,128)(2,1)S(1)} all-to-all(bf16[32,11,192]{2,1,0:T(8,128)(2,1)S(1)} %pad_maximum_fusion), channel_id=1, replica_groups=mesh['band'=16,'z'=16,'c'=2] {'z'}, dimensions={0} | all-to-all | bytes 270336 | tf_op jit(solution)/shard_map/all_to_all | solution.py:63
  59.7 1.9 %collective-permute-start = (bf16[2,16,11,128]{3,0,2,1:T(2,128)(2,1)S(1)}, bf16[2,16,11,128]{3,0,2,1:T(2,128)(2,1)S(1)}, u32[]{:S(2)}, u32[]{:S(2)}) collective-permute-start(bf16[2,16,11,128]{3,0,2,1:T(2,128)(2,1)S(1)} %slice.54), channel_id=1, source_target_pairs={{0,1},{1,0},{2,3},{3,2},{4,5},{5,4},{6,7},{7,6},{8,9},{9,8},{10,11... | collective-permute-start | bytes 270344 | tf_op jit(solution)/shard_map/ppermute | solution.py:68
  61.7 1.2 collective-permute-done
  64.5 17.8 %all_to_all.51 = bf16[16,2,640]{2,1,0:T(2,128)(2,1)S(1)} all-to-all(bf16[16,2,640]{2,1,0:T(2,128)(2,1)S(1)} %reshape.159), channel_id=1, replica_groups=mesh['band'=16,'z'=16,'c'=2] {'z'}, dimensions={0} | all-to-all | bytes 81920 | tf_op jit(solution)/shard_map/all_to_all | solution.py:86
  83.1 0.7 copy.82
  83.8 15.9 %all_to_all.52 = bf16[16,2,10,1024]{3,1,2,0:T(2,128)(2,1)S(1)} all-to-all(bf16[16,2,10,1024]{3,1,2,0:T(2,128)(2,1)S(1)} %copy.82), channel_id=1, replica_groups=mesh['band'=16,'z'=16,'c'=2] {'band'}, dimensions={0} | all-to-all | bytes 1310720 | tf_op jit(solution)/shard_map/all_to_all | solution.py:25
  100.7 14.2 %all_to_all.53 = bf16[16,2,10,1024]{3,1,2,0:T(2,128)(2,1)S(1)} all-to-all(bf16[16,2,10,1024]{3,1,2,0:T(2,128)(2,1)S(1)} %broadcast_in_dim.75), channel_id=1, replica_groups=mesh['band'=16,'z'=16,'c'=2] {'band'}, dimensions={0} | all-to-all | bytes 1310720 | tf_op jit(solution)/shard_map/all_to_all | solution.py:18
  115.3 0.8 copy-done.1
  116.5 0.7 copy-done.9
  117.2 0.9 convolution_convert_fusion.1
  118.3 1.5 %copy.87 = bf16[16,2,10,1024]{3,1,2,0:T(2,128)(2,1)} copy(bf16[16,2,10,1024]{3,2,1,0:T(8,128)(2,1)S(1)} %reshape_reshape.15) | data formatting | bytes 1310720 | tf_op jit(solution)/shard_map/reshape;reshape | solution.py:24
  119.8 5.0 %all-to-all-start.5 = ((bf16[16,2,10,1024]{3,1,2,0:T(2,128)(2,1)}), bf16[16,2,10,1024]{3,1,2,0:T(2,128)(2,1)S(1)}, u32[]{:S(2)}, u32[]{:S(2)}) async-start(bf16[16,2,10,1024]{3,1,2,0:T(2,128)(2,1)} %copy.87), calls=%async_computation.5 | async-start | bytes 1310720 | tf_op jit(solution)/shard_map/all_to_all | solution.py:25
  124.9 9.4 %all-to-all-done.5 = bf16[16,2,10,1024]{3,1,2,0:T(2,128)(2,1)S(1)} async-done(((bf16[16,2,10,1024]{3,1,2,0:T(2,128)(2,1)}), bf16[16,2,10,1024]{3,1,2,0:T(2,128)(2,1)S(1)}, u32[]{:S(2)}, u32[]{:S(2)}) %all-to-all-start.5) | async-done | bytes 655392 | tf_op jit(solution)/shard_map/all_to_all | solution.py:25
  134.9 0.7 copy.93
  (69 shorter events, 9.1 us)
Async XLA Ops:
  0.0 116.5 %copy-start = (bf16[256,1024]{1,0:T(8,128)(2,1)S(1)}, bf16[256,1024]{1,0:T(8,128)(2,1)}, u32[]{:S(2)}) copy-start(bf16[256,1024]{1,0:T(8,128)(2,1)} %param.25) | copy-start | bytes 1572868
  3.1 12.6 %copy-start.8 = (s32[3]{0:T(128)S(1)}, s32[3]{0:T(128)}, u32[]{:S(2)}) copy-start(s32[3]{0:T(128)} %constant.58.clone.1) | copy-start | bytes 40
  5.1 19.1 %all-to-all-start = ((bf16[16,2,10,1024]{3,1,2,0:T(2,128)(2,1)}), bf16[16,2,10,1024]{3,1,2,0:T(2,128)(2,1)S(1)}, u32[]{:S(2)}, u32[]{:S(2)}) async-start(bf16[16,2,10,1024]{3,1,2,0:T(2,128)(2,1)} %broadcast_in_dim.70), calls=%async_computation | async-start | bytes 1310720 | tf_op jit(solution)/shard_map/all_to_all | solution.py:18
  24.4 0.9 copy-start.2
  24.4 1.4 %copy-start.3 = (bf16[1024,64]{0,1:T(8,128)(2,1)S(1)}, bf16[1024,64]{0,1:T(8,128)(2,1)}, u32[]{:S(2)}) copy-start(bf16[1024,64]{0,1:T(8,128)(2,1)} %param.19) | copy-start | bytes 393220
  25.3 1.1 copy-start.4
  59.7 3.2 %collective-permute-start = (bf16[2,16,11,128]{3,0,2,1:T(2,128)(2,1)S(1)}, bf16[2,16,11,128]{3,0,2,1:T(2,128)(2,1)S(1)}, u32[]{:S(2)}, u32[]{:S(2)}) collective-permute-start(bf16[2,16,11,128]{3,0,2,1:T(2,128)(2,1)S(1)} %slice.54), channel_id=1, source_target_pairs={{0,1},{1,0},{2,3},{3,2},{4,5},{5,4},{6,7},{7,6},{8,9},{9,8},{10,11... | collective-permute-start | bytes 270344 | tf_op jit(solution)/shard_map/ppermute | solution.py:68
  64.0 18.5 %copy-start.5 = (bf16[64,1024]{1,0:T(8,128)(2,1)S(1)}, bf16[64,1024]{1,0:T(8,128)(2,1)}, u32[]{:S(2)}) copy-start(bf16[64,1024]{1,0:T(8,128)(2,1)} %param.21) | copy-start | bytes 393220
  83.8 16.5 %copy-start.7 = (f32[1024]{0:T(1024)S(1)}, f32[1024]{0:T(1024)}, u32[]{:S(2)}) copy-start(f32[1024]{0:T(1024)} %param.22) | copy-start | bytes 12292
  115.1 1.0 copy-start.1
  116.1 1.0 copy-start.9
  119.8 5.0 %copy-start.10 = (s32[10]{0:T(128)S(1)}, s32[10]{0:T(128)}, u32[]{:S(2)}) copy-start(s32[10]{0:T(128)} %param.16) | copy-start | bytes 124
  119.8 15.0 %copy-start.6 = (bf16[16,2,1024]{2,1,0:T(2,128)(2,1)S(1)}, bf16[16,2,1024]{2,1,0:T(2,128)(2,1)}, u32[]{:S(2)}) copy-start(bf16[16,2,1024]{2,1,0:T(2,128)(2,1)} %param.14) | copy-start | bytes 196612
  119.8 14.5 %all-to-all-start.5 = ((bf16[16,2,10,1024]{3,1,2,0:T(2,128)(2,1)}), bf16[16,2,10,1024]{3,1,2,0:T(2,128)(2,1)S(1)}, u32[]{:S(2)}, u32[]{:S(2)}) async-start(bf16[16,2,10,1024]{3,1,2,0:T(2,128)(2,1)} %copy.87), calls=%async_computation.5 | async-start | bytes 1310720 | tf_op jit(solution)/shard_map/all_to_all | solution.py:25

commit v6 on v5

--- a/solution.py
+++ b/solution.py
@@ -60,10 +60,11 @@
     at = heads_here * HD
     flag_row = flag_row.at[:, 0, at : at + slots_here].set(live_here.astype(jnp.bfloat16)[None, :])
     payload = jnp.concatenate([qkv, flag_row], axis=1)
-    mine = lax.all_to_all(payload, "z", 0, 1, tiled=True)
     n_z = lax.axis_size("z")
-    spec_mine = mine.shape[0]
-    mine = mine.reshape(spec_mine, n_z, slots_here + 1, width_qkv)
+    spec_mine = spec // n_z
+    mine = lax.all_to_all(payload.reshape(n_z, -1), "z", 0, 0, tiled=True)
+    mine = mine.reshape(n_z, spec_mine, slots_here + 1, width_qkv)
+    mine = jnp.swapaxes(mine, 0, 1)
     kv_flag = mine[..., heads_here * HD :]
     other = lax.ppermute(kv_flag, "c", [(0, 1), (1, 0)])
     kv_flag = jnp.concatenate([kv_flag, other], axis=1)
@@ -83,7 +84,9 @@
     )
     context = (mixed / jnp.transpose(totals, (0, 2, 1))[..., None]).astype(jnp.bfloat16)
     context = context.reshape(spec_mine, q_slots, heads_here * HD)
-    context_rows = lax.all_to_all(context, "z", 1, 0, tiled=True)
+    context = jnp.swapaxes(context.reshape(spec_mine, n_z, -1), 0, 1).reshape(n_z, -1)
+    context_rows = lax.all_to_all(context, "z", 0, 0, tiled=True)
+    context_rows = context_rows.reshape(spec, slots_here, heads_here * HD)
     out = jnp.dot(
         context_rows.reshape(spec * slots_here, heads_here * HD),
         w_out,

time: 136 us -> 136 us (level)
  blocking collectives: 80.2 us -> 74.9 us
  other arithmetic: 5.47 us -> 8.59 us
  local copies, waits for them, and re-layouts: 17.2 us -> 18.6 us
    all_to_all x2, blocking collectives: 50.1 us -> 44.9 us  [the longest x1 29 us: shards(): mine = lax.all_to_all(payload.reshape(n_z, -1), 'z', 0, 0, tiled=True)]
    all_to_all x0 -> x4, other arithmetic: none -> 3.28 us  [the longest x2 2.19 us: shards(): mine = lax.all_to_all(payload.reshape(n_z, -1), 'z', 0, 0, tiled=True)]
where the time goes in v6:
time: 136 us; the launch traced here: 135 us
  blocking collectives  74.9 us (55%)
  local copies, waits for them, and re-layouts  18.6 us (14%)
  starting transfers between devices  16.2 us (12%)
  waiting for transfers between devices  12.2 us (9%)
  other arithmetic  8.59 us (6%)
  matrix products  3.67 us (3%)
    all_to_all x1, blocking collectives, shards(): mine = lax.all_to_all(payload.reshape(n_z, -1), 'z', 0, 0, tiled=True)  29 us
    all_to_all x1, blocking collectives, band_reduce(): got = lax.all_to_all(split, 'band', 0, 0, tiled=True)  15.9 us
    all_to_all x1, blocking collectives, shards(): context_rows = lax.all_to_all(context, 'z', 0, 0, tiled=True)  15.8 us
    all_to_all x1, blocking collectives, band_gather(): got = lax.all_to_all(sent, 'band', 0, 0, tiled=True)  14.2 us
    all_to_all x1, waiting for transfers between devices, band_reduce(): got = lax.all_to_all(split, 'band', 0, 0, tiled=True)  9.43 us
    all_to_all x1, starting transfers between devices, band_gather(): got = lax.all_to_all(sent, 'band', 0, 0, tiled=True)  9.26 us
    scatter x1, local copies, waits for them, and re-layouts, shards(): flag_row.at[:, 0, at:at + slots_here]  5.51 us
    all_to_all x1, starting transfers between devices, band_reduce(): got = lax.all_to_all(split, 'band', 0, 0, tiled=True)  4.97 us
  transfers between devices with their start and end apart: 3, of which 3 were waited for; matrix products, arithmetic and copies ran while one was open for 6% of the time, Pallas kernels for 0%

profile of v6, /device:TPU:2, one launch (start us, length us, event | category | flops | bytes accessed | tf_op | source)
XLA Modules:
  0.0 135.3 jit_solution(2381923352405771394)
XLA Ops:
  0.0 0.7 compare_select_fusion
  1.4 1.5 %gather_fusion = bf16[10,2,1024]{2,1,0:T(2,128)(2,1)S(1)} fusion(bf16[16,2,1024]{2,1,0:T(2,128)(2,1)} %param.14, s32[1024]{0:T(1024)S(1)} %pad_clamp_fusion), kind=kCustom, calls=%fused_computation | custom fusion | bytes 81960 | tf_op jit(solution)/shard_map/jit(_take)/gather | solution.py:44
  3.1 0.8 fusion.25
  3.9 1.2 broadcast_in_dim.70
  5.1 9.3 %all-to-all-start = ((bf16[16,2,10,1024]{3,1,2,0:T(2,128)(2,1)}), bf16[16,2,10,1024]{3,1,2,0:T(2,128)(2,1)S(1)}, u32[]{:S(2)}, u32[]{:S(2)}) async-start(bf16[16,2,10,1024]{3,1,2,0:T(2,128)(2,1)} %broadcast_in_dim.70), calls=%async_computation | async-start | bytes 1310720 | tf_op jit(solution)/shard_map/all_to_all | solution.py:18
  15.6 0.7 and_reduce_fusion
  17.1 5.5 %scatter.4 = bf16[32,1,192]{2,1,0:T(2,128)(2,1)S(1)} dynamic-update-slice(bf16[32,1,192]{2,1,0:T(2,128)(2,1)S(1)} %broadcast_in_dim.71, bf16[32,1,10]{2,1,0:T(2,128)(2,1)S(1)} %broadcast.134, s32[]{:T(128)} %constant.48.clone.1, s32[]{:T(128)} %constant.48.clone.1, s32[]{:T(128)} %bitcast.3) | dynamic-update-slice | bytes 1284 | tf_op jit(solution)/shard_map/scatter | solution.py:61
  22.6 1.6 %all-to-all-done = bf16[16,2,10,1024]{3,1,2,0:T(2,128)(2,1)S(1)} async-done(((bf16[16,2,10,1024]{3,1,2,0:T(2,128)(2,1)}), bf16[16,2,10,1024]{3,1,2,0:T(2,128)(2,1)S(1)}, u32[]{:S(2)}, u32[]{:S(2)}) %all-to-all-start) | async-done | bytes 655392 | tf_op jit(solution)/shard_map/all_to_all | solution.py:18
  27.9 1.4 %reduce.16 = bf16[16,4224]{1,0:T(8,128)(2,1)S(1)} reduce(bf16[16,1,4224]{2,1,0:T(2,128)(2,1)S(1)} %all_to_all.32, bf16[]{:T(256)} %broadcast.150), dimensions={1}, to_apply=%all_to_all.32.reduce_sub_computation | reduce | bytes 270338 | tf_op jit(solution)/shard_map/all_to_all | solution.py:65
  29.4 29.0 %all_to_all.40 = bf16[16,2,2112]{2,1,0:T(2,128)(2,1)S(1)} all-to-all(bf16[16,2,2112]{2,1,0:T(2,128)(2,1)S(1)} %reshape.164), channel_id=1, replica_groups=mesh['band'=16,'z'=16,'c'=2] {'z'}, dimensions={0} | all-to-all | bytes 270336 | tf_op jit(solution)/shard_map/all_to_all | solution.py:65
  58.6 0.8 reduce.11
  59.8 1.9 %collective-permute-start = (bf16[2,16,11,128]{3,2,0,1:T(8,128)(2,1)S(1)}, bf16[2,16,11,128]{3,2,0,1:T(8,128)(2,1)S(1)}, u32[]{:S(2)}, u32[]{:S(2)}) collective-permute-start(bf16[2,16,11,128]{3,2,0,1:T(8,128)(2,1)S(1)} %slice.54), channel_id=1, source_target_pairs={{0,1},{1,0},{2,3},{3,2},{4,5},{5,4},{6,7},{7,6},{8,9},{9,8},{10,11... | collective-permute-start | bytes 270344 | tf_op jit(solution)/shard_map/ppermute | solution.py:69
  61.8 1.2 collective-permute-done
  65.1 0.9 reduce.17
  66.0 15.8 %all_to_all.41 = bf16[16,2,640]{2,1,0:T(2,128)(2,1)S(1)} all-to-all(bf16[16,2,640]{2,1,0:T(2,128)(2,1)S(1)} %reshape.166), channel_id=1, replica_groups=mesh['band'=16,'z'=16,'c'=2] {'z'}, dimensions={0} | all-to-all | bytes 81920 | tf_op jit(solution)/shard_map/all_to_all | solution.py:88
  83.4 15.9 %all_to_all.42 = bf16[16,2,10,1024]{3,1,2,0:T(2,128)(2,1)S(1)} all-to-all(bf16[16,2,10,1024]{3,1,2,0:T(2,128)(2,1)S(1)} %copy.91), channel_id=1, replica_groups=mesh['band'=16,'z'=16,'c'=2] {'band'}, dimensions={0} | all-to-all | bytes 1310720 | tf_op jit(solution)/shard_map/all_to_all | solution.py:25
  100.3 14.2 %all_to_all.43 = bf16[16,2,10,1024]{3,1,2,0:T(2,128)(2,1)S(1)} all-to-all(bf16[16,2,10,1024]{3,1,2,0:T(2,128)(2,1)S(1)} %broadcast_in_dim.75), channel_id=1, replica_groups=mesh['band'=16,'z'=16,'c'=2] {'band'}, dimensions={0} | all-to-all | bytes 1310720 | tf_op jit(solution)/shard_map/all_to_all | solution.py:18
  115.0 0.8 copy-done.1
  116.1 0.7 copy-done.9
  116.8 0.9 convolution_convert_fusion.1
  117.9 1.5 %copy.96 = bf16[16,2,10,1024]{3,1,2,0:T(2,128)(2,1)} copy(bf16[16,2,10,1024]{3,2,1,0:T(8,128)(2,1)S(1)} %reshape_reshape.23) | data formatting | bytes 1310720 | tf_op jit(solution)/shard_map/reshape;reshape | solution.py:24
  119.4 5.0 %all-to-all-start.5 = ((bf16[16,2,10,1024]{3,1,2,0:T(2,128)(2,1)}), bf16[16,2,10,1024]{3,1,2,0:T(2,128)(2,1)S(1)}, u32[]{:S(2)}, u32[]{:S(2)}) async-start(bf16[16,2,10,1024]{3,1,2,0:T(2,128)(2,1)} %copy.96), calls=%async_computation.5 | async-start | bytes 1310720 | tf_op jit(solution)/shard_map/all_to_all | solution.py:25
  124.5 9.4 %all-to-all-done.5 = bf16[16,2,10,1024]{3,1,2,0:T(2,128)(2,1)S(1)} async-done(((bf16[16,2,10,1024]{3,1,2,0:T(2,128)(2,1)}), bf16[16,2,10,1024]{3,1,2,0:T(2,128)(2,1)S(1)}, u32[]{:S(2)}, u32[]{:S(2)}) %all-to-all-start.5) | async-done | bytes 655392 | tf_op jit(solution)/shard_map/all_to_all | solution.py:25
  134.6 0.7 copy.102
  (82 shorter events, 12.8 us)
Async XLA Ops:
  0.0 116.1 %copy-start = (bf16[256,1024]{1,0:T(8,128)(2,1)S(1)}, bf16[256,1024]{1,0:T(8,128)(2,1)}, u32[]{:S(2)}) copy-start(bf16[256,1024]{1,0:T(8,128)(2,1)} %param.25) | copy-start | bytes 1572868
  3.1 12.6 %copy-start.8 = (s32[3]{0:T(128)S(1)}, s32[3]{0:T(128)}, u32[]{:S(2)}) copy-start(s32[3]{0:T(128)} %constant.58.clone.1) | copy-start | bytes 40
  5.1 19.1 %all-to-all-start = ((bf16[16,2,10,1024]{3,1,2,0:T(2,128)(2,1)}), bf16[16,2,10,1024]{3,1,2,0:T(2,128)(2,1)S(1)}, u32[]{:S(2)}, u32[]{:S(2)}) async-start(bf16[16,2,10,1024]{3,1,2,0:T(2,128)(2,1)} %broadcast_in_dim.70), calls=%async_computation | async-start | bytes 1310720 | tf_op jit(solution)/shard_map/all_to_all | solution.py:18
  24.4 0.9 copy-start.2
  24.4 1.4 %copy-start.3 = (bf16[1024,64]{0,1:T(8,128)(2,1)S(1)}, bf16[1024,64]{0,1:T(8,128)(2,1)}, u32[]{:S(2)}) copy-start(bf16[1024,64]{0,1:T(8,128)(2,1)} %param.19) | copy-start | bytes 393220
  25.3 1.1 copy-start.4
  59.8 3.2 %collective-permute-start = (bf16[2,16,11,128]{3,2,0,1:T(8,128)(2,1)S(1)}, bf16[2,16,11,128]{3,2,0,1:T(8,128)(2,1)S(1)}, u32[]{:S(2)}, u32[]{:S(2)}) collective-permute-start(bf16[2,16,11,128]{3,2,0,1:T(8,128)(2,1)S(1)} %slice.54), channel_id=1, source_target_pairs={{0,1},{1,0},{2,3},{3,2},{4,5},{5,4},{6,7},{7,6},{8,9},{9,8},{10,11... | collective-permute-start | bytes 270344 | tf_op jit(solution)/shard_map/ppermute | solution.py:69
  64.4 17.8 %copy-start.5 = (bf16[64,1024]{1,0:T(8,128)(2,1)S(1)}, bf16[64,1024]{1,0:T(8,128)(2,1)}, u32[]{:S(2)}) copy-start(bf16[64,1024]{1,0:T(8,128)(2,1)} %param.21) | copy-start | bytes 393220
  83.4 16.5 %copy-start.7 = (f32[1024]{0:T(1024)S(1)}, f32[1024]{0:T(1024)}, u32[]{:S(2)}) copy-start(f32[1024]{0:T(1024)} %param.22) | copy-start | bytes 12292
  114.7 1.0 copy-start.1
  115.8 1.0 copy-start.9
  119.4 5.0 %copy-start.10 = (s32[10]{0:T(128)S(1)}, s32[10]{0:T(128)}, u32[]{:S(2)}) copy-start(s32[10]{0:T(128)} %param.16) | copy-start | bytes 124
  119.4 15.0 %copy-start.6 = (bf16[16,2,1024]{2,1,0:T(2,128)(2,1)S(1)}, bf16[16,2,1024]{2,1,0:T(2,128)(2,1)}, u32[]{:S(2)}) copy-start(bf16[16,2,1024]{2,1,0:T(2,128)(2,1)} %param.14) | copy-start | bytes 196612
  119.4 14.5 %all-to-all-start.5 = ((bf16[16,2,10,1024]{3,1,2,0:T(2,128)(2,1)}), bf16[16,2,10,1024]{3,1,2,0:T(2,128)(2,1)S(1)}, u32[]{:S(2)}, u32[]{:S(2)}) async-start(bf16[16,2,10,1024]{3,1,2,0:T(2,128)(2,1)} %copy.96), calls=%async_computation.5 | async-start | bytes 1310720 | tf_op jit(solution)/shard_map/all_to_all | solution.py:25

commit v7 on v6

--- a/solution.py
+++ b/solution.py
@@ -44,6 +44,10 @@
     kept = jnp.take(pixels, clear_index, axis=0)
     kept_rows = jnp.swapaxes(kept, 0, 1)
     spec_here, slots_here, width = kept_rows.shape
+    n_sq = lax.axis_size("band")
+    assert n_sq == lax.axis_size("z")
+    transpose = [(b * n_sq + z, z * n_sq + b) for b in range(n_sq) for z in range(n_sq)]
+    kept_t = lax.ppermute(kept_rows, ("band", "z"), transpose)
     attn_in = band_gather(normed(kept_rows, attn_gain))
     spec = attn_in.shape[0]
     flat = attn_in.reshape(spec * slots_here, width)
@@ -83,25 +87,21 @@
         "shqk,skhd->sqhd", expo.astype(jnp.bfloat16), v, preferred_element_type=jnp.float32
     )
     context = (mixed / jnp.transpose(totals, (0, 2, 1))[..., None]).astype(jnp.bfloat16)
-    context = context.reshape(spec_mine, q_slots, heads_here * HD)
-    context = jnp.swapaxes(context.reshape(spec_mine, n_z, -1), 0, 1).reshape(n_z, -1)
-    context_rows = lax.all_to_all(context, "z", 0, 0, tiled=True)
-    context_rows = context_rows.reshape(spec, slots_here, heads_here * HD)
     out = jnp.dot(
-        context_rows.reshape(spec * slots_here, heads_here * HD),
-        w_out,
-        preferred_element_type=jnp.float32,
+        context.reshape(spec_mine * q_slots, heads_here * HD), w_out, preferred_element_type=jnp.float32
     ).astype(jnp.bfloat16)
-    attn_out = band_reduce(out.reshape(spec, slots_here, width))
-    state = (kept_rows.astype(jnp.float32) + attn_out).astype(jnp.bfloat16)
+    out = jnp.swapaxes(out.reshape(spec_mine, n_z, slots_here, width), 0, 1)
+    attn_out = band_reduce(out.reshape(n_z * spec_mine, slots_here, width))
+    state = (kept_t.astype(jnp.float32) + attn_out).astype(jnp.bfloat16)
     mlp_in = band_gather(normed(state, mlp_gain))
-    piece = mlp_in.reshape(spec * slots_here, width)
+    piece = mlp_in.reshape(-1, width)
     gate = jnp.dot(piece, w_gate, preferred_element_type=jnp.float32)
     upper = jnp.dot(piece, w_up, preferred_element_type=jnp.float32)
     hidden = (jax.nn.silu(gate) * upper).astype(jnp.bfloat16)
     out = jnp.dot(hidden, w_down, preferred_element_type=jnp.float32).astype(jnp.bfloat16)
-    mlp_out = band_reduce(out.reshape(spec, slots_here, width))
-    encoded = (state.astype(jnp.float32) + mlp_out).astype(jnp.bfloat16)
+    mlp_out = band_reduce(out.reshape(mlp_in.shape))
+    encoded_t = (state.astype(jnp.float32) + mlp_out).astype(jnp.bfloat16)
+    encoded = lax.ppermute(encoded_t, ("band", "z"), transpose)
     chosen = (
         jnp.arange(pixels.shape[0], dtype=jnp.int32)[:, None] == clear_index[None, :]
     ) & live_here[None, :]

time: 136 us -> 151 us (1.11)
  the two profiles are of different devices: /device:TPU:2 before, /device:TPU:28 now
where the time goes in v7:
time: 151 us; the launch traced here: 150 us
  blocking collectives  47.4 us (31%)
  starting transfers between devices  36.8 us (24%)
  waiting for transfers between devices  33.3 us (22%)
  local copies, waits for them, and re-layouts  19.6 us (13%)
  other arithmetic  7.75 us (5%)
  matrix products  3.71 us (2%)
    all_to_all x1, blocking collectives, shards(): mine = lax.all_to_all(payload.reshape(n_z, -1), 'z', 0, 0, tiled=True)  27.8 us
    all_to_all x1, blocking collectives, band_gather(): got = lax.all_to_all(sent, 'band', 0, 0, tiled=True)  19.6 us
    all_to_all x2, starting transfers between devices, band_reduce(): got = lax.all_to_all(split, 'band', 0, 0, tiled=True)  15.3 us
    all_to_all x2, waiting for transfers between devices, band_reduce(): got = lax.all_to_all(split, 'band', 0, 0, tiled=True)  13 us
    ppermute x1, waiting for transfers between devices, shards(): encoded = lax.ppermute(encoded_t, ('band', 'z'), transpose)  12.3 us
    all_to_all x1, starting transfers between devices, band_gather(): got = lax.all_to_all(sent, 'band', 0, 0, tiled=True)  8.98 us
    ppermute x1, starting transfers between devices, shards(): encoded = lax.ppermute(encoded_t, ('band', 'z'), transpose)  7.38 us
    ppermute x1, waiting for transfers between devices, shards(): kept_t = lax.ppermute(kept_rows, ('band', 'z'), transpose)  6.78 us
  transfers between devices with their start and end apart: 6, of which 5 were waited for; matrix products, arithmetic and copies ran while one was open for 6% of the time, Pallas kernels for 0%

profile of v7, /device:TPU:28, one launch (start us, length us, event | category | flops | bytes accessed | tf_op | source)
XLA Modules:
  0.0 149.7 jit_solution(14646684298197422682)
XLA Ops:
  0.0 0.7 compare_select_fusion
  1.4 1.5 gather_fusion
  3.0 0.8 fusion.21
  3.9 1.2 broadcast_in_dim.70
  5.1 9.0 %all-to-all-start = ((bf16[16,2,10,1024]{3,1,2,0:T(2,128)(2,1)}), bf16[16,2,10,1024]{3,1,2,0:T(2,128)(2,1)S(1)}, u32[]{:S(2)}, u32[]{:S(2)}) async-start(bf16[16,2,10,1024]{3,1,2,0:T(2,128)(2,1)} %broadcast_in_dim.70), calls=%async_computation | async-start | bytes 1310720 | tf_op jit(solution)/shard_map/all_to_all | solution.py:18
  16.8 5.5 %scatter.4 = bf16[32,1,192]{2,1,0:T(2,128)(2,1)S(1)} dynamic-update-slice(bf16[32,1,192]{2,1,0:T(2,128)(2,1)S(1)} %broadcast_in_dim.71, bf16[32,1,10]{2,1,0:T(2,128)(2,1)S(1)} %broadcast.134, s32[]{:T(128)} %constant.48.clone.1, s32[]{:T(128)} %constant.48.clone.1, s32[]{:T(128)} %bitcast.3) | dynamic-update-slice | bytes 1284 | tf_op jit(solution)/shard_map/scatter | solution.py:65
  26.0 1.4 reduce.15
  27.6 27.8 %all_to_all.30 = bf16[16,2,2112]{2,1,0:T(2,128)(2,1)S(1)} all-to-all(bf16[16,2,2112]{2,1,0:T(2,128)(2,1)S(1)} %reshape.166), channel_id=1, replica_groups=mesh['band'=16,'z'=16,'c'=2] {'z'}, dimensions={0} | all-to-all | bytes 270336 | tf_op jit(solution)/shard_map/all_to_all | solution.py:69
  55.5 0.8 reduce.11
  56.7 1.9 %collective-permute-start.1 = (bf16[2,16,11,128]{3,2,0,1:T(8,128)(2,1)S(1)}, bf16[2,16,11,128]{3,2,0,1:T(8,128)(2,1)S(1)}, u32[]{:S(2)}, u32[]{:S(2)}) collective-permute-start(bf16[2,16,11,128]{3,2,0,1:T(8,128)(2,1)S(1)} %slice.54), channel_id=1, source_target_pairs={{0,1},{1,0},{2,3},{3,2},{4,5},{5,4},{6,7},{7,6},{8,9},{9,8},{10,11... | collective-permute-start | bytes 270344 | tf_op jit(solution)/shard_map/ppermute | solution.py:73
  58.7 1.2 collective-permute-done.1
  62.8 1.5 %copy.59 = bf16[16,2,10,1024]{3,1,2,0:T(2,128)(2,1)} copy(bf16[16,2,10,1024]{3,2,0,1:T(8,128)(2,1)S(1)} %bitcast.44) | data formatting | bytes 1310720 | tf_op jit(solution)/shard_map/transpose | solution.py:93
  64.3 7.8 %all-to-all-start.2 = ((bf16[16,2,10,1024]{3,1,2,0:T(2,128)(2,1)}), bf16[16,2,10,1024]{3,1,2,0:T(2,128)(2,1)S(1)}, u32[]{:S(2)}, u32[]{:S(2)}) async-start(bf16[16,2,10,1024]{3,1,2,0:T(2,128)(2,1)} %copy.59), calls=%async_computation.2 | async-start | bytes 1310720 | tf_op jit(solution)/shard_map/all_to_all | solution.py:25
  72.2 3.3 %collective-permute-start = (bf16[2,10,1024]{2,1,0:T(8,128)(2,1)S(1)}, bf16[2,10,1024]{2,1,0:T(8,128)(2,1)S(1)}, u32[]{:S(2)}, u32[]{:S(2)}) collective-permute-start(bf16[2,10,1024]{2,1,0:T(8,128)(2,1)S(1)} %fusion.28), channel_id=1, source_target_pairs={{0,0},{2,32},{4,64},{6,96},{8,128},{10,160},{12,192},{14,224},{16,... | collective-permute-start | bytes 122888 | tf_op jit(solution)/shard_map/ppermute | solution.py:50
  75.5 5.8 %all-to-all-done.2 = bf16[16,2,10,1024]{3,1,2,0:T(2,128)(2,1)S(1)} async-done(((bf16[16,2,10,1024]{3,1,2,0:T(2,128)(2,1)}), bf16[16,2,10,1024]{3,1,2,0:T(2,128)(2,1)S(1)}, u32[]{:S(2)}, u32[]{:S(2)}) %all-to-all-start.2) | async-done | bytes 655392 | tf_op jit(solution)/shard_map/all_to_all | solution.py:25
  81.9 6.8 %collective-permute-done = bf16[2,10,1024]{2,1,0:T(8,128)(2,1)S(1)} collective-permute-done((bf16[2,10,1024]{2,1,0:T(8,128)(2,1)S(1)}, bf16[2,10,1024]{2,1,0:T(8,128)(2,1)S(1)}, u32[]{:S(2)}, u32[]{:S(2)}) %collective-permute-start) | collective-permute-done | bytes 40992 | tf_op jit(solution)/shard_map/ppermute | solution.py:50
  89.3 19.6 %all_to_all.31 = bf16[16,2,10,1024]{3,1,2,0:T(2,128)(2,1)S(1)} all-to-all(bf16[16,2,10,1024]{3,1,2,0:T(2,128)(2,1)S(1)} %broadcast_in_dim.75), channel_id=1, replica_groups=mesh['band'=16,'z'=16,'c'=2] {'band'}, dimensions={0} | all-to-all | bytes 1310720 | tf_op jit(solution)/shard_map/all_to_all | solution.py:18
  109.4 0.8 copy-done.1
  111.2 0.9 convolution_convert_fusion.1
  112.3 1.5 %copy.63 = bf16[16,2,10,1024]{3,1,2,0:T(2,128)(2,1)} copy(bf16[16,2,10,1024]{3,2,1,0:T(8,128)(2,1)S(1)} %reshape_reshape.11) | data formatting | bytes 1310720 | tf_op jit(solution)/shard_map/reshape;reshape | solution.py:24
  113.8 7.4 %all-to-all-start.4 = ((bf16[16,2,10,1024]{3,1,2,0:T(2,128)(2,1)}), bf16[16,2,10,1024]{3,1,2,0:T(2,128)(2,1)S(1)}, u32[]{:S(2)}, u32[]{:S(2)}) async-start(bf16[16,2,10,1024]{3,1,2,0:T(2,128)(2,1)} %copy.63), calls=%async_computation.4 | async-start | bytes 1310720 | tf_op jit(solution)/shard_map/all_to_all | solution.py:25
  121.2 7.2 %all-to-all-done.4 = bf16[16,2,10,1024]{3,1,2,0:T(2,128)(2,1)S(1)} async-done(((bf16[16,2,10,1024]{3,1,2,0:T(2,128)(2,1)}), bf16[16,2,10,1024]{3,1,2,0:T(2,128)(2,1)S(1)}, u32[]{:S(2)}, u32[]{:S(2)}) %all-to-all-start.4) | async-done | bytes 655392 | tf_op jit(solution)/shard_map/all_to_all | solution.py:25
  129.1 7.4 %collective-permute-start.2 = (bf16[2,10,1024]{2,1,0:T(8,128)(2,1)S(1)}, bf16[2,10,1024]{2,1,0:T(8,128)(2,1)S(1)}, u32[]{:S(2)}, u32[]{:S(2)}) collective-permute-start(bf16[2,10,1024]{2,1,0:T(8,128)(2,1)S(1)} %fusion.25), channel_id=1, source_target_pairs={{0,0},{2,32},{4,64},{6,96},{8,128},{10,160},{12,192},{14,224},{16,... | collective-permute-start | bytes 122888 | tf_op jit(solution)/shard_map/ppermute | solution.py:104
  136.6 12.3 %collective-permute-done.2 = bf16[2,10,1024]{2,1,0:T(8,128)(2,1)S(1)} collective-permute-done((bf16[2,10,1024]{2,1,0:T(8,128)(2,1)S(1)}, bf16[2,10,1024]{2,1,0:T(8,128)(2,1)S(1)}, u32[]{:S(2)}, u32[]{:S(2)}) %collective-permute-start.2) | collective-permute-done | bytes 40992 | tf_op jit(solution)/shard_map/ppermute | solution.py:104
  (82 shorter events, 14.5 us)
Async XLA Ops:
  0.0 110.5 %copy-start = (bf16[256,1024]{1,0:T(8,128)(2,1)S(1)}, bf16[256,1024]{1,0:T(8,128)(2,1)}, u32[]{:S(2)}) copy-start(bf16[256,1024]{1,0:T(8,128)(2,1)} %param.25) | copy-start | bytes 1572868
  3.8 11.5 %copy-start.9 = (s32[3]{0:T(128)S(1)}, s32[3]{0:T(128)}, u32[]{:S(2)}) copy-start(s32[3]{0:T(128)} %constant.58.clone.1) | copy-start | bytes 40
  5.1 17.2 %all-to-all-start = ((bf16[16,2,10,1024]{3,1,2,0:T(2,128)(2,1)}), bf16[16,2,10,1024]{3,1,2,0:T(2,128)(2,1)S(1)}, u32[]{:S(2)}, u32[]{:S(2)}) async-start(bf16[16,2,10,1024]{3,1,2,0:T(2,128)(2,1)} %broadcast_in_dim.70), calls=%async_computation | async-start | bytes 1310720 | tf_op jit(solution)/shard_map/all_to_all | solution.py:18
  22.5 0.9 copy-start.3
  22.5 1.4 copy-start.4
  23.4 1.1 copy-start.5
  56.7 3.2 %collective-permute-start.1 = (bf16[2,16,11,128]{3,2,0,1:T(8,128)(2,1)S(1)}, bf16[2,16,11,128]{3,2,0,1:T(8,128)(2,1)S(1)}, u32[]{:S(2)}, u32[]{:S(2)}) collective-permute-start(bf16[2,16,11,128]{3,2,0,1:T(8,128)(2,1)S(1)} %slice.54), channel_id=1, source_target_pairs={{0,1},{1,0},{2,3},{3,2},{4,5},{5,4},{6,7},{7,6},{8,9},{9,8},{10,11... | collective-permute-start | bytes 270344 | tf_op jit(solution)/shard_map/ppermute | solution.py:73
  61.3 0.9 copy-start.6
  64.3 24.5 %copy-start.7 = (f32[1024]{0:T(1024)S(1)}, f32[1024]{0:T(1024)}, u32[]{:S(2)}) copy-start(f32[1024]{0:T(1024)} %param.22) | copy-start | bytes 12292
  64.3 17.0 %all-to-all-start.2 = ((bf16[16,2,10,1024]{3,1,2,0:T(2,128)(2,1)}), bf16[16,2,10,1024]{3,1,2,0:T(2,128)(2,1)S(1)}, u32[]{:S(2)}, u32[]{:S(2)}) async-start(bf16[16,2,10,1024]{3,1,2,0:T(2,128)(2,1)} %copy.59), calls=%async_computation.2 | async-start | bytes 1310720 | tf_op jit(solution)/shard_map/all_to_all | solution.py:25
  72.2 16.4 %collective-permute-start = (bf16[2,10,1024]{2,1,0:T(8,128)(2,1)S(1)}, bf16[2,10,1024]{2,1,0:T(8,128)(2,1)S(1)}, u32[]{:S(2)}, u32[]{:S(2)}) collective-permute-start(bf16[2,10,1024]{2,1,0:T(8,128)(2,1)S(1)} %fusion.28), channel_id=1, source_target_pairs={{0,0},{2,32},{4,64},{6,96},{8,128},{10,160},{12,192},{14,224},{16,... | collective-permute-start | bytes 122888 | tf_op jit(solution)/shard_map/ppermute | solution.py:50
  109.1 1.0 copy-start.1
  110.2 1.0 copy-start.10
  113.8 22.6 %copy-start.8 = (s32[10]{0:T(128)S(1)}, s32[10]{0:T(128)}, u32[]{:S(2)}) copy-start(s32[10]{0:T(128)} %param.16) | copy-start | bytes 124
  113.8 35.1 %copy-start.2 = (bf16[16,2,1024]{2,1,0:T(2,128)(2,1)S(1)}, bf16[16,2,1024]{2,1,0:T(2,128)(2,1)}, u32[]{:S(2)}) copy-start(bf16[16,2,1024]{2,1,0:T(2,128)(2,1)} %param.14) | copy-start | bytes 196612
  113.8 14.6 %all-to-all-start.4 = ((bf16[16,2,10,1024]{3,1,2,0:T(2,128)(2,1)}), bf16[16,2,10,1024]{3,1,2,0:T(2,128)(2,1)S(1)}, u32[]{:S(2)}, u32[]{:S(2)}) async-start(bf16[16,2,10,1024]{3,1,2,0:T(2,128)(2,1)} %copy.63), calls=%async_computation.4 | async-start | bytes 1310720 | tf_op jit(solution)/shard_map/all_to_all | solution.py:25
  129.1 19.8 %collective-permute-start.2 = (bf16[2,10,1024]{2,1,0:T(8,128)(2,1)S(1)}, bf16[2,10,1024]{2,1,0:T(8,128)(2,1)S(1)}, u32[]{:S(2)}, u32[]{:S(2)}) collective-permute-start(bf16[2,10,1024]{2,1,0:T(8,128)(2,1)S(1)} %fusion.25), channel_id=1, source_target_pairs={{0,0},{2,32},{4,64},{6,96},{8,128},{10,160},{12,192},{14,224},{16,... | collective-permute-start | bytes 122888 | tf_op jit(solution)/shard_map/ppermute | solution.py:104

commit v8 on v6

--- a/solution.py
+++ b/solution.py
@@ -23,6 +23,11 @@
     n = lax.axis_size("band")
     split = part.reshape((n, part.shape[0] // n) + part.shape[1:])
     got = lax.all_to_all(split, "band", 0, 0, tiled=True)
+    return jnp.sum(got.astype(jnp.float32), axis=0)
+
+
+def band_sum(part):
+    got = lax.all_to_all(jnp.swapaxes(part, 1, 2), "band", 0, 0, tiled=True)
     return jnp.sum(got.astype(jnp.float32), axis=0)
 
 
@@ -87,20 +92,20 @@
     context = jnp.swapaxes(context.reshape(spec_mine, n_z, -1), 0, 1).reshape(n_z, -1)
     context_rows = lax.all_to_all(context, "z", 0, 0, tiled=True)
     context_rows = context_rows.reshape(spec, slots_here, heads_here * HD)
-    out = jnp.dot(
-        context_rows.reshape(spec * slots_here, heads_here * HD),
-        w_out,
-        preferred_element_type=jnp.float32,
-    ).astype(jnp.bfloat16)
-    attn_out = band_reduce(out.reshape(spec, slots_here, width))
+    n_band = lax.axis_size("band")
+    context_rows = context_rows.reshape(n_band, spec_here, slots_here, heads_here * HD)
+    context_rows = jnp.swapaxes(context_rows, 1, 2).reshape(spec * slots_here, heads_here * HD)
+    out = jnp.dot(context_rows, w_out, preferred_element_type=jnp.float32).astype(jnp.bfloat16)
+    attn_out = band_sum(out.reshape(n_band, slots_here, spec_here, width))
     state = (kept_rows.astype(jnp.float32) + attn_out).astype(jnp.bfloat16)
     mlp_in = band_gather(normed(state, mlp_gain))
-    piece = mlp_in.reshape(spec * slots_here, width)
+    piece = jnp.swapaxes(mlp_in.reshape(n_band, spec_here, slots_here, width), 1, 2)
+    piece = piece.reshape(spec * slots_here, width)
     gate = jnp.dot(piece, w_gate, preferred_element_type=jnp.float32)
     upper = jnp.dot(piece, w_up, preferred_element_type=jnp.float32)
     hidden = (jax.nn.silu(gate) * upper).astype(jnp.bfloat16)
     out = jnp.dot(hidden, w_down, preferred_element_type=jnp.float32).astype(jnp.bfloat16)
-    mlp_out = band_reduce(out.reshape(spec, slots_here, width))
+    mlp_out = band_sum(out.reshape(n_band, slots_here, spec_here, width))
     encoded = (state.astype(jnp.float32) + mlp_out).astype(jnp.bfloat16)
     chosen = (
         jnp.arange(pixels.shape[0], dtype=jnp.int32)[:, None] == clear_index[None, :]

time: 136 us -> 134 us (0.985)
  local copies, waits for them, and re-layouts: 18.6 us -> 16.4 us
    another operation x8 -> x3, local copies, waits for them, and re-layouts: 3.6 us -> 0.8 us  [the longest x4 2.61 us: band_reduce(): split = part.reshape((n, part.shape[0] // n) + part.shape[1:])]
    reshape x0 -> x3, local copies, waits for them, and re-layouts: none -> 1.58 us  [the longest x1 1.08 us: shards(): mlp_out = band_sum(out.reshape(n_band, slots_here, spec_here, width))]
where the time goes in v8:
time: 134 us
  blocking collectives  75 us (56%)
  local copies, waits for them, and re-layouts  16.4 us (12%)
  starting transfers between devices  16.2 us (12%)
  waiting for transfers between devices  12.2 us (9%)
  other arithmetic  8.91 us (7%)
  matrix products  3.68 us (3%)
    all_to_all x1, blocking collectives, shards(): mine = lax.all_to_all(payload.reshape(n_z, -1), 'z', 0, 0, tiled=True)  29 us
    all_to_all x1, blocking collectives, band_sum(): got = lax.all_to_all(jnp.swapaxes(part, 1, 2), 'band', 0, 0, tiled=True)  15.9 us
    all_to_all x1, blocking collectives, shards(): context_rows = lax.all_to_all(context, 'z', 0, 0, tiled=True)  15.8 us
    all_to_all x1, blocking collectives, band_gather(): got = lax.all_to_all(sent, 'band', 0, 0, tiled=True)  14.3 us
    all_to_all x1, waiting for transfers between devices, band_sum(): got = lax.all_to_all(jnp.swapaxes(part, 1, 2), 'band', 0, 0, tiled=True)  9.43 us
    all_to_all x1, starting transfers between devices, band_gather(): got = lax.all_to_all(sent, 'band', 0, 0, tiled=True)  9.26 us
    scatter x1, local copies, waits for them, and re-layouts, shards(): flag_row.at[:, 0, at:at + slots_here]  5.51 us
    all_to_all x1, starting transfers between devices, band_sum(): got = lax.all_to_all(jnp.swapaxes(part, 1, 2), 'band', 0, 0, tiled=True)  4.97 us
  transfers between devices with their start and end apart: 3, of which 3 were waited for; matrix products, arithmetic and copies ran while one was open for 6% of the time, Pallas kernels for 0%

profile of v8, /device:TPU:2, one launch (start us, length us, event | category | flops | bytes accessed | tf_op | source)
XLA Modules:
  0.0 133.6 jit_solution(14417136246832270921)
XLA Ops:
  0.0 0.7 compare_select_fusion
  0.7 0.7 compare_and_fusion
  1.4 1.5 %gather_fusion = bf16[10,2,1024]{2,1,0:T(2,128)(2,1)S(1)} fusion(bf16[16,2,1024]{2,1,0:T(2,128)(2,1)} %param.14, s32[1024]{0:T(1024)S(1)} %pad_clamp_fusion), kind=kCustom, calls=%fused_computation | custom fusion | bytes 81960 | tf_op jit(solution)/shard_map/jit(_take)/gather | solution.py:49
  3.1 0.8 fusion.25
  3.9 1.2 broadcast_in_dim.70
  5.1 9.3 %all-to-all-start = ((bf16[16,2,10,1024]{3,1,2,0:T(2,128)(2,1)}), bf16[16,2,10,1024]{3,1,2,0:T(2,128)(2,1)S(1)}, u32[]{:S(2)}, u32[]{:S(2)}) async-start(bf16[16,2,10,1024]{3,1,2,0:T(2,128)(2,1)} %broadcast_in_dim.70), calls=%async_computation | async-start | bytes 1310720 | tf_op jit(solution)/shard_map/all_to_all | solution.py:18
  15.6 0.7 and_reduce_fusion
  17.1 5.5 %scatter.4 = bf16[32,1,192]{2,1,0:T(2,128)(2,1)S(1)} dynamic-update-slice(bf16[32,1,192]{2,1,0:T(2,128)(2,1)S(1)} %broadcast_in_dim.71, bf16[32,1,10]{2,1,0:T(2,128)(2,1)S(1)} %broadcast.134, s32[]{:T(128)} %constant.48.clone.1, s32[]{:T(128)} %constant.48.clone.1, s32[]{:T(128)} %bitcast.3) | dynamic-update-slice | bytes 1284 | tf_op jit(solution)/shard_map/scatter | solution.py:66
  22.6 1.6 %all-to-all-done = bf16[16,2,10,1024]{3,1,2,0:T(2,128)(2,1)S(1)} async-done(((bf16[16,2,10,1024]{3,1,2,0:T(2,128)(2,1)}), bf16[16,2,10,1024]{3,1,2,0:T(2,128)(2,1)S(1)}, u32[]{:S(2)}, u32[]{:S(2)}) %all-to-all-start) | async-done | bytes 655392 | tf_op jit(solution)/shard_map/all_to_all | solution.py:18
  27.9 1.4 %reduce.16 = bf16[16,4224]{1,0:T(8,128)(2,1)S(1)} reduce(bf16[16,1,4224]{2,1,0:T(2,128)(2,1)S(1)} %all_to_all.32, bf16[]{:T(256)} %broadcast.150), dimensions={1}, to_apply=%all_to_all.32.reduce_sub_computation | reduce | bytes 270338 | tf_op jit(solution)/shard_map/all_to_all | solution.py:70
  29.4 29.0 %all_to_all.40 = bf16[16,2,2112]{2,1,0:T(2,128)(2,1)S(1)} all-to-all(bf16[16,2,2112]{2,1,0:T(2,128)(2,1)S(1)} %reshape.180), channel_id=1, replica_groups=mesh['band'=16,'z'=16,'c'=2] {'z'}, dimensions={0} | all-to-all | bytes 270336 | tf_op jit(solution)/shard_map/all_to_all | solution.py:70
  58.6 0.8 reduce.11
  59.8 1.9 %collective-permute-start = (bf16[2,16,11,128]{3,2,0,1:T(8,128)(2,1)S(1)}, bf16[2,16,11,128]{3,2,0,1:T(8,128)(2,1)S(1)}, u32[]{:S(2)}, u32[]{:S(2)}) collective-permute-start(bf16[2,16,11,128]{3,2,0,1:T(8,128)(2,1)S(1)} %slice.54), channel_id=1, source_target_pairs={{0,1},{1,0},{2,3},{3,2},{4,5},{5,4},{6,7},{7,6},{8,9},{9,8},{10,11... | collective-permute-start | bytes 270344 | tf_op jit(solution)/shard_map/ppermute | solution.py:74
  61.8 1.2 collective-permute-done
  65.1 0.9 reduce.17
  66.0 15.8 %all_to_all.41 = bf16[16,2,640]{2,1,0:T(2,128)(2,1)S(1)} all-to-all(bf16[16,2,640]{2,1,0:T(2,128)(2,1)S(1)} %reshape.182), channel_id=1, replica_groups=mesh['band'=16,'z'=16,'c'=2] {'z'}, dimensions={0} | all-to-all | bytes 81920 | tf_op jit(solution)/shard_map/all_to_all | solution.py:93
  82.9 15.9 %all_to_all.42 = bf16[16,2,10,1024]{3,1,2,0:T(2,128)(2,1)S(1)} all-to-all(bf16[16,2,10,1024]{3,1,2,0:T(2,128)(2,1)S(1)} %bitcast.57), channel_id=1, replica_groups=mesh['band'=16,'z'=16,'c'=2] {'band'}, dimensions={0} | all-to-all | bytes 1310720 | tf_op jit(solution)/shard_map/all_to_all | solution.py:30
  100.0 14.3 %all_to_all.43 = bf16[16,2,10,1024]{3,1,2,0:T(2,128)(2,1)S(1)} all-to-all(bf16[16,2,10,1024]{3,1,2,0:T(2,128)(2,1)S(1)} %broadcast_in_dim.75), channel_id=1, replica_groups=mesh['band'=16,'z'=16,'c'=2] {'band'}, dimensions={0} | all-to-all | bytes 1310720 | tf_op jit(solution)/shard_map/all_to_all | solution.py:18
  114.9 0.7 copy-done.9
  115.6 0.9 convolution_convert_fusion.1
  116.5 1.1 reshape.166
  117.6 5.0 %all-to-all-start.5 = ((bf16[16,2,10,1024]{3,1,2,0:T(2,128)(2,1)}), bf16[16,2,10,1024]{3,1,2,0:T(2,128)(2,1)S(1)}, u32[]{:S(2)}, u32[]{:S(2)}) async-start(bf16[16,2,10,1024]{3,1,2,0:T(2,128)(2,1)} %bitcast.14), calls=%async_computation.5 | async-start | bytes 1310720 | tf_op jit(solution)/shard_map/all_to_all | solution.py:30
  122.7 9.4 %all-to-all-done.5 = bf16[16,2,10,1024]{3,1,2,0:T(2,128)(2,1)S(1)} async-done(((bf16[16,2,10,1024]{3,1,2,0:T(2,128)(2,1)}), bf16[16,2,10,1024]{3,1,2,0:T(2,128)(2,1)S(1)}, u32[]{:S(2)}, u32[]{:S(2)}) %all-to-all-start.5) | async-done | bytes 655392 | tf_op jit(solution)/shard_map/all_to_all | solution.py:30
  132.9 0.7 copy.49
  (80 shorter events, 11.6 us)
Async XLA Ops:
  0.0 114.9 %copy-start = (bf16[256,1024]{1,0:T(8,128)(2,1)S(1)}, bf16[256,1024]{1,0:T(8,128)(2,1)}, u32[]{:S(2)}) copy-start(bf16[256,1024]{1,0:T(8,128)(2,1)} %param.25) | copy-start | bytes 1572868
  3.1 12.6 %copy-start.8 = (s32[3]{0:T(128)S(1)}, s32[3]{0:T(128)}, u32[]{:S(2)}) copy-start(s32[3]{0:T(128)} %constant.58.clone.1) | copy-start | bytes 40
  5.1 19.1 %all-to-all-start = ((bf16[16,2,10,1024]{3,1,2,0:T(2,128)(2,1)}), bf16[16,2,10,1024]{3,1,2,0:T(2,128)(2,1)S(1)}, u32[]{:S(2)}, u32[]{:S(2)}) async-start(bf16[16,2,10,1024]{3,1,2,0:T(2,128)(2,1)} %broadcast_in_dim.70), calls=%async_computation | async-start | bytes 1310720 | tf_op jit(solution)/shard_map/all_to_all | solution.py:18
  24.4 0.9 copy-start.2
  24.4 1.4 %copy-start.3 = (bf16[1024,64]{0,1:T(8,128)(2,1)S(1)}, bf16[1024,64]{0,1:T(8,128)(2,1)}, u32[]{:S(2)}) copy-start(bf16[1024,64]{0,1:T(8,128)(2,1)} %param.19) | copy-start | bytes 393220
  25.3 1.1 copy-start.4
  59.8 3.2 %collective-permute-start = (bf16[2,16,11,128]{3,2,0,1:T(8,128)(2,1)S(1)}, bf16[2,16,11,128]{3,2,0,1:T(8,128)(2,1)S(1)}, u32[]{:S(2)}, u32[]{:S(2)}) collective-permute-start(bf16[2,16,11,128]{3,2,0,1:T(8,128)(2,1)S(1)} %slice.54), channel_id=1, source_target_pairs={{0,1},{1,0},{2,3},{3,2},{4,5},{5,4},{6,7},{7,6},{8,9},{9,8},{10,11... | collective-permute-start | bytes 270344 | tf_op jit(solution)/shard_map/ppermute | solution.py:74
  64.4 17.9 %copy-start.5 = (bf16[64,1024]{1,0:T(8,128)(2,1)S(1)}, bf16[64,1024]{1,0:T(8,128)(2,1)}, u32[]{:S(2)}) copy-start(bf16[64,1024]{1,0:T(8,128)(2,1)} %param.21) | copy-start | bytes 393220
  82.9 16.6 %copy-start.7 = (f32[1024]{0:T(1024)S(1)}, f32[1024]{0:T(1024)}, u32[]{:S(2)}) copy-start(f32[1024]{0:T(1024)} %param.22) | copy-start | bytes 12292
  100.0 14.6 %copy-start.1 = (bf16[1024,256]{1,0:T(8,128)(2,1)S(1)}, bf16[1024,256]{1,0:T(8,128)(2,1)}, u32[]{:S(2)}) copy-start(bf16[1024,256]{1,0:T(8,128)(2,1)} %param.23) | copy-start | bytes 1572868
  114.5 1.0 copy-start.9
  116.5 6.1 %copy-start.10 = (s32[10]{0:T(128)S(1)}, s32[10]{0:T(128)}, u32[]{:S(2)}) copy-start(s32[10]{0:T(128)} %param.16) | copy-start | bytes 124
  117.6 15.2 %copy-start.6 = (bf16[16,2,1024]{2,1,0:T(2,128)(2,1)S(1)}, bf16[16,2,1024]{2,1,0:T(2,128)(2,1)}, u32[]{:S(2)}) copy-start(bf16[16,2,1024]{2,1,0:T(2,128)(2,1)} %param.14) | copy-start | bytes 196612
  117.6 14.5 %all-to-all-start.5 = ((bf16[16,2,10,1024]{3,1,2,0:T(2,128)(2,1)}), bf16[16,2,10,1024]{3,1,2,0:T(2,128)(2,1)S(1)}, u32[]{:S(2)}, u32[]{:S(2)}) async-start(bf16[16,2,10,1024]{3,1,2,0:T(2,128)(2,1)} %bitcast.14), calls=%async_computation.5 | async-start | bytes 1310720 | tf_op jit(solution)/shard_map/all_to_all | solution.py:30

commit v9 on v8

--- a/solution.py
+++ b/solution.py
@@ -67,7 +67,7 @@
     payload = jnp.concatenate([qkv, flag_row], axis=1)
     n_z = lax.axis_size("z")
     spec_mine = spec // n_z
-    mine = lax.all_to_all(payload.reshape(n_z, -1), "z", 0, 0, tiled=True)
+    mine = lax.all_to_all(payload.reshape(n_z, spec_mine, -1), "z", 0, 0, tiled=True)
     mine = mine.reshape(n_z, spec_mine, slots_here + 1, width_qkv)
     mine = jnp.swapaxes(mine, 0, 1)
     kv_flag = mine[..., heads_here * HD :]
@@ -89,7 +89,7 @@
     )
     context = (mixed / jnp.transpose(totals, (0, 2, 1))[..., None]).astype(jnp.bfloat16)
     context = context.reshape(spec_mine, q_slots, heads_here * HD)
-    context = jnp.swapaxes(context.reshape(spec_mine, n_z, -1), 0, 1).reshape(n_z, -1)
+    context = jnp.swapaxes(context.reshape(spec_mine, n_z, -1), 0, 1)
     context_rows = lax.all_to_all(context, "z", 0, 0, tiled=True)
     context_rows = context_rows.reshape(spec, slots_here, heads_here * HD)
     n_band = lax.axis_size("band")

time: 134 us -> 130 us (0.970)
  other arithmetic: 8.91 us -> 5.63 us
    all_to_all x4 -> x0, other arithmetic: 3.28 us -> none  [the longest x2 2.19 us: shards(): mine = lax.all_to_all(payload.reshape(n_z, -1), 'z', 0, 0, tiled=True)]
where the time goes in v9:
time: 130 us; the launch traced here: 129 us
  blocking collectives  75 us (58%)
  starting transfers between devices  16.2 us (12%)
  local copies, waits for them, and re-layouts  15.6 us (12%)
  waiting for transfers between devices  12.2 us (9%)
  other arithmetic  5.63 us (4%)
  matrix products  3.68 us (3%)
    all_to_all x1, blocking collectives, shards(): lax.all_to_all(payload.reshape(n_z, spec_mine, -1), 'z', 0, 0, tiled=True)  29 us
    all_to_all x1, blocking collectives, band_sum(): got = lax.all_to_all(jnp.swapaxes(part, 1, 2), 'band', 0, 0, tiled=True)  15.9 us
    all_to_all x1, blocking collectives, shards(): context_rows = lax.all_to_all(context, 'z', 0, 0, tiled=True)  15.8 us
    all_to_all x1, blocking collectives, band_gather(): got = lax.all_to_all(sent, 'band', 0, 0, tiled=True)  14.3 us
    all_to_all x1, waiting for transfers between devices, band_sum(): got = lax.all_to_all(jnp.swapaxes(part, 1, 2), 'band', 0, 0, tiled=True)  9.44 us
    all_to_all x1, starting transfers between devices, band_gather(): got = lax.all_to_all(sent, 'band', 0, 0, tiled=True)  9.26 us
    scatter x1, local copies, waits for them, and re-layouts, shards(): flag_row.at[:, 0, at:at + slots_here]  5.51 us
    all_to_all x1, starting transfers between devices, band_sum(): got = lax.all_to_all(jnp.swapaxes(part, 1, 2), 'band', 0, 0, tiled=True)  4.97 us
  transfers between devices with their start and end apart: 3, of which 3 were waited for; matrix products, arithmetic and copies ran while one was open for 6% of the time, Pallas kernels for 0%

profile of v9, /device:TPU:2, one launch (start us, length us, event | category | flops | bytes accessed | tf_op | source)
XLA Modules:
  0.0 129.4 jit_solution(4295050972060248527)
XLA Ops:
  0.0 0.7 compare_select_fusion
  0.7 0.7 compare_and_fusion
  1.4 1.5 %gather_fusion = bf16[10,2,1024]{2,1,0:T(2,128)(2,1)S(1)} fusion(bf16[16,2,1024]{2,1,0:T(2,128)(2,1)} %param.14, s32[1024]{0:T(1024)S(1)} %pad_clamp_fusion), kind=kCustom, calls=%fused_computation | custom fusion | bytes 81960 | tf_op jit(solution)/shard_map/jit(_take)/gather | solution.py:49
  3.1 0.8 fusion.25
  3.9 1.2 broadcast_in_dim.70
  5.1 9.3 %all-to-all-start = ((bf16[16,2,10,1024]{3,1,2,0:T(2,128)(2,1)}), bf16[16,2,10,1024]{3,1,2,0:T(2,128)(2,1)S(1)}, u32[]{:S(2)}, u32[]{:S(2)}) async-start(bf16[16,2,10,1024]{3,1,2,0:T(2,128)(2,1)} %broadcast_in_dim.70), calls=%async_computation | async-start | bytes 1310720 | tf_op jit(solution)/shard_map/all_to_all | solution.py:18
  15.0 0.6 slice.45
  15.6 0.7 and_reduce_fusion
  16.3 0.6 broadcast_select_fusion.1
  17.1 5.5 %scatter.4 = bf16[32,1,192]{2,1,0:T(2,128)(2,1)S(1)} dynamic-update-slice(bf16[32,1,192]{2,1,0:T(2,128)(2,1)S(1)} %broadcast_in_dim.71, bf16[32,1,10]{2,1,0:T(2,128)(2,1)S(1)} %broadcast.134, s32[]{:T(128)} %constant.48.clone.1, s32[]{:T(128)} %constant.48.clone.1, s32[]{:T(128)} %bitcast.3) | dynamic-update-slice | bytes 1284 | tf_op jit(solution)/shard_map/scatter | solution.py:66
  22.6 1.6 %all-to-all-done = bf16[16,2,10,1024]{3,1,2,0:T(2,128)(2,1)S(1)} async-done(((bf16[16,2,10,1024]{3,1,2,0:T(2,128)(2,1)}), bf16[16,2,10,1024]{3,1,2,0:T(2,128)(2,1)S(1)}, u32[]{:S(2)}, u32[]{:S(2)}) %all-to-all-start) | async-done | bytes 655392 | tf_op jit(solution)/shard_map/all_to_all | solution.py:18
  24.7 0.6 copy-done.2
  27.3 29.0 %all_to_all.30 = bf16[16,2,2112]{2,1,0:T(2,128)(2,1)S(1)} all-to-all(bf16[16,2,2112]{2,1,0:T(2,128)(2,1)S(1)} %reshape.153), channel_id=1, replica_groups=mesh['band'=16,'z'=16,'c'=2] {'z'}, dimensions={0} | all-to-all | bytes 270336 | tf_op jit(solution)/shard_map/all_to_all | solution.py:70
  56.7 1.9 %collective-permute-start = (bf16[2,16,11,128]{3,2,1,0:T(8,128)(2,1)S(1)}, bf16[2,16,11,128]{3,2,1,0:T(8,128)(2,1)S(1)}, u32[]{:S(2)}, u32[]{:S(2)}) collective-permute-start(bf16[2,16,11,128]{3,2,1,0:T(8,128)(2,1)S(1)} %slice.54), channel_id=1, source_target_pairs={{0,1},{1,0},{2,3},{3,2},{4,5},{5,4},{6,7},{7,6},{8,9},{9,8},{10,11... | collective-permute-start | bytes 270344 | tf_op jit(solution)/shard_map/ppermute | solution.py:74
  58.8 1.2 collective-permute-done
  62.0 15.8 %all_to_all.31 = bf16[16,2,640]{2,1,0:T(2,128)(2,1)S(1)} all-to-all(bf16[16,2,640]{2,1,0:T(2,128)(2,1)S(1)} %copy.44), channel_id=1, replica_groups=mesh['band'=16,'z'=16,'c'=2] {'z'}, dimensions={0} | all-to-all | bytes 81920 | tf_op jit(solution)/shard_map/all_to_all | solution.py:93
  78.7 15.9 %all_to_all.32 = bf16[16,2,10,1024]{3,1,2,0:T(2,128)(2,1)S(1)} all-to-all(bf16[16,2,10,1024]{3,1,2,0:T(2,128)(2,1)S(1)} %bitcast.61), channel_id=1, replica_groups=mesh['band'=16,'z'=16,'c'=2] {'band'}, dimensions={0} | all-to-all | bytes 1310720 | tf_op jit(solution)/shard_map/all_to_all | solution.py:30
  95.8 14.3 %all_to_all.33 = bf16[16,2,10,1024]{3,1,2,0:T(2,128)(2,1)S(1)} all-to-all(bf16[16,2,10,1024]{3,1,2,0:T(2,128)(2,1)S(1)} %broadcast_in_dim.75), channel_id=1, replica_groups=mesh['band'=16,'z'=16,'c'=2] {'band'}, dimensions={0} | all-to-all | bytes 1310720 | tf_op jit(solution)/shard_map/all_to_all | solution.py:18
  110.7 0.7 copy-done.9
  111.4 0.9 convolution_convert_fusion.1
  112.3 1.1 reshape.160
  113.4 5.0 %all-to-all-start.5 = ((bf16[16,2,10,1024]{3,1,2,0:T(2,128)(2,1)}), bf16[16,2,10,1024]{3,1,2,0:T(2,128)(2,1)S(1)}, u32[]{:S(2)}, u32[]{:S(2)}) async-start(bf16[16,2,10,1024]{3,1,2,0:T(2,128)(2,1)} %bitcast.14), calls=%async_computation.5 | async-start | bytes 1310720 | tf_op jit(solution)/shard_map/all_to_all | solution.py:30
  118.5 9.4 %all-to-all-done.5 = bf16[16,2,10,1024]{3,1,2,0:T(2,128)(2,1)S(1)} async-done(((bf16[16,2,10,1024]{3,1,2,0:T(2,128)(2,1)}), bf16[16,2,10,1024]{3,1,2,0:T(2,128)(2,1)S(1)}, u32[]{:S(2)}, u32[]{:S(2)}) %all-to-all-start.5) | async-done | bytes 655392 | tf_op jit(solution)/shard_map/all_to_all | solution.py:30
  128.7 0.7 copy.49
  (72 shorter events, 8.6 us)
Async XLA Ops:
  0.0 110.7 %copy-start = (bf16[256,1024]{1,0:T(8,128)(2,1)S(1)}, bf16[256,1024]{1,0:T(8,128)(2,1)}, u32[]{:S(2)}) copy-start(bf16[256,1024]{1,0:T(8,128)(2,1)} %param.25) | copy-start | bytes 1572868
  3.1 12.6 %copy-start.8 = (s32[3]{0:T(128)S(1)}, s32[3]{0:T(128)}, u32[]{:S(2)}) copy-start(s32[3]{0:T(128)} %constant.58.clone.1) | copy-start | bytes 40
  5.1 19.1 %all-to-all-start = ((bf16[16,2,10,1024]{3,1,2,0:T(2,128)(2,1)}), bf16[16,2,10,1024]{3,1,2,0:T(2,128)(2,1)S(1)}, u32[]{:S(2)}, u32[]{:S(2)}) async-start(bf16[16,2,10,1024]{3,1,2,0:T(2,128)(2,1)} %broadcast_in_dim.70), calls=%async_computation | async-start | bytes 1310720 | tf_op jit(solution)/shard_map/all_to_all | solution.py:18
  24.4 0.9 copy-start.2
  24.4 1.4 %copy-start.3 = (bf16[1024,64]{0,1:T(8,128)(2,1)S(1)}, bf16[1024,64]{0,1:T(8,128)(2,1)}, u32[]{:S(2)}) copy-start(bf16[1024,64]{0,1:T(8,128)(2,1)} %param.19) | copy-start | bytes 393220
  25.3 1.1 copy-start.4
  56.7 3.2 %collective-permute-start = (bf16[2,16,11,128]{3,2,1,0:T(8,128)(2,1)S(1)}, bf16[2,16,11,128]{3,2,1,0:T(8,128)(2,1)S(1)}, u32[]{:S(2)}, u32[]{:S(2)}) collective-permute-start(bf16[2,16,11,128]{3,2,1,0:T(8,128)(2,1)S(1)} %slice.54), channel_id=1, source_target_pairs={{0,1},{1,0},{2,3},{3,2},{4,5},{5,4},{6,7},{7,6},{8,9},{9,8},{10,11... | collective-permute-start | bytes 270344 | tf_op jit(solution)/shard_map/ppermute | solution.py:74
  61.4 16.7 %copy-start.5 = (bf16[64,1024]{1,0:T(8,128)(2,1)S(1)}, bf16[64,1024]{1,0:T(8,128)(2,1)}, u32[]{:S(2)}) copy-start(bf16[64,1024]{1,0:T(8,128)(2,1)} %param.21) | copy-start | bytes 393220
  78.7 16.6 %copy-start.7 = (f32[1024]{0:T(1024)S(1)}, f32[1024]{0:T(1024)}, u32[]{:S(2)}) copy-start(f32[1024]{0:T(1024)} %param.22) | copy-start | bytes 12292
  95.8 14.6 %copy-start.1 = (bf16[1024,256]{1,0:T(8,128)(2,1)S(1)}, bf16[1024,256]{1,0:T(8,128)(2,1)}, u32[]{:S(2)}) copy-start(bf16[1024,256]{1,0:T(8,128)(2,1)} %param.23) | copy-start | bytes 1572868
  110.4 1.0 copy-start.9
  112.3 6.1 %copy-start.10 = (s32[10]{0:T(128)S(1)}, s32[10]{0:T(128)}, u32[]{:S(2)}) copy-start(s32[10]{0:T(128)} %param.16) | copy-start | bytes 124
  113.4 15.2 %copy-start.6 = (bf16[16,2,1024]{2,1,0:T(2,128)(2,1)S(1)}, bf16[16,2,1024]{2,1,0:T(2,128)(2,1)}, u32[]{:S(2)}) copy-start(bf16[16,2,1024]{2,1,0:T(2,128)(2,1)} %param.14) | copy-start | bytes 196612
  113.4 14.5 %all-to-all-start.5 = ((bf16[16,2,10,1024]{3,1,2,0:T(2,128)(2,1)}), bf16[16,2,10,1024]{3,1,2,0:T(2,128)(2,1)S(1)}, u32[]{:S(2)}, u32[]{:S(2)}) async-start(bf16[16,2,10,1024]{3,1,2,0:T(2,128)(2,1)} %bitcast.14), calls=%async_computation.5 | async-start | bytes 1310720 | tf_op jit(solution)/shard_map/all_to_all | solution.py:30

commit v10 on v9

--- a/solution.py
+++ b/solution.py
@@ -15,19 +15,11 @@
 def band_gather(rows):
     n = lax.axis_size("band")
     sent = jnp.broadcast_to(rows[None], (n,) + rows.shape)
-    got = lax.all_to_all(sent, "band", 0, 0, tiled=True)
-    return got.reshape((n * rows.shape[0],) + rows.shape[1:])
-
-
-def band_reduce(part):
-    n = lax.axis_size("band")
-    split = part.reshape((n, part.shape[0] // n) + part.shape[1:])
-    got = lax.all_to_all(split, "band", 0, 0, tiled=True)
-    return jnp.sum(got.astype(jnp.float32), axis=0)
+    return lax.all_to_all(sent, "band", 0, 0, tiled=True)
 
 
 def band_sum(part):
-    got = lax.all_to_all(jnp.swapaxes(part, 1, 2), "band", 0, 0, tiled=True)
+    got = lax.all_to_all(part, "band", 0, 0, tiled=True)
     return jnp.sum(got.astype(jnp.float32), axis=0)
 
 
@@ -47,24 +39,25 @@
 ):
     own_count = clear_count[0]
     kept = jnp.take(pixels, clear_index, axis=0)
-    kept_rows = jnp.swapaxes(kept, 0, 1)
-    spec_here, slots_here, width = kept_rows.shape
-    attn_in = band_gather(normed(kept_rows, attn_gain))
-    spec = attn_in.shape[0]
-    flat = attn_in.reshape(spec * slots_here, width)
+    slots_here, spec_here, width = kept.shape
+    n_band = lax.axis_size("band")
+    spec = n_band * spec_here
+    attn_in = band_gather(normed(kept, attn_gain))
+    flat = attn_in.reshape(-1, width)
     heads_here = w_query.shape[1] // HD
 
     def project(weight):
         out = jnp.dot(flat, weight, preferred_element_type=jnp.float32).astype(jnp.bfloat16)
-        return out.reshape(spec, slots_here, heads_here * HD)
+        return out.reshape(n_band, slots_here, spec_here, heads_here * HD)
 
     live_here = jnp.arange(slots_here, dtype=jnp.int32) < own_count
     qkv = jnp.concatenate([project(w_query), project(w_key), project(w_value)], axis=-1)
+    qkv = jnp.swapaxes(qkv, 1, 2)
     width_qkv = qkv.shape[-1]
-    flag_row = jnp.zeros((spec, 1, width_qkv), jnp.bfloat16)
     at = heads_here * HD
-    flag_row = flag_row.at[:, 0, at : at + slots_here].set(live_here.astype(jnp.bfloat16)[None, :])
-    payload = jnp.concatenate([qkv, flag_row], axis=1)
+    flags = jnp.zeros((width_qkv,), jnp.bfloat16).at[at : at + slots_here].set(live_here.astype(jnp.bfloat16))
+    flag_row = jnp.broadcast_to(flags, (n_band, spec_here, 1, width_qkv))
+    payload = jnp.concatenate([qkv, flag_row], axis=2)
     n_z = lax.axis_size("z")
     spec_mine = spec // n_z
     mine = lax.all_to_all(payload.reshape(n_z, spec_mine, -1), "z", 0, 0, tiled=True)
@@ -91,16 +84,13 @@
     context = context.reshape(spec_mine, q_slots, heads_here * HD)
     context = jnp.swapaxes(context.reshape(spec_mine, n_z, -1), 0, 1)
     context_rows = lax.all_to_all(context, "z", 0, 0, tiled=True)
-    context_rows = context_rows.reshape(spec, slots_here, heads_here * HD)
-    n_band = lax.axis_size("band")
     context_rows = context_rows.reshape(n_band, spec_here, slots_here, heads_here * HD)
-    context_rows = jnp.swapaxes(context_rows, 1, 2).reshape(spec * slots_here, heads_here * HD)
+    context_rows = jnp.swapaxes(context_rows, 1, 2).reshape(-1, heads_here * HD)
     out = jnp.dot(context_rows, w_out, preferred_element_type=jnp.float32).astype(jnp.bfloat16)
     attn_out = band_sum(out.reshape(n_band, slots_here, spec_here, width))
-    state = (kept_rows.astype(jnp.float32) + attn_out).astype(jnp.bfloat16)
+    state = (kept.astype(jnp.float32) + attn_out).astype(jnp.bfloat16)
     mlp_in = band_gather(normed(state, mlp_gain))
-    piece = jnp.swapaxes(mlp_in.reshape(n_band, spec_here, slots_here, width), 1, 2)
-    piece = piece.reshape(spec * slots_here, width)
+    piece = mlp_in.reshape(-1, width)
     gate = jnp.dot(piece, w_gate, preferred_element_type=jnp.float32)
     upper = jnp.dot(piece, w_up, preferred_element_type=jnp.float32)
     hidden = (jax.nn.silu(gate) * upper).astype(jnp.bfloat16)
@@ -111,7 +101,7 @@
         jnp.arange(pixels.shape[0], dtype=jnp.int32)[:, None] == clear_index[None, :]
     ) & live_here[None, :]
     placed = jnp.einsum(
-        "pc,scd->psd", chosen.astype(jnp.bfloat16), encoded, preferred_element_type=jnp.float32
+        "pc,csd->psd", chosen.astype(jnp.bfloat16), encoded, preferred_element_type=jnp.float32
     ).astype(jnp.bfloat16)
     taken = jnp.any(chosen, axis=1)
     return jnp.where(taken[:, None, None], placed, pixels)

time: 130 us -> 131 us (level)
  waiting for transfers between devices: 12.2 us -> 19.7 us
  local copies, waits for them, and re-layouts: 15.6 us -> 9.69 us
    all_to_all x2, waiting for transfers between devices: 11 us -> 18.5 us  [the longest x1 9.43 us: band_sum(): got = lax.all_to_all(part, 'band', 0, 0, tiled=True)]
    scatter x1 -> x0, local copies, waits for them, and re-layouts: 5.51 us -> none  [shards(): flag_row.at[:, 0, at:at + slots_here]]
    another operation x3 -> x0, other arithmetic: 1.36 us -> none
  transfers between devices with their start and end apart: 3 -> 3, of which waited for: 3 -> 3; matrix products, arithmetic and copies ran while one was open for 6% -> 0% of each run, Pallas kernels for 0% -> 0%
where the time goes in v10:
time: 131 us; the launch traced here: 130 us
  blocking collectives  74.9 us (57%)
  waiting for transfers between devices  19.7 us (15%)
  starting transfers between devices  16.2 us (12%)
  local copies, waits for them, and re-layouts  9.69 us (7%)
  other arithmetic  4.79 us (4%)
  matrix products  3.68 us (3%)
    all_to_all x1, blocking collectives, shards(): lax.all_to_all(payload.reshape(n_z, spec_mine, -1), 'z', 0, 0, tiled=True)  29 us
    all_to_all x1, blocking collectives, band_sum(): got = lax.all_to_all(part, 'band', 0, 0, tiled=True)  15.9 us
    all_to_all x1, blocking collectives, shards(): context_rows = lax.all_to_all(context, 'z', 0, 0, tiled=True)  15.8 us
    all_to_all x1, blocking collectives, band_gather(): return lax.all_to_all(sent, 'band', 0, 0, tiled=True)  14.2 us
    all_to_all x1, waiting for transfers between devices, band_sum(): got = lax.all_to_all(part, 'band', 0, 0, tiled=True)  9.43 us
    all_to_all x1, starting transfers between devices, band_gather(): return lax.all_to_all(sent, 'band', 0, 0, tiled=True)  9.26 us
    all_to_all x1, waiting for transfers between devices, band_gather(): return lax.all_to_all(sent, 'band', 0, 0, tiled=True)  9.09 us
    all_to_all x1, starting transfers between devices, band_sum(): got = lax.all_to_all(part, 'band', 0, 0, tiled=True)  4.97 us
  transfers between devices with their start and end apart: 3, of which 3 were waited for; matrix products, arithmetic and copies ran while one was open for 0% of the time, Pallas kernels for 0%

profile of v10, /device:TPU:2, one launch (start us, length us, event | category | flops | bytes accessed | tf_op | source)
XLA Modules:
  0.0 129.9 jit_solution(6179310509306475937)
XLA Ops:
  0.0 0.7 compare_select_fusion
  0.7 0.7 compare_and_fusion
  1.4 1.5 %gather_fusion = bf16[10,2,1024]{2,1,0:T(2,128)(2,1)S(1)} fusion(bf16[16,2,1024]{2,1,0:T(2,128)(2,1)} %param.14, s32[1024]{0:T(1024)S(1)} %pad_clamp_fusion), kind=kCustom, calls=%fused_computation | custom fusion | bytes 81960 | tf_op jit(solution)/shard_map/jit(_take)/gather | solution.py:41
  3.1 0.8 fusion.21
  3.9 1.2 broadcast_in_dim.67
  5.1 9.3 %all-to-all-start = ((bf16[16,10,2,1024]{3,2,1,0:T(2,128)(2,1)}), bf16[16,10,2,1024]{3,2,1,0:T(2,128)(2,1)S(1)}, u32[]{:S(2)}, u32[]{:S(2)}) async-start(bf16[16,10,2,1024]{3,2,1,0:T(2,128)(2,1)} %broadcast_in_dim.67), calls=%async_computation | async-start | bytes 1310720 | tf_op jit(solution)/shard_map/all_to_all | solution.py:18
  15.1 9.1 %all-to-all-done = bf16[16,10,2,1024]{3,2,1,0:T(2,128)(2,1)S(1)} async-done(((bf16[16,10,2,1024]{3,2,1,0:T(2,128)(2,1)}), bf16[16,10,2,1024]{3,2,1,0:T(2,128)(2,1)S(1)}, u32[]{:S(2)}, u32[]{:S(2)}) %all-to-all-start) | async-done | bytes 655392 | tf_op jit(solution)/shard_map/all_to_all | solution.py:18
  24.9 0.4 copy-done.3
  27.3 29.0 %all_to_all.30 = bf16[16,2,2112]{2,1,0:T(2,128)(2,1)S(1)} all-to-all(bf16[16,2,2112]{2,1,0:T(2,128)(2,1)S(1)} %reshape.167), channel_id=1, replica_groups=mesh['band'=16,'z'=16,'c'=2] {'z'}, dimensions={0} | all-to-all | bytes 270336 | tf_op jit(solution)/shard_map/all_to_all | solution.py:63
  56.7 1.9 %collective-permute-start = (bf16[2,16,11,128]{3,2,1,0:T(8,128)(2,1)S(1)}, bf16[2,16,11,128]{3,2,1,0:T(8,128)(2,1)S(1)}, u32[]{:S(2)}, u32[]{:S(2)}) collective-permute-start(bf16[2,16,11,128]{3,2,1,0:T(8,128)(2,1)S(1)} %slice.37), channel_id=1, source_target_pairs={{0,1},{1,0},{2,3},{3,2},{4,5},{5,4},{6,7},{7,6},{8,9},{9,8},{10,11... | collective-permute-start | bytes 270344 | tf_op jit(solution)/shard_map/ppermute | solution.py:67
  58.7 1.2 collective-permute-done
  60.9 0.4 fusion.46
  61.9 15.8 %all_to_all.31 = bf16[16,2,640]{2,1,0:T(2,128)(2,1)S(1)} all-to-all(bf16[16,2,640]{2,1,0:T(2,128)(2,1)S(1)} %copy.42), channel_id=1, replica_groups=mesh['band'=16,'z'=16,'c'=2] {'z'}, dimensions={0} | all-to-all | bytes 81920 | tf_op jit(solution)/shard_map/all_to_all | solution.py:86
  78.6 15.9 %all_to_all.32 = bf16[16,10,2,1024]{3,2,1,0:T(2,128)(2,1)S(1)} all-to-all(bf16[16,10,2,1024]{3,2,1,0:T(2,128)(2,1)S(1)} %reshape.154), channel_id=1, replica_groups=mesh['band'=16,'z'=16,'c'=2] {'band'}, dimensions={0} | all-to-all | bytes 1310720 | tf_op jit(solution)/shard_map/all_to_all | solution.py:22
  94.5 0.6 convert_reduce_fusion.1
  95.7 14.2 %all_to_all.33 = bf16[16,10,2,1024]{3,2,1,0:T(2,128)(2,1)S(1)} all-to-all(bf16[16,10,2,1024]{3,2,1,0:T(2,128)(2,1)S(1)} %broadcast_in_dim.72), channel_id=1, replica_groups=mesh['band'=16,'z'=16,'c'=2] {'band'}, dimensions={0} | all-to-all | bytes 1310720 | tf_op jit(solution)/shard_map/all_to_all | solution.py:18
  110.1 0.8 copy-done.1
  111.3 0.7 copy-done.8
  112.0 0.9 convolution_convert_fusion.1
  112.8 1.1 reshape.156
  113.9 5.0 %all-to-all-start.5 = ((bf16[16,10,2,1024]{3,2,1,0:T(2,128)(2,1)}), bf16[16,10,2,1024]{3,2,1,0:T(2,128)(2,1)S(1)}, u32[]{:S(2)}, u32[]{:S(2)}) async-start(bf16[16,10,2,1024]{3,2,1,0:T(2,128)(2,1)} %reshape.156), calls=%async_computation.5 | async-start | bytes 1310720 | tf_op jit(solution)/shard_map/all_to_all | solution.py:22
  119.0 9.4 %all-to-all-done.5 = bf16[16,10,2,1024]{3,2,1,0:T(2,128)(2,1)S(1)} async-done(((bf16[16,10,2,1024]{3,2,1,0:T(2,128)(2,1)}), bf16[16,10,2,1024]{3,2,1,0:T(2,128)(2,1)S(1)}, u32[]{:S(2)}, u32[]{:S(2)}) %all-to-all-start.5) | async-done | bytes 655392 | tf_op jit(solution)/shard_map/all_to_all | solution.py:22
  128.5 0.6 convert_reduce_fusion
  129.2 0.7 copy.47
  (63 shorter events, 7.3 us)
Async XLA Ops:
  0.0 111.3 %copy-start = (bf16[256,1024]{1,0:T(8,128)(2,1)S(1)}, bf16[256,1024]{1,0:T(8,128)(2,1)}, u32[]{:S(2)}) copy-start(bf16[256,1024]{1,0:T(8,128)(2,1)} %param.25) | copy-start | bytes 1572868
  5.1 19.1 %all-to-all-start = ((bf16[16,10,2,1024]{3,2,1,0:T(2,128)(2,1)}), bf16[16,10,2,1024]{3,2,1,0:T(2,128)(2,1)S(1)}, u32[]{:S(2)}, u32[]{:S(2)}) async-start(bf16[16,10,2,1024]{3,2,1,0:T(2,128)(2,1)} %broadcast_in_dim.67), calls=%async_computation | async-start | bytes 1310720 | tf_op jit(solution)/shard_map/all_to_all | solution.py:18
  15.1 9.4 %copy-start.2 = (bf16[1024,64]{0,1:T(8,128)(2,1)S(1)}, bf16[1024,64]{0,1:T(8,128)(2,1)}, u32[]{:S(2)}) copy-start(bf16[1024,64]{0,1:T(8,128)(2,1)} %param.18) | copy-start | bytes 393220
  24.4 0.9 copy-start.3
  24.8 1.0 copy-start.4
  56.7 3.2 %collective-permute-start = (bf16[2,16,11,128]{3,2,1,0:T(8,128)(2,1)S(1)}, bf16[2,16,11,128]{3,2,1,0:T(8,128)(2,1)S(1)}, u32[]{:S(2)}, u32[]{:S(2)}) collective-permute-start(bf16[2,16,11,128]{3,2,1,0:T(8,128)(2,1)S(1)} %slice.37), channel_id=1, source_target_pairs={{0,1},{1,0},{2,3},{3,2},{4,5},{5,4},{6,7},{7,6},{8,9},{9,8},{10,11... | collective-permute-start | bytes 270344 | tf_op jit(solution)/shard_map/ppermute | solution.py:67
  61.7 16.4 %copy-start.5 = (bf16[64,1024]{1,0:T(8,128)(2,1)S(1)}, bf16[64,1024]{1,0:T(8,128)(2,1)}, u32[]{:S(2)}) copy-start(bf16[64,1024]{1,0:T(8,128)(2,1)} %param.21) | copy-start | bytes 393220
  94.5 0.7 copy-start.7
  109.9 1.0 copy-start.1
  110.9 1.0 copy-start.8
  113.9 5.0 %copy-start.9 = (s32[10]{0:T(128)S(1)}, s32[10]{0:T(128)}, u32[]{:S(2)}) copy-start(s32[10]{0:T(128)} %param.16) | copy-start | bytes 124
  113.9 14.5 %all-to-all-start.5 = ((bf16[16,10,2,1024]{3,2,1,0:T(2,128)(2,1)}), bf16[16,10,2,1024]{3,2,1,0:T(2,128)(2,1)S(1)}, u32[]{:S(2)}, u32[]{:S(2)}) async-start(bf16[16,10,2,1024]{3,2,1,0:T(2,128)(2,1)} %reshape.156), calls=%async_computation.5 | async-start | bytes 1310720 | tf_op jit(solution)/shard_map/all_to_all | solution.py:22
  118.9 10.2 %copy-start.6 = (bf16[16,2,1024]{2,1,0:T(2,128)(2,1)S(1)}, bf16[16,2,1024]{2,1,0:T(2,128)(2,1)}, u32[]{:S(2)}) copy-start(bf16[16,2,1024]{2,1,0:T(2,128)(2,1)} %param.14) | copy-start | bytes 196612

commit v11 on v10

--- a/solution.py
+++ b/solution.py
@@ -38,11 +38,11 @@
     w_down,
 ):
     own_count = clear_count[0]
-    kept = jnp.take(pixels, clear_index, axis=0)
+    kept = jnp.take(pixels, clear_index, axis=0, mode="clip")
     slots_here, spec_here, width = kept.shape
     n_band = lax.axis_size("band")
     spec = n_band * spec_here
-    attn_in = band_gather(normed(kept, attn_gain))
+    attn_in = band_gather(jnp.take(normed(pixels, attn_gain), clear_index, axis=0, mode="clip"))
     flat = attn_in.reshape(-1, width)
     heads_here = w_query.shape[1] // HD
 

time: 131 us -> 131 us (level)
  the two profiles are of different devices: /device:TPU:2 before, /device:TPU:32 now
where the time goes in v11:
time: 131 us
  blocking collectives  58.2 us (44%)
  waiting for transfers between devices  35.4 us (27%)
  starting transfers between devices  17 us (13%)
  local copies, waits for them, and re-layouts  10.3 us (8%)
  other arithmetic  5.09 us (4%)
  matrix products  3.68 us (3%)
    all_to_all x1, blocking collectives, shards(): lax.all_to_all(payload.reshape(n_z, spec_mine, -1), 'z', 0, 0, tiled=True)  27.7 us
    all_to_all x2, waiting for transfers between devices, band_sum(): got = lax.all_to_all(part, 'band', 0, 0, tiled=True)  22 us
    all_to_all x1, blocking collectives, shards(): context_rows = lax.all_to_all(context, 'z', 0, 0, tiled=True)  16.1 us
    all_to_all x1, blocking collectives, band_gather(): return lax.all_to_all(sent, 'band', 0, 0, tiled=True)  14.3 us
    all_to_all x1, waiting for transfers between devices, band_gather(): return lax.all_to_all(sent, 'band', 0, 0, tiled=True)  12.2 us
    all_to_all x2, starting transfers between devices, band_sum(): got = lax.all_to_all(part, 'band', 0, 0, tiled=True)  8.02 us
    all_to_all x1, starting transfers between devices, band_gather(): return lax.all_to_all(sent, 'band', 0, 0, tiled=True)  7.03 us
  transfers between devices with their start and end apart: 4, of which 4 were waited for; matrix products, arithmetic and copies ran while one was open for 1% of the time, Pallas kernels for 0%

profile of v11, /device:TPU:32, one launch (start us, length us, event | category | flops | bytes accessed | tf_op | source)
XLA Modules:
  0.0 130.6 jit_solution(1803416087037208175)
XLA Ops:
  0.0 0.7 pad_clamp_fusion
  0.7 1.0 fusion.19
  1.7 1.0 fusion.21
  2.7 0.6 gather_fusion.1
  3.3 1.2 broadcast_in_dim.58
  4.5 7.0 %all-to-all-start = ((bf16[16,10,2,1024]{3,2,1,0:T(2,128)(2,1)}), bf16[16,10,2,1024]{3,2,1,0:T(2,128)(2,1)S(1)}, u32[]{:S(2)}, u32[]{:S(2)}) async-start(bf16[16,10,2,1024]{3,2,1,0:T(2,128)(2,1)} %broadcast_in_dim.58), calls=%async_computation | async-start | bytes 1310720 | tf_op jit(solution)/shard_map/all_to_all | solution.py:18
  12.3 12.2 %all-to-all-done = bf16[16,10,2,1024]{3,2,1,0:T(2,128)(2,1)S(1)} async-done(((bf16[16,10,2,1024]{3,2,1,0:T(2,128)(2,1)}), bf16[16,10,2,1024]{3,2,1,0:T(2,128)(2,1)S(1)}, u32[]{:S(2)}, u32[]{:S(2)}) %all-to-all-start) | async-done | bytes 655392 | tf_op jit(solution)/shard_map/all_to_all | solution.py:18
  27.6 27.7 %all_to_all.30 = bf16[16,2,2112]{2,1,0:T(2,128)(2,1)S(1)} all-to-all(bf16[16,2,2112]{2,1,0:T(2,128)(2,1)S(1)} %reshape.166), channel_id=1, replica_groups=mesh['band'=16,'z'=16,'c'=2] {'z'}, dimensions={0} | all-to-all | bytes 270336 | tf_op jit(solution)/shard_map/all_to_all | solution.py:63
  55.7 1.9 %collective-permute-start = (bf16[2,16,11,128]{3,2,1,0:T(8,128)(2,1)S(1)}, bf16[2,16,11,128]{3,2,1,0:T(8,128)(2,1)S(1)}, u32[]{:S(2)}, u32[]{:S(2)}) collective-permute-start(bf16[2,16,11,128]{3,2,1,0:T(8,128)(2,1)S(1)} %slice.39), channel_id=1, source_target_pairs={{0,1},{1,0},{2,3},{3,2},{4,5},{5,4},{6,7},{7,6},{8,9},{9,8},{10,11... | collective-permute-start | bytes 270344 | tf_op jit(solution)/shard_map/ppermute | solution.py:67
  57.8 1.2 collective-permute-done
  61.0 16.1 %all_to_all.31 = bf16[16,2,640]{2,1,0:T(2,128)(2,1)S(1)} all-to-all(bf16[16,2,640]{2,1,0:T(2,128)(2,1)S(1)} %copy.81), channel_id=1, replica_groups=mesh['band'=16,'z'=16,'c'=2] {'z'}, dimensions={0} | all-to-all | bytes 81920 | tf_op jit(solution)/shard_map/all_to_all | solution.py:86
  77.7 1.1 reshape.144
  78.8 4.3 %all-to-all-start.3 = ((bf16[16,10,2,1024]{3,2,1,0:T(2,128)(2,1)}), bf16[16,10,2,1024]{3,2,1,0:T(2,128)(2,1)S(1)}, u32[]{:S(2)}, u32[]{:S(2)}) async-start(bf16[16,10,2,1024]{3,2,1,0:T(2,128)(2,1)} %reshape.144), calls=%async_computation.3 | async-start | bytes 1310720 | tf_op jit(solution)/shard_map/all_to_all | solution.py:22
  83.1 0.6 gather_fusion
  83.7 11.3 %all-to-all-done.3 = bf16[16,10,2,1024]{3,2,1,0:T(2,128)(2,1)S(1)} async-done(((bf16[16,10,2,1024]{3,2,1,0:T(2,128)(2,1)}), bf16[16,10,2,1024]{3,2,1,0:T(2,128)(2,1)S(1)}, u32[]{:S(2)}, u32[]{:S(2)}) %all-to-all-start.3) | async-done | bytes 655392 | tf_op jit(solution)/shard_map/all_to_all | solution.py:22
  96.3 14.3 %all_to_all.32 = bf16[16,10,2,1024]{3,2,1,0:T(2,128)(2,1)S(1)} all-to-all(bf16[16,10,2,1024]{3,2,1,0:T(2,128)(2,1)S(1)} %broadcast_in_dim.63), channel_id=1, replica_groups=mesh['band'=16,'z'=16,'c'=2] {'band'}, dimensions={0} | all-to-all | bytes 1310720 | tf_op jit(solution)/shard_map/all_to_all | solution.py:18
  110.9 0.8 copy-done.1
  112.0 0.7 copy-done.9
  112.7 0.9 convolution_convert_fusion.1
  113.6 1.1 reshape.146
  114.6 3.7 %all-to-all-start.5 = ((bf16[16,10,2,1024]{3,2,1,0:T(2,128)(2,1)}), bf16[16,10,2,1024]{3,2,1,0:T(2,128)(2,1)S(1)}, u32[]{:S(2)}, u32[]{:S(2)}) async-start(bf16[16,10,2,1024]{3,2,1,0:T(2,128)(2,1)} %reshape.146), calls=%async_computation.5 | async-start | bytes 1310720 | tf_op jit(solution)/shard_map/all_to_all | solution.py:22
  118.5 10.7 %all-to-all-done.5 = bf16[16,10,2,1024]{3,2,1,0:T(2,128)(2,1)S(1)} async-done(((bf16[16,10,2,1024]{3,2,1,0:T(2,128)(2,1)}), bf16[16,10,2,1024]{3,2,1,0:T(2,128)(2,1)S(1)}, u32[]{:S(2)}, u32[]{:S(2)}) %all-to-all-start.5) | async-done | bytes 655392 | tf_op jit(solution)/shard_map/all_to_all | solution.py:22
  129.2 0.6 convert_reduce_fusion
  129.9 0.7 copy.86
  (63 shorter events, 8.2 us)
Async XLA Ops:
  0.0 112.0 %copy-start = (bf16[256,1024]{1,0:T(8,128)(2,1)S(1)}, bf16[256,1024]{1,0:T(8,128)(2,1)}, u32[]{:S(2)}) copy-start(bf16[256,1024]{1,0:T(8,128)(2,1)} %param.25) | copy-start | bytes 1572868
  4.5 20.0 %all-to-all-start = ((bf16[16,10,2,1024]{3,2,1,0:T(2,128)(2,1)}), bf16[16,10,2,1024]{3,2,1,0:T(2,128)(2,1)S(1)}, u32[]{:S(2)}, u32[]{:S(2)}) async-start(bf16[16,10,2,1024]{3,2,1,0:T(2,128)(2,1)} %broadcast_in_dim.58), calls=%async_computation | async-start | bytes 1310720 | tf_op jit(solution)/shard_map/all_to_all | solution.py:18
  12.3 12.5 %copy-start.3 = (bf16[1024,64]{0,1:T(8,128)(2,1)S(1)}, bf16[1024,64]{0,1:T(8,128)(2,1)}, u32[]{:S(2)}) copy-start(bf16[1024,64]{0,1:T(8,128)(2,1)} %param.18) | copy-start | bytes 393220
  24.8 0.9 copy-start.4
  25.1 1.0 copy-start.5
  55.7 3.2 %collective-permute-start = (bf16[2,16,11,128]{3,2,1,0:T(8,128)(2,1)S(1)}, bf16[2,16,11,128]{3,2,1,0:T(8,128)(2,1)S(1)}, u32[]{:S(2)}, u32[]{:S(2)}) collective-permute-start(bf16[2,16,11,128]{3,2,1,0:T(8,128)(2,1)S(1)} %slice.39), channel_id=1, source_target_pairs={{0,1},{1,0},{2,3},{3,2},{4,5},{5,4},{6,7},{7,6},{8,9},{9,8},{10,11... | collective-permute-start | bytes 270344 | tf_op jit(solution)/shard_map/ppermute | solution.py:67
  60.7 16.6 %copy-start.6 = (bf16[64,1024]{1,0:T(8,128)(2,1)S(1)}, bf16[64,1024]{1,0:T(8,128)(2,1)}, u32[]{:S(2)}) copy-start(bf16[64,1024]{1,0:T(8,128)(2,1)} %param.21) | copy-start | bytes 393220
  78.8 4.3 %copy-start.2 = (bf16[16,2,1024]{2,1,0:T(2,128)(2,1)S(1)}, bf16[16,2,1024]{2,1,0:T(2,128)(2,1)}, u32[]{:S(2)}) copy-start(bf16[16,2,1024]{2,1,0:T(2,128)(2,1)} %param.14) | copy-start | bytes 196612
  78.8 16.3 %all-to-all-start.3 = ((bf16[16,10,2,1024]{3,2,1,0:T(2,128)(2,1)}), bf16[16,10,2,1024]{3,2,1,0:T(2,128)(2,1)S(1)}, u32[]{:S(2)}, u32[]{:S(2)}) async-start(bf16[16,10,2,1024]{3,2,1,0:T(2,128)(2,1)} %reshape.144), calls=%async_computation.3 | async-start | bytes 1310720 | tf_op jit(solution)/shard_map/all_to_all | solution.py:22
  83.1 12.7 %copy-start.7 = (f32[1024]{0:T(1024)S(1)}, f32[1024]{0:T(1024)}, u32[]{:S(2)}) copy-start(f32[1024]{0:T(1024)} %param.22) | copy-start | bytes 12292
  110.6 1.0 copy-start.1
  111.6 1.0 copy-start.9
  114.6 3.7 %copy-start.8 = (s32[10]{0:T(128)S(1)}, s32[10]{0:T(128)}, u32[]{:S(2)}) copy-start(s32[10]{0:T(128)} %param.16) | copy-start | bytes 124
  114.6 14.5 %all-to-all-start.5 = ((bf16[16,10,2,1024]{3,2,1,0:T(2,128)(2,1)}), bf16[16,10,2,1024]{3,2,1,0:T(2,128)(2,1)S(1)}, u32[]{:S(2)}, u32[]{:S(2)}) async-start(bf16[16,10,2,1024]{3,2,1,0:T(2,128)(2,1)} %reshape.146), calls=%async_computation.5 | async-start | bytes 1310720 | tf_op jit(solution)/shard_map/all_to_all | solution.py:22

commit v12 on v11

--- a/solution.py
+++ b/solution.py
@@ -46,24 +46,24 @@
     flat = attn_in.reshape(-1, width)
     heads_here = w_query.shape[1] // HD
 
-    def project(weight):
-        out = jnp.dot(flat, weight, preferred_element_type=jnp.float32).astype(jnp.bfloat16)
-        return out.reshape(n_band, slots_here, spec_here, heads_here * HD)
-
     live_here = jnp.arange(slots_here, dtype=jnp.int32) < own_count
-    qkv = jnp.concatenate([project(w_query), project(w_key), project(w_value)], axis=-1)
-    qkv = jnp.swapaxes(qkv, 1, 2)
+    w_qkv = jnp.concatenate([w_query, w_key, w_value], axis=1)
+    qkv = jnp.dot(flat, w_qkv, preferred_element_type=jnp.float32).astype(jnp.bfloat16)
+    qkv = jnp.swapaxes(qkv.reshape(n_band, slots_here, spec_here, -1), 1, 2)
     width_qkv = qkv.shape[-1]
-    at = heads_here * HD
-    flags = jnp.zeros((width_qkv,), jnp.bfloat16).at[at : at + slots_here].set(live_here.astype(jnp.bfloat16))
-    flag_row = jnp.broadcast_to(flags, (n_band, spec_here, 1, width_qkv))
-    payload = jnp.concatenate([qkv, flag_row], axis=2)
+    n_flag = 64
+    flags = jnp.pad(live_here.astype(jnp.bfloat16), (0, n_flag - slots_here))
+    flags = jnp.broadcast_to(flags, (n_band, spec_here, n_flag))
+    payload = jnp.concatenate([qkv.reshape(n_band, spec_here, -1), flags], axis=2)
     n_z = lax.axis_size("z")
     spec_mine = spec // n_z
     mine = lax.all_to_all(payload.reshape(n_z, spec_mine, -1), "z", 0, 0, tiled=True)
-    mine = mine.reshape(n_z, spec_mine, slots_here + 1, width_qkv)
+    live_mine = mine[:, 0, slots_here * width_qkv :]
+    mine = mine[..., : slots_here * width_qkv].reshape(n_z, spec_mine, slots_here, width_qkv)
     mine = jnp.swapaxes(mine, 0, 1)
-    kv_flag = mine[..., heads_here * HD :]
+    kv = mine[..., heads_here * HD :]
+    flag_rows = jnp.pad(live_mine, ((0, 0), (0, kv.shape[-1] - n_flag)))
+    kv_flag = jnp.concatenate([kv, jnp.broadcast_to(flag_rows[None, :, None], (spec_mine,) + flag_rows.shape[:1] + (1, kv.shape[-1]))], axis=2)
     other = lax.ppermute(kv_flag, "c", [(0, 1), (1, 0)])
     kv_flag = jnp.concatenate([kv_flag, other], axis=1)
     live = (kv_flag[0, :, slots_here, :slots_here] > 0.5).reshape(-1)
@@ -85,17 +85,16 @@
     context = jnp.swapaxes(context.reshape(spec_mine, n_z, -1), 0, 1)
     context_rows = lax.all_to_all(context, "z", 0, 0, tiled=True)
     context_rows = context_rows.reshape(n_band, spec_here, slots_here, heads_here * HD)
-    context_rows = jnp.swapaxes(context_rows, 1, 2).reshape(-1, heads_here * HD)
-    out = jnp.dot(context_rows, w_out, preferred_element_type=jnp.float32).astype(jnp.bfloat16)
-    attn_out = band_sum(out.reshape(n_band, slots_here, spec_here, width))
+    context_rows = jnp.swapaxes(context_rows, 1, 2)
+    out = jnp.einsum("bsjh,hd->bsjd", context_rows, w_out, preferred_element_type=jnp.float32)
+    attn_out = band_sum(out.astype(jnp.bfloat16))
     state = (kept.astype(jnp.float32) + attn_out).astype(jnp.bfloat16)
     mlp_in = band_gather(normed(state, mlp_gain))
-    piece = mlp_in.reshape(-1, width)
-    gate = jnp.dot(piece, w_gate, preferred_element_type=jnp.float32)
-    upper = jnp.dot(piece, w_up, preferred_element_type=jnp.float32)
+    gate = jnp.einsum("bsjd,df->bsjf", mlp_in, w_gate, preferred_element_type=jnp.float32)
+    upper = jnp.einsum("bsjd,df->bsjf", mlp_in, w_up, preferred_element_type=jnp.float32)
     hidden = (jax.nn.silu(gate) * upper).astype(jnp.bfloat16)
-    out = jnp.dot(hidden, w_down, preferred_element_type=jnp.float32).astype(jnp.bfloat16)
-    mlp_out = band_sum(out.reshape(n_band, slots_here, spec_here, width))
+    out = jnp.einsum("bsjf,fd->bsjd", hidden, w_down, preferred_element_type=jnp.float32)
+    mlp_out = band_sum(out.astype(jnp.bfloat16))
     encoded = (state.astype(jnp.float32) + mlp_out).astype(jnp.bfloat16)
     chosen = (
         jnp.arange(pixels.shape[0], dtype=jnp.int32)[:, None] == clear_index[None, :]

time: 131 us -> 129 us (0.985)
  the two profiles are of different devices: /device:TPU:32 before, /device:TPU:2 now
where the time goes in v12:
time: 129 us
  blocking collectives  58.8 us (46%)
  waiting for transfers between devices  29.6 us (23%)
  starting transfers between devices  21.8 us (17%)
  local copies, waits for them, and re-layouts  9.67 us (7%)
  other arithmetic  4.48 us (3%)
  matrix products  3.11 us (2%)
    all_to_all x1, blocking collectives, shards(): lax.all_to_all(payload.reshape(n_z, spec_mine, -1), 'z', 0, 0, tiled=True)  28.7 us
    all_to_all x2, waiting for transfers between devices, band_sum(): got = lax.all_to_all(part, 'band', 0, 0, tiled=True)  19.3 us
    all_to_all x1, blocking collectives, shards(): context_rows = lax.all_to_all(context, 'z', 0, 0, tiled=True)  15.8 us
    all_to_all x1, blocking collectives, band_gather(): return lax.all_to_all(sent, 'band', 0, 0, tiled=True)  14.3 us
    all_to_all x2, starting transfers between devices, band_sum(): got = lax.all_to_all(part, 'band', 0, 0, tiled=True)  10.6 us
    all_to_all x1, starting transfers between devices, band_gather(): return lax.all_to_all(sent, 'band', 0, 0, tiled=True)  9.26 us
    all_to_all x1, waiting for transfers between devices, band_gather(): return lax.all_to_all(sent, 'band', 0, 0, tiled=True)  9.11 us
  transfers between devices with their start and end apart: 4, of which 4 were waited for; matrix products, arithmetic and copies ran while one was open for 1% of the time, Pallas kernels for 0%

profile of v12, /device:TPU:2, one launch (start us, length us, event | category | flops | bytes accessed | tf_op | source)
XLA Modules:
  0.0 128.5 jit_solution(17801745749179981816)
XLA Ops:
  0.0 0.7 pad_clamp_fusion
  0.7 1.0 fusion.32
  1.7 1.0 fusion.34
  2.7 0.6 gather_fusion.1
  3.3 1.2 broadcast_in_dim.63
  4.5 9.3 %all-to-all-start = ((bf16[16,10,2,1024]{3,2,1,0:T(2,128)(2,1)}), bf16[16,10,2,1024]{3,2,1,0:T(2,128)(2,1)S(1)}, u32[]{:S(2)}, u32[]{:S(2)}) async-start(bf16[16,10,2,1024]{3,2,1,0:T(2,128)(2,1)} %broadcast_in_dim.63), calls=%async_computation | async-start | bytes 1310720 | tf_op jit(solution)/shard_map/all_to_all | solution.py:18
  14.5 9.1 %all-to-all-done = bf16[16,10,2,1024]{3,2,1,0:T(2,128)(2,1)S(1)} async-done(((bf16[16,10,2,1024]{3,2,1,0:T(2,128)(2,1)}), bf16[16,10,2,1024]{3,2,1,0:T(2,128)(2,1)S(1)}, u32[]{:S(2)}, u32[]{:S(2)}) %all-to-all-start) | async-done | bytes 655392 | tf_op jit(solution)/shard_map/all_to_all | solution.py:18
  25.0 28.7 %all_to_all.30 = bf16[16,2,1984]{2,1,0:T(2,128)(2,1)S(1)} all-to-all(bf16[16,2,1984]{2,1,0:T(2,128)(2,1)S(1)} %copy.114), channel_id=1, replica_groups=mesh['band'=16,'z'=16,'c'=2] {'z'}, dimensions={0} | all-to-all | bytes 253952 | tf_op jit(solution)/shard_map/all_to_all | solution.py:60
  54.4 1.9 %collective-permute-start = (bf16[2,16,11,128]{3,2,1,0:T(8,128)(2,1)S(1)}, bf16[2,16,11,128]{3,2,1,0:T(8,128)(2,1)S(1)}, u32[]{:S(2)}, u32[]{:S(2)}) collective-permute-start(bf16[2,16,11,128]{3,2,1,0:T(8,128)(2,1)S(1)} %pad_maximum_fusion.2), channel_id=1, source_target_pairs={{0,1},{1,0},{2,3},{3,2},{4,5},{5,4},{6,7},{7,6},{8,9},{9,8},{10,11... | collective-permute-start | bytes 270344 | tf_op jit(solution)/shard_map/ppermute | solution.py:67
  56.4 1.2 collective-permute-done
  59.7 15.8 %all_to_all.31 = bf16[16,2,640]{2,1,0:T(2,128)(2,1)S(1)} all-to-all(bf16[16,2,640]{2,1,0:T(2,128)(2,1)S(1)} %copy.123), channel_id=1, replica_groups=mesh['band'=16,'z'=16,'c'=2] {'z'}, dimensions={0} | all-to-all | bytes 81920 | tf_op jit(solution)/shard_map/all_to_all | solution.py:86
  75.9 1.5 %copy.126 = bf16[16,10,2,1024]{3,2,1,0:T(2,128)(2,1)} copy(bf16[16,10,2,1024]{3,0,2,1:T(8,128)(2,1)S(1)} %convolution_convert_fusion) | data formatting | bytes 1310720 | tf_op jit(solution)/shard_map/convert_element_type | solution.py:90
  77.4 5.7 %all-to-all-start.3 = ((bf16[16,10,2,1024]{3,2,1,0:T(2,128)(2,1)}), bf16[16,10,2,1024]{3,2,1,0:T(2,128)(2,1)S(1)}, u32[]{:S(2)}, u32[]{:S(2)}) async-start(bf16[16,10,2,1024]{3,2,1,0:T(2,128)(2,1)} %copy.126), calls=%async_computation.3 | async-start | bytes 1310720 | tf_op jit(solution)/shard_map/all_to_all | solution.py:22
  83.1 0.6 gather_fusion
  83.7 9.9 %all-to-all-done.3 = bf16[16,10,2,1024]{3,2,1,0:T(2,128)(2,1)S(1)} async-done(((bf16[16,10,2,1024]{3,2,1,0:T(2,128)(2,1)}), bf16[16,10,2,1024]{3,2,1,0:T(2,128)(2,1)S(1)}, u32[]{:S(2)}, u32[]{:S(2)}) %all-to-all-start.3) | async-done | bytes 655392 | tf_op jit(solution)/shard_map/all_to_all | solution.py:22
  93.7 0.6 convert_reduce_fusion.1
  94.8 14.3 %all_to_all.32 = bf16[16,10,2,1024]{3,2,1,0:T(2,128)(2,1)S(1)} all-to-all(bf16[16,10,2,1024]{3,2,1,0:T(2,128)(2,1)S(1)} %broadcast_in_dim.69), channel_id=1, replica_groups=mesh['band'=16,'z'=16,'c'=2] {'band'}, dimensions={0} | all-to-all | bytes 1310720 | tf_op jit(solution)/shard_map/all_to_all | solution.py:18
  109.5 0.7 copy-done.6
  110.2 0.9 convolution_convert_fusion.1
  111.1 1.5 %copy.129 = bf16[16,10,2,1024]{3,2,1,0:T(2,128)(2,1)} copy(bf16[16,10,2,1024]{3,0,2,1:T(8,128)(2,1)S(1)} %convolution_convert_fusion.1) | data formatting | bytes 1310720 | tf_op jit(solution)/shard_map/convert_element_type | solution.py:97
  112.6 5.0 %all-to-all-start.5 = ((bf16[16,10,2,1024]{3,2,1,0:T(2,128)(2,1)}), bf16[16,10,2,1024]{3,2,1,0:T(2,128)(2,1)S(1)}, u32[]{:S(2)}, u32[]{:S(2)}) async-start(bf16[16,10,2,1024]{3,2,1,0:T(2,128)(2,1)} %copy.129), calls=%async_computation.5 | async-start | bytes 1310720 | tf_op jit(solution)/shard_map/all_to_all | solution.py:22
  117.7 9.4 %all-to-all-done.5 = bf16[16,10,2,1024]{3,2,1,0:T(2,128)(2,1)S(1)} async-done(((bf16[16,10,2,1024]{3,2,1,0:T(2,128)(2,1)}), bf16[16,10,2,1024]{3,2,1,0:T(2,128)(2,1)S(1)}, u32[]{:S(2)}, u32[]{:S(2)}) %all-to-all-start.5) | async-done | bytes 655392 | tf_op jit(solution)/shard_map/all_to_all | solution.py:22
  127.1 0.6 convert_reduce_fusion
  127.8 0.7 copy.132
  (63 shorter events, 5.8 us)
Async XLA Ops:
  0.0 109.5 %copy-start = (bf16[256,1024]{1,0:T(8,128)(2,1)S(1)}, bf16[256,1024]{1,0:T(8,128)(2,1)}, u32[]{:S(2)}) copy-start(bf16[256,1024]{1,0:T(8,128)(2,1)} %param.23) | copy-start | bytes 1572868
  4.5 19.1 %all-to-all-start = ((bf16[16,10,2,1024]{3,2,1,0:T(2,128)(2,1)}), bf16[16,10,2,1024]{3,2,1,0:T(2,128)(2,1)S(1)}, u32[]{:S(2)}, u32[]{:S(2)}) async-start(bf16[16,10,2,1024]{3,2,1,0:T(2,128)(2,1)} %broadcast_in_dim.63), calls=%async_computation | async-start | bytes 1310720 | tf_op jit(solution)/shard_map/all_to_all | solution.py:18
  14.5 9.4 %copy-start.7 = (bf16[1024,64]{0,1:T(8,128)(2,1)S(1)}, bf16[1024,64]{0,1:T(8,128)(2,1)}, u32[]{:S(2)}) copy-start(bf16[1024,64]{0,1:T(8,128)(2,1)} %param.18) | copy-start | bytes 393220
  14.5 9.4 %copy-start.8 = (bf16[1024,64]{0,1:T(8,128)(2,1)S(1)}, bf16[1024,64]{0,1:T(8,128)(2,1)}, u32[]{:S(2)}) copy-start(bf16[1024,64]{0,1:T(8,128)(2,1)} %param.17) | copy-start | bytes 393220
  14.5 9.4 %copy-start.9 = (bf16[1024,64]{0,1:T(8,128)(2,1)S(1)}, bf16[1024,64]{0,1:T(8,128)(2,1)}, u32[]{:S(2)}) copy-start(bf16[1024,64]{0,1:T(8,128)(2,1)} %param.16) | copy-start | bytes 393220
  54.4 3.2 %collective-permute-start = (bf16[2,16,11,128]{3,2,1,0:T(8,128)(2,1)S(1)}, bf16[2,16,11,128]{3,2,1,0:T(8,128)(2,1)S(1)}, u32[]{:S(2)}, u32[]{:S(2)}) collective-permute-start(bf16[2,16,11,128]{3,2,1,0:T(8,128)(2,1)S(1)} %pad_maximum_fusion.2), channel_id=1, source_target_pairs={{0,1},{1,0},{2,3},{3,2},{4,5},{5,4},{6,7},{7,6},{8,9},{9,8},{10,11... | collective-permute-start | bytes 270344 | tf_op jit(solution)/shard_map/ppermute | solution.py:67
  59.0 16.5 %copy-start.2 = (bf16[64,1024]{1,0:T(8,128)(2,1)S(1)}, bf16[64,1024]{1,0:T(8,128)(2,1)}, u32[]{:S(2)}) copy-start(bf16[64,1024]{1,0:T(8,128)(2,1)} %param.19) | copy-start | bytes 393220
  77.4 5.7 %copy-start.1 = (bf16[16,2,1024]{2,1,0:T(2,128)(2,1)S(1)}, bf16[16,2,1024]{2,1,0:T(2,128)(2,1)}, u32[]{:S(2)}) copy-start(bf16[16,2,1024]{2,1,0:T(2,128)(2,1)} %param.12) | copy-start | bytes 196612
  77.4 16.2 %all-to-all-start.3 = ((bf16[16,10,2,1024]{3,2,1,0:T(2,128)(2,1)}), bf16[16,10,2,1024]{3,2,1,0:T(2,128)(2,1)S(1)}, u32[]{:S(2)}, u32[]{:S(2)}) async-start(bf16[16,10,2,1024]{3,2,1,0:T(2,128)(2,1)} %copy.126), calls=%async_computation.3 | async-start | bytes 1310720 | tf_op jit(solution)/shard_map/all_to_all | solution.py:22
  83.1 11.3 %copy-start.3 = (f32[1024]{0:T(1024)S(1)}, f32[1024]{0:T(1024)}, u32[]{:S(2)}) copy-start(f32[1024]{0:T(1024)} %param.20) | copy-start | bytes 12292
  94.8 14.3 %copy-start.5 = (bf16[1024,256]{1,0:T(8,128)(2,1)S(1)}, bf16[1024,256]{1,0:T(8,128)(2,1)}, u32[]{:S(2)}) copy-start(bf16[1024,256]{1,0:T(8,128)(2,1)} %param.21) | copy-start | bytes 1572868
  109.2 1.0 copy-start.6
  112.6 5.0 %copy-start.4 = (s32[10]{0:T(128)S(1)}, s32[10]{0:T(128)}, u32[]{:S(2)}) copy-start(s32[10]{0:T(128)} %param.14) | copy-start | bytes 124
  112.6 14.5 %all-to-all-start.5 = ((bf16[16,10,2,1024]{3,2,1,0:T(2,128)(2,1)}), bf16[16,10,2,1024]{3,2,1,0:T(2,128)(2,1)S(1)}, u32[]{:S(2)}, u32[]{:S(2)}) async-start(bf16[16,10,2,1024]{3,2,1,0:T(2,128)(2,1)} %copy.129), calls=%async_computation.5 | async-start | bytes 1310720 | tf_op jit(solution)/shard_map/all_to_all | solution.py:22

commit v13 on v12

--- a/solution.py
+++ b/solution.py
@@ -55,23 +55,15 @@
     flags = jnp.pad(live_here.astype(jnp.bfloat16), (0, n_flag - slots_here))
     flags = jnp.broadcast_to(flags, (n_band, spec_here, n_flag))
     payload = jnp.concatenate([qkv.reshape(n_band, spec_here, -1), flags], axis=2)
-    n_z = lax.axis_size("z")
-    spec_mine = spec // n_z
-    mine = lax.all_to_all(payload.reshape(n_z, spec_mine, -1), "z", 0, 0, tiled=True)
-    live_mine = mine[:, 0, slots_here * width_qkv :]
-    mine = mine[..., : slots_here * width_qkv].reshape(n_z, spec_mine, slots_here, width_qkv)
-    mine = jnp.swapaxes(mine, 0, 1)
-    kv = mine[..., heads_here * HD :]
-    flag_rows = jnp.pad(live_mine, ((0, 0), (0, kv.shape[-1] - n_flag)))
-    kv_flag = jnp.concatenate([kv, jnp.broadcast_to(flag_rows[None, :, None], (spec_mine,) + flag_rows.shape[:1] + (1, kv.shape[-1]))], axis=2)
-    other = lax.ppermute(kv_flag, "c", [(0, 1), (1, 0)])
-    kv_flag = jnp.concatenate([kv_flag, other], axis=1)
-    live = (kv_flag[0, :, slots_here, :slots_here] > 0.5).reshape(-1)
-    kv = kv_flag[:, :, :slots_here].reshape(spec_mine, -1, 2 * heads_here * HD)
-    q_slots = n_z * slots_here
-    q = mine[:, :, :slots_here, : heads_here * HD].reshape(spec_mine, q_slots, heads_here, HD)
-    k = kv[..., : heads_here * HD].reshape(spec_mine, -1, heads_here, HD)
-    v = kv[..., heads_here * HD :].reshape(spec_mine, -1, heads_here, HD)
+    pix = ("z", "c")
+    n_pix = lax.axis_size(pix)
+    mine = lax.all_to_all(payload.reshape(n_pix, spec // n_pix, -1), pix, 0, 0, tiled=True)
+    live = (mine[:, 0, slots_here * width_qkv : slots_here * width_qkv + slots_here] > 0.5).reshape(-1)
+    rows = mine[..., : slots_here * width_qkv].reshape(-1, n_pix * slots_here, width_qkv)
+    spec_mine = rows.shape[0]
+    q = rows[..., : heads_here * HD].reshape(spec_mine, -1, heads_here, HD)
+    k = rows[..., heads_here * HD : 2 * heads_here * HD].reshape(spec_mine, -1, heads_here, HD)
+    v = rows[..., 2 * heads_here * HD :].reshape(spec_mine, -1, heads_here, HD)
     scores = jnp.einsum("sqhd,skhd->shqk", q, k, preferred_element_type=jnp.float32) * HD ** (-0.5)
     masked = jnp.where(live[None, None, None, :], scores, -1e30)
     top = jnp.max(masked, axis=-1)
@@ -81,9 +73,8 @@
         "shqk,skhd->sqhd", expo.astype(jnp.bfloat16), v, preferred_element_type=jnp.float32
     )
     context = (mixed / jnp.transpose(totals, (0, 2, 1))[..., None]).astype(jnp.bfloat16)
-    context = context.reshape(spec_mine, q_slots, heads_here * HD)
-    context = jnp.swapaxes(context.reshape(spec_mine, n_z, -1), 0, 1)
-    context_rows = lax.all_to_all(context, "z", 0, 0, tiled=True)
+    context = jnp.swapaxes(context.reshape(spec_mine, n_pix, -1), 0, 1)
+    context_rows = lax.all_to_all(context, pix, 0, 0, tiled=True)
     context_rows = context_rows.reshape(n_band, spec_here, slots_here, heads_here * HD)
     context_rows = jnp.swapaxes(context_rows, 1, 2)
     out = jnp.einsum("bsjh,hd->bsjd", context_rows, w_out, preferred_element_type=jnp.float32)

time: 129 us -> 134 us (1.039)
  the two profiles are of different devices: /device:TPU:2 before, /device:TPU:64 now
where the time goes in v13:
time: 134 us; the launch traced here: 133 us
  blocking collectives  61.7 us (46%)
  waiting for transfers between devices  36.5 us (27%)
  starting transfers between devices  14.5 us (11%)
  local copies, waits for them, and re-layouts  10.3 us (8%)
  other arithmetic  6.23 us (5%)
  matrix products  2.67 us (2%)
    all_to_all x1, blocking collectives, shards(): lax.all_to_all(payload.reshape(n_pix, spec // n_pix, -1), pix, 0, 0, tile...  28.9 us
    all_to_all x2, waiting for transfers between devices, band_sum(): got = lax.all_to_all(part, 'band', 0, 0, tiled=True)  24.3 us
    all_to_all x1, blocking collectives, shards(): context_rows = lax.all_to_all(context, pix, 0, 0, tiled=True)  17.1 us
    all_to_all x1, blocking collectives, band_gather(): return lax.all_to_all(sent, 'band', 0, 0, tiled=True)  15.7 us
    all_to_all x1, waiting for transfers between devices, band_gather(): return lax.all_to_all(sent, 'band', 0, 0, tiled=True)  12.2 us
    all_to_all x2, starting transfers between devices, band_sum(): got = lax.all_to_all(part, 'band', 0, 0, tiled=True)  7.45 us
    all_to_all x1, starting transfers between devices, band_gather(): return lax.all_to_all(sent, 'band', 0, 0, tiled=True)  7.03 us
  transfers between devices with their start and end apart: 3, of which 3 were waited for; matrix products, arithmetic and copies ran while one was open for 1% of the time, Pallas kernels for 0%

profile of v13, /device:TPU:64, one launch (start us, length us, event | category | flops | bytes accessed | tf_op | source)
XLA Modules:
  0.0 132.9 jit_solution(1471004196893191641)
XLA Ops:
  0.0 0.7 pad_clamp_fusion
  0.7 1.0 fusion.31
  1.7 1.0 fusion.33
  2.7 0.6 gather_fusion.1
  3.3 1.2 broadcast_in_dim.57
  4.5 7.0 %all-to-all-start = ((bf16[16,10,2,1024]{3,2,1,0:T(2,128)(2,1)}), bf16[16,10,2,1024]{3,2,1,0:T(2,128)(2,1)S(1)}, u32[]{:S(2)}, u32[]{:S(2)}) async-start(bf16[16,10,2,1024]{3,2,1,0:T(2,128)(2,1)} %broadcast_in_dim.57), calls=%async_computation | async-start | bytes 1310720 | tf_op jit(solution)/shard_map/all_to_all | solution.py:18
  12.3 12.2 %all-to-all-done = bf16[16,10,2,1024]{3,2,1,0:T(2,128)(2,1)S(1)} async-done(((bf16[16,10,2,1024]{3,2,1,0:T(2,128)(2,1)}), bf16[16,10,2,1024]{3,2,1,0:T(2,128)(2,1)S(1)}, u32[]{:S(2)}, u32[]{:S(2)}) %all-to-all-start) | async-done | bytes 655392 | tf_op jit(solution)/shard_map/all_to_all | solution.py:18
  26.3 0.7 reduce.9
  27.1 28.9 %all_to_all.30 = bf16[32,2,992]{2,1,0:T(2,128)(2,1)S(1)} all-to-all(bf16[32,2,992]{2,1,0:T(2,128)(2,1)S(1)} %reshape.131), channel_id=1, replica_groups=mesh['band'=16,'z'=16,'c'=2] {'z','c'}, dimensions={0} | all-to-all | bytes 253952 | tf_op jit(solution)/shard_map/all_to_all | solution.py:60
  56.2 0.7 slice_reduce_fusion
  58.2 0.9 reduce.10
  59.1 17.1 %all_to_all.31 = bf16[32,2,320]{2,1,0:T(2,128)(2,1)S(1)} all-to-all(bf16[32,2,320]{2,1,0:T(2,128)(2,1)S(1)} %reshape.133), channel_id=1, replica_groups=mesh['band'=16,'z'=16,'c'=2] {'z','c'}, dimensions={0} | all-to-all | bytes 81920 | tf_op jit(solution)/shard_map/all_to_all | solution.py:77
  77.0 1.5 %copy.70 = bf16[16,10,2,1024]{3,2,1,0:T(2,128)(2,1)} copy(bf16[16,10,2,1024]{3,0,2,1:T(8,128)(2,1)S(1)} %convolution_convert_fusion) | data formatting | bytes 1310720 | tf_op jit(solution)/shard_map/convert_element_type | solution.py:81
  78.5 3.7 %all-to-all-start.3 = ((bf16[16,10,2,1024]{3,2,1,0:T(2,128)(2,1)}), bf16[16,10,2,1024]{3,2,1,0:T(2,128)(2,1)S(1)}, u32[]{:S(2)}, u32[]{:S(2)}) async-start(bf16[16,10,2,1024]{3,2,1,0:T(2,128)(2,1)} %copy.70), calls=%async_computation.3 | async-start | bytes 1310720 | tf_op jit(solution)/shard_map/all_to_all | solution.py:22
  82.3 0.6 gather_fusion
  82.9 12.8 %all-to-all-done.3 = bf16[16,10,2,1024]{3,2,1,0:T(2,128)(2,1)S(1)} async-done(((bf16[16,10,2,1024]{3,2,1,0:T(2,128)(2,1)}), bf16[16,10,2,1024]{3,2,1,0:T(2,128)(2,1)S(1)}, u32[]{:S(2)}, u32[]{:S(2)}) %all-to-all-start.3) | async-done | bytes 655392 | tf_op jit(solution)/shard_map/all_to_all | solution.py:22
  95.7 0.6 convert_reduce_fusion.1
  96.9 15.7 %all_to_all.32 = bf16[16,10,2,1024]{3,2,1,0:T(2,128)(2,1)S(1)} all-to-all(bf16[16,10,2,1024]{3,2,1,0:T(2,128)(2,1)S(1)} %broadcast_in_dim.62), channel_id=1, replica_groups=mesh['band'=16,'z'=16,'c'=2] {'band'}, dimensions={0} | all-to-all | bytes 1310720 | tf_op jit(solution)/shard_map/all_to_all | solution.py:18
  113.0 0.7 copy-done.6
  113.7 0.9 convolution_convert_fusion.1
  114.6 1.5 %copy.73 = bf16[16,10,2,1024]{3,2,1,0:T(2,128)(2,1)} copy(bf16[16,10,2,1024]{3,0,2,1:T(8,128)(2,1)S(1)} %convolution_convert_fusion.1) | data formatting | bytes 1310720 | tf_op jit(solution)/shard_map/convert_element_type | solution.py:88
  116.1 3.7 %all-to-all-start.5 = ((bf16[16,10,2,1024]{3,2,1,0:T(2,128)(2,1)}), bf16[16,10,2,1024]{3,2,1,0:T(2,128)(2,1)S(1)}, u32[]{:S(2)}, u32[]{:S(2)}) async-start(bf16[16,10,2,1024]{3,2,1,0:T(2,128)(2,1)} %copy.73), calls=%async_computation.5 | async-start | bytes 1310720 | tf_op jit(solution)/shard_map/all_to_all | solution.py:22
  119.9 11.5 %all-to-all-done.5 = bf16[16,10,2,1024]{3,2,1,0:T(2,128)(2,1)S(1)} async-done(((bf16[16,10,2,1024]{3,2,1,0:T(2,128)(2,1)}), bf16[16,10,2,1024]{3,2,1,0:T(2,128)(2,1)S(1)}, u32[]{:S(2)}, u32[]{:S(2)}) %all-to-all-start.5) | async-done | bytes 655392 | tf_op jit(solution)/shard_map/all_to_all | solution.py:22
  132.2 0.7 copy.76
  (55 shorter events, 6.1 us)
Async XLA Ops:
  0.0 113.0 %copy-start = (bf16[256,1024]{1,0:T(8,128)(2,1)S(1)}, bf16[256,1024]{1,0:T(8,128)(2,1)}, u32[]{:S(2)}) copy-start(bf16[256,1024]{1,0:T(8,128)(2,1)} %param.23) | copy-start | bytes 1572868
  4.5 20.0 %all-to-all-start = ((bf16[16,10,2,1024]{3,2,1,0:T(2,128)(2,1)}), bf16[16,10,2,1024]{3,2,1,0:T(2,128)(2,1)S(1)}, u32[]{:S(2)}, u32[]{:S(2)}) async-start(bf16[16,10,2,1024]{3,2,1,0:T(2,128)(2,1)} %broadcast_in_dim.57), calls=%async_computation | async-start | bytes 1310720 | tf_op jit(solution)/shard_map/all_to_all | solution.py:18
  12.2 12.5 %copy-start.7 = (bf16[1024,64]{0,1:T(8,128)(2,1)S(1)}, bf16[1024,64]{0,1:T(8,128)(2,1)}, u32[]{:S(2)}) copy-start(bf16[1024,64]{0,1:T(8,128)(2,1)} %param.18) | copy-start | bytes 393220
  12.3 12.5 %copy-start.8 = (bf16[1024,64]{0,1:T(8,128)(2,1)S(1)}, bf16[1024,64]{0,1:T(8,128)(2,1)}, u32[]{:S(2)}) copy-start(bf16[1024,64]{0,1:T(8,128)(2,1)} %param.17) | copy-start | bytes 393220
  12.3 12.5 %copy-start.9 = (bf16[1024,64]{0,1:T(8,128)(2,1)S(1)}, bf16[1024,64]{0,1:T(8,128)(2,1)}, u32[]{:S(2)}) copy-start(bf16[1024,64]{0,1:T(8,128)(2,1)} %param.16) | copy-start | bytes 393220
  57.9 18.8 %copy-start.2 = (bf16[64,1024]{1,0:T(8,128)(2,1)S(1)}, bf16[64,1024]{1,0:T(8,128)(2,1)}, u32[]{:S(2)}) copy-start(bf16[64,1024]{1,0:T(8,128)(2,1)} %param.19) | copy-start | bytes 393220
  78.5 3.7 %copy-start.1 = (bf16[16,2,1024]{2,1,0:T(2,128)(2,1)S(1)}, bf16[16,2,1024]{2,1,0:T(2,128)(2,1)}, u32[]{:S(2)}) copy-start(bf16[16,2,1024]{2,1,0:T(2,128)(2,1)} %param.12) | copy-start | bytes 196612
  78.5 17.2 %all-to-all-start.3 = ((bf16[16,10,2,1024]{3,2,1,0:T(2,128)(2,1)}), bf16[16,10,2,1024]{3,2,1,0:T(2,128)(2,1)S(1)}, u32[]{:S(2)}, u32[]{:S(2)}) async-start(bf16[16,10,2,1024]{3,2,1,0:T(2,128)(2,1)} %copy.70), calls=%async_computation.3 | async-start | bytes 1310720 | tf_op jit(solution)/shard_map/all_to_all | solution.py:22
  82.3 14.2 %copy-start.3 = (f32[1024]{0:T(1024)S(1)}, f32[1024]{0:T(1024)}, u32[]{:S(2)}) copy-start(f32[1024]{0:T(1024)} %param.20) | copy-start | bytes 12292
  96.9 15.7 %copy-start.5 = (bf16[1024,256]{1,0:T(8,128)(2,1)S(1)}, bf16[1024,256]{1,0:T(8,128)(2,1)}, u32[]{:S(2)}) copy-start(bf16[1024,256]{1,0:T(8,128)(2,1)} %param.21) | copy-start | bytes 1572868
  112.7 1.0 copy-start.6
  116.1 3.7 %copy-start.4 = (s32[10]{0:T(128)S(1)}, s32[10]{0:T(128)}, u32[]{:S(2)}) copy-start(s32[10]{0:T(128)} %param.14) | copy-start | bytes 124
  116.1 15.3 %all-to-all-start.5 = ((bf16[16,10,2,1024]{3,2,1,0:T(2,128)(2,1)}), bf16[16,10,2,1024]{3,2,1,0:T(2,128)(2,1)S(1)}, u32[]{:S(2)}, u32[]{:S(2)}) async-start(bf16[16,10,2,1024]{3,2,1,0:T(2,128)(2,1)} %copy.73), calls=%async_computation.5 | async-start | bytes 1310720 | tf_op jit(solution)/shard_map/all_to_all | solution.py:22

commit v14 on v12

--- a/solution.py
+++ b/solution.py
@@ -48,7 +48,7 @@
 
     live_here = jnp.arange(slots_here, dtype=jnp.int32) < own_count
     w_qkv = jnp.concatenate([w_query, w_key, w_value], axis=1)
-    qkv = jnp.dot(flat, w_qkv, preferred_element_type=jnp.float32).astype(jnp.bfloat16)
+    qkv = jnp.dot(flat, w_qkv, preferred_element_type=jnp.bfloat16)
     qkv = jnp.swapaxes(qkv.reshape(n_band, slots_here, spec_here, -1), 1, 2)
     width_qkv = qkv.shape[-1]
     n_flag = 64
@@ -86,15 +86,15 @@
     context_rows = lax.all_to_all(context, "z", 0, 0, tiled=True)
     context_rows = context_rows.reshape(n_band, spec_here, slots_here, heads_here * HD)
     context_rows = jnp.swapaxes(context_rows, 1, 2)
-    out = jnp.einsum("bsjh,hd->bsjd", context_rows, w_out, preferred_element_type=jnp.float32)
-    attn_out = band_sum(out.astype(jnp.bfloat16))
+    out = jnp.einsum("bsjh,hd->bsjd", context_rows, w_out, preferred_element_type=jnp.bfloat16)
+    attn_out = band_sum(out)
     state = (kept.astype(jnp.float32) + attn_out).astype(jnp.bfloat16)
     mlp_in = band_gather(normed(state, mlp_gain))
     gate = jnp.einsum("bsjd,df->bsjf", mlp_in, w_gate, preferred_element_type=jnp.float32)
     upper = jnp.einsum("bsjd,df->bsjf", mlp_in, w_up, preferred_element_type=jnp.float32)
     hidden = (jax.nn.silu(gate) * upper).astype(jnp.bfloat16)
-    out = jnp.einsum("bsjf,fd->bsjd", hidden, w_down, preferred_element_type=jnp.float32)
-    mlp_out = band_sum(out.astype(jnp.bfloat16))
+    out = jnp.einsum("bsjf,fd->bsjd", hidden, w_down, preferred_element_type=jnp.bfloat16)
+    mlp_out = band_sum(out)
     encoded = (state.astype(jnp.float32) + mlp_out).astype(jnp.bfloat16)
     chosen = (
         jnp.arange(pixels.shape[0], dtype=jnp.int32)[:, None] == clear_index[None, :]

time: 129 us -> 129 us (level)
    convert_element_type x3 -> x0, local copies, waits for them, and re-layouts: 3.14 us -> none  [the longest x1 1.51 us: shards(): attn_out = band_sum(out.astype(jnp.bfloat16))]
    dot_general x0 -> x2, local copies, waits for them, and re-layouts: none -> 3.02 us  [the longest x1 1.51 us: shards(): jnp.einsum('bsjh,hd->bsjd', context_rows, w_out, preferred_element_type=j...]
where the time goes in v14:
time: 129 us; the launch traced here: 128 us
  blocking collectives  58.8 us (46%)
  waiting for transfers between devices  29.6 us (23%)
  starting transfers between devices  21.9 us (17%)
  local copies, waits for them, and re-layouts  9.26 us (7%)
  other arithmetic  4.48 us (3%)
  matrix products  3.03 us (2%)
    all_to_all x1, blocking collectives, shards(): lax.all_to_all(payload.reshape(n_z, spec_mine, -1), 'z', 0, 0, tiled=True)  28.7 us
    all_to_all x2, waiting for transfers between devices, band_sum(): got = lax.all_to_all(part, 'band', 0, 0, tiled=True)  19.3 us
    all_to_all x1, blocking collectives, shards(): context_rows = lax.all_to_all(context, 'z', 0, 0, tiled=True)  15.8 us
    all_to_all x1, blocking collectives, band_gather(): return lax.all_to_all(sent, 'band', 0, 0, tiled=True)  14.3 us
    all_to_all x2, starting transfers between devices, band_sum(): got = lax.all_to_all(part, 'band', 0, 0, tiled=True)  10.6 us
    all_to_all x1, starting transfers between devices, band_gather(): return lax.all_to_all(sent, 'band', 0, 0, tiled=True)  9.39 us
    all_to_all x1, waiting for transfers between devices, band_gather(): return lax.all_to_all(sent, 'band', 0, 0, tiled=True)  9.15 us
  transfers between devices with their start and end apart: 4, of which 4 were waited for; matrix products, arithmetic and copies ran while one was open for 1% of the time, Pallas kernels for 0%

profile of v14, /device:TPU:2, one launch (start us, length us, event | category | flops | bytes accessed | tf_op | source)
XLA Modules:
  0.0 128.2 jit_solution(6682560050802743626)
XLA Ops:
  0.0 0.7 pad_clamp_fusion
  0.7 1.0 fusion.33
  1.7 1.0 fusion.35
  2.7 0.6 gather_fusion.1
  3.3 1.2 broadcast_in_dim.63
  4.5 9.4 %all-to-all-start = ((bf16[16,10,2,1024]{3,2,1,0:T(2,128)(2,1)}), bf16[16,10,2,1024]{3,2,1,0:T(2,128)(2,1)S(1)}, u32[]{:S(2)}, u32[]{:S(2)}) async-start(bf16[16,10,2,1024]{3,2,1,0:T(2,128)(2,1)} %broadcast_in_dim.63), calls=%async_computation | async-start | bytes 1310720 | tf_op jit(solution)/shard_map/all_to_all | solution.py:18
  14.6 9.1 %all-to-all-done = bf16[16,10,2,1024]{3,2,1,0:T(2,128)(2,1)S(1)} async-done(((bf16[16,10,2,1024]{3,2,1,0:T(2,128)(2,1)}), bf16[16,10,2,1024]{3,2,1,0:T(2,128)(2,1)S(1)}, u32[]{:S(2)}, u32[]{:S(2)}) %all-to-all-start) | async-done | bytes 655392 | tf_op jit(solution)/shard_map/all_to_all | solution.py:18
  24.6 28.7 %all_to_all.30 = bf16[16,2,1984]{2,1,0:T(2,128)(2,1)S(1)} all-to-all(bf16[16,2,1984]{2,1,0:T(2,128)(2,1)S(1)} %copy.113), channel_id=1, replica_groups=mesh['band'=16,'z'=16,'c'=2] {'z'}, dimensions={0} | all-to-all | bytes 253952 | tf_op jit(solution)/shard_map/all_to_all | solution.py:60
  54.0 1.9 %collective-permute-start = (bf16[2,16,11,128]{3,2,1,0:T(8,128)(2,1)S(1)}, bf16[2,16,11,128]{3,2,1,0:T(8,128)(2,1)S(1)}, u32[]{:S(2)}, u32[]{:S(2)}) collective-permute-start(bf16[2,16,11,128]{3,2,1,0:T(8,128)(2,1)S(1)} %pad_maximum_fusion.2), channel_id=1, source_target_pairs={{0,1},{1,0},{2,3},{3,2},{4,5},{5,4},{6,7},{7,6},{8,9},{9,8},{10,11... | collective-permute-start | bytes 270344 | tf_op jit(solution)/shard_map/ppermute | solution.py:67
  56.0 1.2 collective-permute-done
  59.3 15.8 %all_to_all.31 = bf16[16,2,640]{2,1,0:T(2,128)(2,1)S(1)} all-to-all(bf16[16,2,640]{2,1,0:T(2,128)(2,1)S(1)} %copy.122), channel_id=1, replica_groups=mesh['band'=16,'z'=16,'c'=2] {'z'}, dimensions={0} | all-to-all | bytes 81920 | tf_op jit(solution)/shard_map/all_to_all | solution.py:86
  75.5 1.5 %copy.125 = bf16[16,10,2,1024]{3,2,1,0:T(2,128)(2,1)} copy(bf16[16,10,2,1024]{3,0,2,1:T(8,128)(2,1)S(1)} %fusion.36) | data formatting | bytes 1310720 | tf_op jit(solution)/shard_map/bsjh,hd->bsjd/dot_general | solution.py:89
  77.0 5.7 %all-to-all-start.3 = ((bf16[16,10,2,1024]{3,2,1,0:T(2,128)(2,1)}), bf16[16,10,2,1024]{3,2,1,0:T(2,128)(2,1)S(1)}, u32[]{:S(2)}, u32[]{:S(2)}) async-start(bf16[16,10,2,1024]{3,2,1,0:T(2,128)(2,1)} %copy.125), calls=%async_computation.3 | async-start | bytes 1310720 | tf_op jit(solution)/shard_map/all_to_all | solution.py:22
  82.7 0.6 gather_fusion
  83.4 9.9 %all-to-all-done.3 = bf16[16,10,2,1024]{3,2,1,0:T(2,128)(2,1)S(1)} async-done(((bf16[16,10,2,1024]{3,2,1,0:T(2,128)(2,1)}), bf16[16,10,2,1024]{3,2,1,0:T(2,128)(2,1)S(1)}, u32[]{:S(2)}, u32[]{:S(2)}) %all-to-all-start.3) | async-done | bytes 655392 | tf_op jit(solution)/shard_map/all_to_all | solution.py:22
  93.3 0.6 convert_reduce_fusion.1
  94.5 14.3 %all_to_all.32 = bf16[16,10,2,1024]{3,2,1,0:T(2,128)(2,1)S(1)} all-to-all(bf16[16,10,2,1024]{3,2,1,0:T(2,128)(2,1)S(1)} %broadcast_in_dim.69), channel_id=1, replica_groups=mesh['band'=16,'z'=16,'c'=2] {'band'}, dimensions={0} | all-to-all | bytes 1310720 | tf_op jit(solution)/shard_map/all_to_all | solution.py:18
  109.1 0.7 copy-done.6
  109.8 0.9 fusion.6
  110.7 1.5 %copy.128 = bf16[16,10,2,1024]{3,2,1,0:T(2,128)(2,1)} copy(bf16[16,10,2,1024]{3,0,2,1:T(8,128)(2,1)S(1)} %fusion.6) | data formatting | bytes 1310720 | tf_op jit(solution)/shard_map/bsjf,fd->bsjd/dot_general | solution.py:96
  112.2 5.0 %all-to-all-start.5 = ((bf16[16,10,2,1024]{3,2,1,0:T(2,128)(2,1)}), bf16[16,10,2,1024]{3,2,1,0:T(2,128)(2,1)S(1)}, u32[]{:S(2)}, u32[]{:S(2)}) async-start(bf16[16,10,2,1024]{3,2,1,0:T(2,128)(2,1)} %copy.128), calls=%async_computation.5 | async-start | bytes 1310720 | tf_op jit(solution)/shard_map/all_to_all | solution.py:22
  117.3 9.4 %all-to-all-done.5 = bf16[16,10,2,1024]{3,2,1,0:T(2,128)(2,1)S(1)} async-done(((bf16[16,10,2,1024]{3,2,1,0:T(2,128)(2,1)}), bf16[16,10,2,1024]{3,2,1,0:T(2,128)(2,1)S(1)}, u32[]{:S(2)}, u32[]{:S(2)}) %all-to-all-start.5) | async-done | bytes 655392 | tf_op jit(solution)/shard_map/all_to_all | solution.py:22
  126.7 0.6 convert_reduce_fusion
  127.5 0.7 copy.131
  (60 shorter events, 5.3 us)
Async XLA Ops:
  0.0 109.1 %copy-start = (bf16[256,1024]{1,0:T(8,128)(2,1)S(1)}, bf16[256,1024]{1,0:T(8,128)(2,1)}, u32[]{:S(2)}) copy-start(bf16[256,1024]{1,0:T(8,128)(2,1)} %param.23) | copy-start | bytes 1572868
  4.5 19.2 %copy-start.7 = (bf16[1024,64]{0,1:T(8,128)(2,1)S(1)}, bf16[1024,64]{0,1:T(8,128)(2,1)}, u32[]{:S(2)}) copy-start(bf16[1024,64]{0,1:T(8,128)(2,1)} %param.18) | copy-start | bytes 393220
  4.5 19.2 %copy-start.8 = (bf16[1024,64]{0,1:T(8,128)(2,1)S(1)}, bf16[1024,64]{0,1:T(8,128)(2,1)}, u32[]{:S(2)}) copy-start(bf16[1024,64]{0,1:T(8,128)(2,1)} %param.17) | copy-start | bytes 393220
  4.5 19.2 %copy-start.9 = (bf16[1024,64]{0,1:T(8,128)(2,1)S(1)}, bf16[1024,64]{0,1:T(8,128)(2,1)}, u32[]{:S(2)}) copy-start(bf16[1024,64]{0,1:T(8,128)(2,1)} %param.16) | copy-start | bytes 393220
  4.5 19.2 %all-to-all-start = ((bf16[16,10,2,1024]{3,2,1,0:T(2,128)(2,1)}), bf16[16,10,2,1024]{3,2,1,0:T(2,128)(2,1)S(1)}, u32[]{:S(2)}, u32[]{:S(2)}) async-start(bf16[16,10,2,1024]{3,2,1,0:T(2,128)(2,1)} %broadcast_in_dim.63), calls=%async_computation | async-start | bytes 1310720 | tf_op jit(solution)/shard_map/all_to_all | solution.py:18
  54.0 3.2 %collective-permute-start = (bf16[2,16,11,128]{3,2,1,0:T(8,128)(2,1)S(1)}, bf16[2,16,11,128]{3,2,1,0:T(8,128)(2,1)S(1)}, u32[]{:S(2)}, u32[]{:S(2)}) collective-permute-start(bf16[2,16,11,128]{3,2,1,0:T(8,128)(2,1)S(1)} %pad_maximum_fusion.2), channel_id=1, source_target_pairs={{0,1},{1,0},{2,3},{3,2},{4,5},{5,4},{6,7},{7,6},{8,9},{9,8},{10,11... | collective-permute-start | bytes 270344 | tf_op jit(solution)/shard_map/ppermute | solution.py:67
  58.7 16.5 %copy-start.2 = (bf16[64,1024]{1,0:T(8,128)(2,1)S(1)}, bf16[64,1024]{1,0:T(8,128)(2,1)}, u32[]{:S(2)}) copy-start(bf16[64,1024]{1,0:T(8,128)(2,1)} %param.19) | copy-start | bytes 393220
  77.0 5.7 %copy-start.1 = (bf16[16,2,1024]{2,1,0:T(2,128)(2,1)S(1)}, bf16[16,2,1024]{2,1,0:T(2,128)(2,1)}, u32[]{:S(2)}) copy-start(bf16[16,2,1024]{2,1,0:T(2,128)(2,1)} %param.12) | copy-start | bytes 196612
  77.0 16.2 %all-to-all-start.3 = ((bf16[16,10,2,1024]{3,2,1,0:T(2,128)(2,1)}), bf16[16,10,2,1024]{3,2,1,0:T(2,128)(2,1)S(1)}, u32[]{:S(2)}, u32[]{:S(2)}) async-start(bf16[16,10,2,1024]{3,2,1,0:T(2,128)(2,1)} %copy.125), calls=%async_computation.3 | async-start | bytes 1310720 | tf_op jit(solution)/shard_map/all_to_all | solution.py:22
  82.7 11.3 %copy-start.3 = (f32[1024]{0:T(1024)S(1)}, f32[1024]{0:T(1024)}, u32[]{:S(2)}) copy-start(f32[1024]{0:T(1024)} %param.20) | copy-start | bytes 12292
  94.4 14.3 %copy-start.5 = (bf16[1024,256]{1,0:T(8,128)(2,1)S(1)}, bf16[1024,256]{1,0:T(8,128)(2,1)}, u32[]{:S(2)}) copy-start(bf16[1024,256]{1,0:T(8,128)(2,1)} %param.21) | copy-start | bytes 1572868
  108.8 1.0 copy-start.6
  112.2 5.0 %copy-start.4 = (s32[10]{0:T(128)S(1)}, s32[10]{0:T(128)}, u32[]{:S(2)}) copy-start(s32[10]{0:T(128)} %param.14) | copy-start | bytes 124
  112.2 14.5 %all-to-all-start.5 = ((bf16[16,10,2,1024]{3,2,1,0:T(2,128)(2,1)}), bf16[16,10,2,1024]{3,2,1,0:T(2,128)(2,1)S(1)}, u32[]{:S(2)}, u32[]{:S(2)}) async-start(bf16[16,10,2,1024]{3,2,1,0:T(2,128)(2,1)} %copy.128), calls=%async_computation.5 | async-start | bytes 1310720 | tf_op jit(solution)/shard_map/all_to_all | solution.py:22

commit v15 on v14

--- a/solution.py
+++ b/solution.py
@@ -65,14 +65,18 @@
     flag_rows = jnp.pad(live_mine, ((0, 0), (0, kv.shape[-1] - n_flag)))
     kv_flag = jnp.concatenate([kv, jnp.broadcast_to(flag_rows[None, :, None], (spec_mine,) + flag_rows.shape[:1] + (1, kv.shape[-1]))], axis=2)
     other = lax.ppermute(kv_flag, "c", [(0, 1), (1, 0)])
+    q_slots = n_z * slots_here
+    q = mine[:, :, :slots_here, : heads_here * HD].reshape(spec_mine, q_slots, heads_here, HD)
+
+    def scores_of(part):
+        k_part = part[:, :, :slots_here, : heads_here * HD].reshape(spec_mine, -1, heads_here, HD)
+        return jnp.einsum("sqhd,skhd->shqk", q, k_part, preferred_element_type=jnp.float32)
+
+    scores = jnp.concatenate([scores_of(kv_flag), scores_of(other)], axis=-1) * HD ** (-0.5)
     kv_flag = jnp.concatenate([kv_flag, other], axis=1)
     live = (kv_flag[0, :, slots_here, :slots_here] > 0.5).reshape(-1)
     kv = kv_flag[:, :, :slots_here].reshape(spec_mine, -1, 2 * heads_here * HD)
-    q_slots = n_z * slots_here
-    q = mine[:, :, :slots_here, : heads_here * HD].reshape(spec_mine, q_slots, heads_here, HD)
-    k = kv[..., : heads_here * HD].reshape(spec_mine, -1, heads_here, HD)
     v = kv[..., heads_here * HD :].reshape(spec_mine, -1, heads_here, HD)
-    scores = jnp.einsum("sqhd,skhd->shqk", q, k, preferred_element_type=jnp.float32) * HD ** (-0.5)
     masked = jnp.where(live[None, None, None, :], scores, -1e30)
     top = jnp.max(masked, axis=-1)
     expo = jnp.where(live[None, None, None, :], jnp.exp(masked - top[..., None]), 0.0)
@@ -90,8 +94,9 @@
     attn_out = band_sum(out)
     state = (kept.astype(jnp.float32) + attn_out).astype(jnp.bfloat16)
     mlp_in = band_gather(normed(state, mlp_gain))
-    gate = jnp.einsum("bsjd,df->bsjf", mlp_in, w_gate, preferred_element_type=jnp.float32)
-    upper = jnp.einsum("bsjd,df->bsjf", mlp_in, w_up, preferred_element_type=jnp.float32)
+    w_gate_up = jnp.concatenate([w_gate, w_up], axis=1)
+    both = jnp.einsum("bsjd,df->bsjf", mlp_in, w_gate_up, preferred_element_type=jnp.float32)
+    gate, upper = both[..., : w_gate.shape[1]], both[..., w_gate.shape[1] :]
     hidden = (jax.nn.silu(gate) * upper).astype(jnp.bfloat16)
     out = jnp.einsum("bsjf,fd->bsjd", hidden, w_down, preferred_element_type=jnp.bfloat16)
     mlp_out = band_sum(out)

time: 129 us -> 128 us (level)
  the two profiles are of different devices: /device:TPU:2 before, /device:TPU:32 now
where the time goes in v15:
time: 128 us
  blocking collectives  57.9 us (45%)
  waiting for transfers between devices  35.1 us (27%)
  starting transfers between devices  17.1 us (13%)
  local copies, waits for them, and re-layouts  8.88 us (7%)
  other arithmetic  5.14 us (4%)
  matrix products  2.55 us (2%)
    all_to_all x1, blocking collectives, shards(): lax.all_to_all(payload.reshape(n_z, spec_mine, -1), 'z', 0, 0, tiled=True)  27.6 us
    all_to_all x2, waiting for transfers between devices, band_sum(): got = lax.all_to_all(part, 'band', 0, 0, tiled=True)  22 us
    all_to_all x1, blocking collectives, shards(): context_rows = lax.all_to_all(context, 'z', 0, 0, tiled=True)  15.9 us
    all_to_all x1, blocking collectives, band_gather(): return lax.all_to_all(sent, 'band', 0, 0, tiled=True)  14.5 us
    all_to_all x1, waiting for transfers between devices, band_gather(): return lax.all_to_all(sent, 'band', 0, 0, tiled=True)  12.3 us
    all_to_all x2, starting transfers between devices, band_sum(): got = lax.all_to_all(part, 'band', 0, 0, tiled=True)  8.02 us
    all_to_all x1, starting transfers between devices, band_gather(): return lax.all_to_all(sent, 'band', 0, 0, tiled=True)  7.17 us
  transfers between devices with their start and end apart: 4, of which 4 were waited for; matrix products, arithmetic and copies ran while one was open for 1% of the time, Pallas kernels for 0%

profile of v15, /device:TPU:32, one launch (start us, length us, event | category | flops | bytes accessed | tf_op | source)
XLA Modules:
  0.0 127.7 jit_solution(77370938145319882)
XLA Ops:
  0.0 0.7 pad_clamp_fusion
  0.7 1.0 fusion.32
  1.7 1.0 fusion.34
  2.7 0.6 gather_fusion.1
  3.3 1.2 broadcast_in_dim.69
  4.5 7.2 %all-to-all-start = ((bf16[16,10,2,1024]{3,2,1,0:T(2,128)(2,1)}), bf16[16,10,2,1024]{3,2,1,0:T(2,128)(2,1)S(1)}, u32[]{:S(2)}, u32[]{:S(2)}) async-start(bf16[16,10,2,1024]{3,2,1,0:T(2,128)(2,1)} %broadcast_in_dim.69), calls=%async_computation | async-start | bytes 1310720 | tf_op jit(solution)/shard_map/all_to_all | solution.py:18
  12.4 12.3 %all-to-all-done = bf16[16,10,2,1024]{3,2,1,0:T(2,128)(2,1)S(1)} async-done(((bf16[16,10,2,1024]{3,2,1,0:T(2,128)(2,1)}), bf16[16,10,2,1024]{3,2,1,0:T(2,128)(2,1)S(1)}, u32[]{:S(2)}, u32[]{:S(2)}) %all-to-all-start) | async-done | bytes 655392 | tf_op jit(solution)/shard_map/all_to_all | solution.py:18
  25.5 27.6 %all_to_all.30 = bf16[16,2,1984]{2,1,0:T(2,128)(2,1)S(1)} all-to-all(bf16[16,2,1984]{2,1,0:T(2,128)(2,1)S(1)} %copy.129), channel_id=1, replica_groups=mesh['band'=16,'z'=16,'c'=2] {'z'}, dimensions={0} | all-to-all | bytes 253952 | tf_op jit(solution)/shard_map/all_to_all | solution.py:60
  53.8 1.9 %collective-permute-start = (bf16[2,16,11,128]{3,2,1,0:T(8,128)(2,1)S(1)}, bf16[2,16,11,128]{3,2,1,0:T(8,128)(2,1)S(1)}, u32[]{:S(2)}, u32[]{:S(2)}) collective-permute-start(bf16[2,16,11,128]{3,2,1,0:T(8,128)(2,1)S(1)} %pad_maximum_fusion.2), channel_id=1, source_target_pairs={{0,1},{1,0},{2,3},{3,2},{4,5},{5,4},{6,7},{7,6},{8,9},{9,8},{10,11... | collective-permute-start | bytes 270344 | tf_op jit(solution)/shard_map/ppermute | solution.py:67
  56.2 0.8 collective-permute-done
  58.7 0.4 fusion.3
  59.4 15.9 %all_to_all.31 = bf16[16,2,640]{2,1,0:T(2,128)(2,1)S(1)} all-to-all(bf16[16,2,640]{2,1,0:T(2,128)(2,1)S(1)} %copy.142), channel_id=1, replica_groups=mesh['band'=16,'z'=16,'c'=2] {'z'}, dimensions={0} | all-to-all | bytes 81920 | tf_op jit(solution)/shard_map/all_to_all | solution.py:90
  75.8 1.5 %copy.145 = bf16[16,10,2,1024]{3,2,1,0:T(2,128)(2,1)} copy(bf16[16,10,2,1024]{3,0,2,1:T(8,128)(2,1)S(1)} %fusion.35) | data formatting | bytes 1310720 | tf_op jit(solution)/shard_map/bsjh,hd->bsjd/dot_general | solution.py:93
  77.3 4.3 %all-to-all-start.3 = ((bf16[16,10,2,1024]{3,2,1,0:T(2,128)(2,1)}), bf16[16,10,2,1024]{3,2,1,0:T(2,128)(2,1)S(1)}, u32[]{:S(2)}, u32[]{:S(2)}) async-start(bf16[16,10,2,1024]{3,2,1,0:T(2,128)(2,1)} %copy.145), calls=%async_computation.3 | async-start | bytes 1310720 | tf_op jit(solution)/shard_map/all_to_all | solution.py:22
  81.6 0.6 gather_fusion
  82.3 11.3 %all-to-all-done.3 = bf16[16,10,2,1024]{3,2,1,0:T(2,128)(2,1)S(1)} async-done(((bf16[16,10,2,1024]{3,2,1,0:T(2,128)(2,1)}), bf16[16,10,2,1024]{3,2,1,0:T(2,128)(2,1)S(1)}, u32[]{:S(2)}, u32[]{:S(2)}) %all-to-all-start.3) | async-done | bytes 655392 | tf_op jit(solution)/shard_map/all_to_all | solution.py:22
  93.6 0.6 convert_reduce_fusion.1
  94.8 14.5 %all_to_all.32 = bf16[16,10,2,1024]{3,2,1,0:T(2,128)(2,1)S(1)} all-to-all(bf16[16,10,2,1024]{3,2,1,0:T(2,128)(2,1)S(1)} %broadcast_in_dim.78), channel_id=1, replica_groups=mesh['band'=16,'z'=16,'c'=2] {'band'}, dimensions={0} | all-to-all | bytes 1310720 | tf_op jit(solution)/shard_map/all_to_all | solution.py:18
  109.3 0.5 fusion.4
  110.2 1.5 %copy.147 = bf16[16,10,2,1024]{3,2,1,0:T(2,128)(2,1)} copy(bf16[16,10,2,1024]{3,0,2,1:T(8,128)(2,1)S(1)} %fusion.9) | data formatting | bytes 1310720 | tf_op jit(solution)/shard_map/bsjf,fd->bsjd/dot_general | solution.py:101
  111.7 3.7 %all-to-all-start.5 = ((bf16[16,10,2,1024]{3,2,1,0:T(2,128)(2,1)}), bf16[16,10,2,1024]{3,2,1,0:T(2,128)(2,1)S(1)}, u32[]{:S(2)}, u32[]{:S(2)}) async-start(bf16[16,10,2,1024]{3,2,1,0:T(2,128)(2,1)} %copy.147), calls=%async_computation.5 | async-start | bytes 1310720 | tf_op jit(solution)/shard_map/all_to_all | solution.py:22
  115.6 10.7 %all-to-all-done.5 = bf16[16,10,2,1024]{3,2,1,0:T(2,128)(2,1)S(1)} async-done(((bf16[16,10,2,1024]{3,2,1,0:T(2,128)(2,1)}), bf16[16,10,2,1024]{3,2,1,0:T(2,128)(2,1)S(1)}, u32[]{:S(2)}, u32[]{:S(2)}) %all-to-all-start.5) | async-done | bytes 655392 | tf_op jit(solution)/shard_map/all_to_all | solution.py:22
  126.2 0.6 convert_reduce_fusion
  127.0 0.7 copy.150
  (65 shorter events, 5.7 us)
Async XLA Ops:
  0.0 109.8 %copy-start = (bf16[256,1024]{1,0:T(8,128)(2,1)S(1)}, bf16[256,1024]{1,0:T(8,128)(2,1)}, u32[]{:S(2)}) copy-start(bf16[256,1024]{1,0:T(8,128)(2,1)} %param.23) | copy-start | bytes 1572868
  4.5 20.1 %copy-start.7 = (bf16[1024,64]{0,1:T(8,128)(2,1)S(1)}, bf16[1024,64]{0,1:T(8,128)(2,1)}, u32[]{:S(2)}) copy-start(bf16[1024,64]{0,1:T(8,128)(2,1)} %param.18) | copy-start | bytes 393220
  4.5 20.1 %copy-start.8 = (bf16[1024,64]{0,1:T(8,128)(2,1)S(1)}, bf16[1024,64]{0,1:T(8,128)(2,1)}, u32[]{:S(2)}) copy-start(bf16[1024,64]{0,1:T(8,128)(2,1)} %param.17) | copy-start | bytes 393220
  4.5 20.1 %copy-start.9 = (bf16[1024,64]{0,1:T(8,128)(2,1)S(1)}, bf16[1024,64]{0,1:T(8,128)(2,1)}, u32[]{:S(2)}) copy-start(bf16[1024,64]{0,1:T(8,128)(2,1)} %param.16) | copy-start | bytes 393220
  4.5 20.1 %all-to-all-start = ((bf16[16,10,2,1024]{3,2,1,0:T(2,128)(2,1)}), bf16[16,10,2,1024]{3,2,1,0:T(2,128)(2,1)S(1)}, u32[]{:S(2)}, u32[]{:S(2)}) async-start(bf16[16,10,2,1024]{3,2,1,0:T(2,128)(2,1)} %broadcast_in_dim.69), calls=%async_computation | async-start | bytes 1310720 | tf_op jit(solution)/shard_map/all_to_all | solution.py:18
  53.8 3.2 %collective-permute-start = (bf16[2,16,11,128]{3,2,1,0:T(8,128)(2,1)S(1)}, bf16[2,16,11,128]{3,2,1,0:T(8,128)(2,1)S(1)}, u32[]{:S(2)}, u32[]{:S(2)}) collective-permute-start(bf16[2,16,11,128]{3,2,1,0:T(8,128)(2,1)S(1)} %pad_maximum_fusion.2), channel_id=1, source_target_pairs={{0,1},{1,0},{2,3},{3,2},{4,5},{5,4},{6,7},{7,6},{8,9},{9,8},{10,11... | collective-permute-start | bytes 270344 | tf_op jit(solution)/shard_map/ppermute | solution.py:67
  59.1 16.3 %copy-start.2 = (bf16[64,1024]{1,0:T(8,128)(2,1)S(1)}, bf16[64,1024]{1,0:T(8,128)(2,1)}, u32[]{:S(2)}) copy-start(bf16[64,1024]{1,0:T(8,128)(2,1)} %param.19) | copy-start | bytes 393220
  77.3 4.3 %copy-start.1 = (bf16[16,2,1024]{2,1,0:T(2,128)(2,1)S(1)}, bf16[16,2,1024]{2,1,0:T(2,128)(2,1)}, u32[]{:S(2)}) copy-start(bf16[16,2,1024]{2,1,0:T(2,128)(2,1)} %param.12) | copy-start | bytes 196612
  77.3 16.3 %all-to-all-start.3 = ((bf16[16,10,2,1024]{3,2,1,0:T(2,128)(2,1)}), bf16[16,10,2,1024]{3,2,1,0:T(2,128)(2,1)S(1)}, u32[]{:S(2)}, u32[]{:S(2)}) async-start(bf16[16,10,2,1024]{3,2,1,0:T(2,128)(2,1)} %copy.145), calls=%async_computation.3 | async-start | bytes 1310720 | tf_op jit(solution)/shard_map/all_to_all | solution.py:22
  81.6 12.7 %copy-start.3 = (f32[1024]{0:T(1024)S(1)}, f32[1024]{0:T(1024)}, u32[]{:S(2)}) copy-start(f32[1024]{0:T(1024)} %param.20) | copy-start | bytes 12292
  94.8 14.5 %copy-start.5 = (bf16[1024,256]{1,0:T(8,128)(2,1)S(1)}, bf16[1024,256]{1,0:T(8,128)(2,1)}, u32[]{:S(2)}) copy-start(bf16[1024,256]{1,0:T(8,128)(2,1)} %param.22) | copy-start | bytes 1572868
  94.8 14.5 %copy-start.6 = (bf16[1024,256]{1,0:T(8,128)(2,1)S(1)}, bf16[1024,256]{1,0:T(8,128)(2,1)}, u32[]{:S(2)}) copy-start(bf16[1024,256]{1,0:T(8,128)(2,1)} %param.21) | copy-start | bytes 1572868
  111.7 3.7 %copy-start.4 = (s32[10]{0:T(128)S(1)}, s32[10]{0:T(128)}, u32[]{:S(2)}) copy-start(s32[10]{0:T(128)} %param.14) | copy-start | bytes 124
  111.7 14.5 %all-to-all-start.5 = ((bf16[16,10,2,1024]{3,2,1,0:T(2,128)(2,1)}), bf16[16,10,2,1024]{3,2,1,0:T(2,128)(2,1)S(1)}, u32[]{:S(2)}, u32[]{:S(2)}) async-start(bf16[16,10,2,1024]{3,2,1,0:T(2,128)(2,1)} %copy.147), calls=%async_computation.5 | async-start | bytes 1310720 | tf_op jit(solution)/shard_map/all_to_all | solution.py:22

commit v16 on v15

--- a/solution.py
+++ b/solution.py
@@ -42,7 +42,7 @@
     slots_here, spec_here, width = kept.shape
     n_band = lax.axis_size("band")
     spec = n_band * spec_here
-    attn_in = band_gather(jnp.take(normed(pixels, attn_gain), clear_index, axis=0, mode="clip"))
+    attn_in = normed(band_gather(kept), attn_gain)
     flat = attn_in.reshape(-1, width)
     heads_here = w_query.shape[1] // HD
 

time: 128 us -> 126 us (0.984)
  the two profiles are of different devices: /device:TPU:32 before, /device:TPU:2 now
where the time goes in v16:
time: 126 us
  blocking collectives  74.7 us (59%)
  waiting for transfers between devices  19.3 us (15%)
  starting transfers between devices  16.2 us (13%)
  local copies, waits for them, and re-layouts  8.26 us (7%)
  other arithmetic  3.46 us (3%)
  matrix products  2.62 us (2%)
    all_to_all x1, blocking collectives, shards(): lax.all_to_all(payload.reshape(n_z, spec_mine, -1), 'z', 0, 0, tiled=True)  28.7 us
    all_to_all x1, blocking collectives, band_sum(): got = lax.all_to_all(part, 'band', 0, 0, tiled=True)  15.9 us
    all_to_all x1, blocking collectives, shards(): context_rows = lax.all_to_all(context, 'z', 0, 0, tiled=True)  15.8 us
    all_to_all x1, blocking collectives, band_gather(): return lax.all_to_all(sent, 'band', 0, 0, tiled=True)  14.3 us
    all_to_all x1, waiting for transfers between devices, band_sum(): got = lax.all_to_all(part, 'band', 0, 0, tiled=True)  9.43 us
    all_to_all x1, starting transfers between devices, band_gather(): return lax.all_to_all(sent, 'band', 0, 0, tiled=True)  9.26 us
    all_to_all x1, waiting for transfers between devices, band_gather(): return lax.all_to_all(sent, 'band', 0, 0, tiled=True)  9.05 us
    all_to_all x1, starting transfers between devices, band_sum(): got = lax.all_to_all(part, 'band', 0, 0, tiled=True)  4.98 us
  transfers between devices with their start and end apart: 3, of which 3 were waited for; matrix products, arithmetic and copies ran while one was open for 1% of the time, Pallas kernels for 0%

profile of v16, /device:TPU:2, one launch (start us, length us, event | category | flops | bytes accessed | tf_op | source)
XLA Modules:
  0.0 125.6 jit_solution(9369106310463445320)
XLA Ops:
  0.0 0.7 pad_clamp_fusion
  0.7 1.5 %gather_fusion = bf16[10,2,1024]{2,1,0:T(2,128)(2,1)S(1)} fusion(bf16[16,2,1024]{2,1,0:T(2,128)(2,1)} %param.12, s32[1024]{0:T(1024)S(1)} %pad_clamp_fusion), kind=kCustom, calls=%fused_computation | custom fusion | bytes 81960 | tf_op jit(solution)/shard_map/jit(_take)/gather | solution.py:41
  2.2 1.2 broadcast_in_dim.68
  3.4 9.3 %all-to-all-start = ((bf16[16,10,2,1024]{3,2,1,0:T(2,128)(2,1)}), bf16[16,10,2,1024]{3,2,1,0:T(2,128)(2,1)S(1)}, u32[]{:S(2)}, u32[]{:S(2)}) async-start(bf16[16,10,2,1024]{3,2,1,0:T(2,128)(2,1)} %broadcast_in_dim.68), calls=%async_computation | async-start | bytes 1310720 | tf_op jit(solution)/shard_map/all_to_all | solution.py:18
  13.4 9.1 %all-to-all-done = bf16[16,10,2,1024]{3,2,1,0:T(2,128)(2,1)S(1)} async-done(((bf16[16,10,2,1024]{3,2,1,0:T(2,128)(2,1)}), bf16[16,10,2,1024]{3,2,1,0:T(2,128)(2,1)S(1)}, u32[]{:S(2)}, u32[]{:S(2)}) %all-to-all-start) | async-done | bytes 655392 | tf_op jit(solution)/shard_map/all_to_all | solution.py:18
  22.8 0.4 convolution_bitcast_fusion
  23.7 28.7 %all_to_all.30 = bf16[16,2,1984]{2,1,0:T(2,128)(2,1)S(1)} all-to-all(bf16[16,2,1984]{2,1,0:T(2,128)(2,1)S(1)} %copy.102), channel_id=1, replica_groups=mesh['band'=16,'z'=16,'c'=2] {'z'}, dimensions={0} | all-to-all | bytes 253952 | tf_op jit(solution)/shard_map/all_to_all | solution.py:60
  53.2 1.9 %collective-permute-start = (bf16[2,16,11,128]{3,2,1,0:T(8,128)(2,1)S(1)}, bf16[2,16,11,128]{3,2,1,0:T(8,128)(2,1)S(1)}, u32[]{:S(2)}, u32[]{:S(2)}) collective-permute-start(bf16[2,16,11,128]{3,2,1,0:T(8,128)(2,1)S(1)} %pad_maximum_fusion.2), channel_id=1, source_target_pairs={{0,1},{1,0},{2,3},{3,2},{4,5},{5,4},{6,7},{7,6},{8,9},{9,8},{10,11... | collective-permute-start | bytes 270344 | tf_op jit(solution)/shard_map/ppermute | solution.py:67
  55.7 0.8 collective-permute-done
  57.3 0.4 select_reduce_fusion
  58.1 0.4 fusion.6
  58.8 15.8 %all_to_all.31 = bf16[16,2,640]{2,1,0:T(2,128)(2,1)S(1)} all-to-all(bf16[16,2,640]{2,1,0:T(2,128)(2,1)S(1)} %copy.115), channel_id=1, replica_groups=mesh['band'=16,'z'=16,'c'=2] {'z'}, dimensions={0} | all-to-all | bytes 81920 | tf_op jit(solution)/shard_map/all_to_all | solution.py:90
  75.1 0.7 copy.118
  75.7 15.9 %all_to_all.32 = bf16[16,10,2,1024]{3,2,1,0:T(2,128)(2,1)S(1)} all-to-all(bf16[16,10,2,1024]{3,2,1,0:T(2,128)(2,1)S(1)} %copy.118), channel_id=1, replica_groups=mesh['band'=16,'z'=16,'c'=2] {'band'}, dimensions={0} | all-to-all | bytes 1310720 | tf_op jit(solution)/shard_map/all_to_all | solution.py:22
  91.6 0.6 convert_reduce_fusion.1
  92.5 0.3 broadcast_in_dim.77
  92.8 14.3 %all_to_all.33 = bf16[16,10,2,1024]{3,2,1,0:T(2,128)(2,1)S(1)} all-to-all(bf16[16,10,2,1024]{3,2,1,0:T(2,128)(2,1)S(1)} %broadcast_in_dim.77), channel_id=1, replica_groups=mesh['band'=16,'z'=16,'c'=2] {'band'}, dimensions={0} | all-to-all | bytes 1310720 | tf_op jit(solution)/shard_map/all_to_all | solution.py:18
  107.1 0.5 fusion.7
  107.7 0.3 fusion.15
  108.0 1.5 %copy.120 = bf16[16,10,2,1024]{3,2,1,0:T(2,128)(2,1)} copy(bf16[16,10,2,1024]{3,0,2,1:T(8,128)(2,1)S(1)} %fusion.15) | data formatting | bytes 1310720 | tf_op jit(solution)/shard_map/bsjf,fd->bsjd/dot_general | solution.py:101
  109.5 5.0 %all-to-all-start.5 = ((bf16[16,10,2,1024]{3,2,1,0:T(2,128)(2,1)}), bf16[16,10,2,1024]{3,2,1,0:T(2,128)(2,1)S(1)}, u32[]{:S(2)}, u32[]{:S(2)}) async-start(bf16[16,10,2,1024]{3,2,1,0:T(2,128)(2,1)} %copy.120), calls=%async_computation.5 | async-start | bytes 1310720 | tf_op jit(solution)/shard_map/all_to_all | solution.py:22
  114.6 9.4 %all-to-all-done.5 = bf16[16,10,2,1024]{3,2,1,0:T(2,128)(2,1)S(1)} async-done(((bf16[16,10,2,1024]{3,2,1,0:T(2,128)(2,1)}), bf16[16,10,2,1024]{3,2,1,0:T(2,128)(2,1)S(1)}, u32[]{:S(2)}, u32[]{:S(2)}) %all-to-all-start.5) | async-done | bytes 655392 | tf_op jit(solution)/shard_map/all_to_all | solution.py:22
  124.1 0.6 convert_reduce_fusion
  124.9 0.7 copy.123
  (64 shorter events, 4.6 us)
Async XLA Ops:
  0.0 107.7 %copy-start = (bf16[256,1024]{1,0:T(8,128)(2,1)S(1)}, bf16[256,1024]{1,0:T(8,128)(2,1)}, u32[]{:S(2)}) copy-start(bf16[256,1024]{1,0:T(8,128)(2,1)} %param.23) | copy-start | bytes 1572868
  3.4 19.1 %all-to-all-start = ((bf16[16,10,2,1024]{3,2,1,0:T(2,128)(2,1)}), bf16[16,10,2,1024]{3,2,1,0:T(2,128)(2,1)S(1)}, u32[]{:S(2)}, u32[]{:S(2)}) async-start(bf16[16,10,2,1024]{3,2,1,0:T(2,128)(2,1)} %broadcast_in_dim.68), calls=%async_computation | async-start | bytes 1310720 | tf_op jit(solution)/shard_map/all_to_all | solution.py:18
  12.6 10.1 %copy-start.7 = (bf16[1024,64]{0,1:T(8,128)(2,1)S(1)}, bf16[1024,64]{0,1:T(8,128)(2,1)}, u32[]{:S(2)}) copy-start(bf16[1024,64]{0,1:T(8,128)(2,1)} %param.18) | copy-start | bytes 393220
  12.6 10.1 %copy-start.8 = (bf16[1024,64]{0,1:T(8,128)(2,1)S(1)}, bf16[1024,64]{0,1:T(8,128)(2,1)}, u32[]{:S(2)}) copy-start(bf16[1024,64]{0,1:T(8,128)(2,1)} %param.17) | copy-start | bytes 393220
  12.7 10.1 %copy-start.9 = (bf16[1024,64]{0,1:T(8,128)(2,1)S(1)}, bf16[1024,64]{0,1:T(8,128)(2,1)}, u32[]{:S(2)}) copy-start(bf16[1024,64]{0,1:T(8,128)(2,1)} %param.16) | copy-start | bytes 393220
  12.7 10.1 %copy-start.10 = (f32[1024]{0:T(1024)S(1)}, f32[1024]{0:T(1024)}, u32[]{:S(2)}) copy-start(f32[1024]{0:T(1024)} %param.15) | copy-start | bytes 12292
  53.2 3.2 %collective-permute-start = (bf16[2,16,11,128]{3,2,1,0:T(8,128)(2,1)S(1)}, bf16[2,16,11,128]{3,2,1,0:T(8,128)(2,1)S(1)}, u32[]{:S(2)}, u32[]{:S(2)}) collective-permute-start(bf16[2,16,11,128]{3,2,1,0:T(8,128)(2,1)S(1)} %pad_maximum_fusion.2), channel_id=1, source_target_pairs={{0,1},{1,0},{2,3},{3,2},{4,5},{5,4},{6,7},{7,6},{8,9},{9,8},{10,11... | collective-permute-start | bytes 270344 | tf_op jit(solution)/shard_map/ppermute | solution.py:67
  58.5 16.2 %copy-start.1 = (bf16[64,1024]{1,0:T(8,128)(2,1)S(1)}, bf16[64,1024]{1,0:T(8,128)(2,1)}, u32[]{:S(2)}) copy-start(bf16[64,1024]{1,0:T(8,128)(2,1)} %param.19) | copy-start | bytes 393220
  91.6 0.7 copy-start.3
  92.8 14.3 %copy-start.5 = (bf16[1024,256]{1,0:T(8,128)(2,1)S(1)}, bf16[1024,256]{1,0:T(8,128)(2,1)}, u32[]{:S(2)}) copy-start(bf16[1024,256]{1,0:T(8,128)(2,1)} %param.22) | copy-start | bytes 1572868
  92.8 14.3 %copy-start.6 = (bf16[1024,256]{1,0:T(8,128)(2,1)S(1)}, bf16[1024,256]{1,0:T(8,128)(2,1)}, u32[]{:S(2)}) copy-start(bf16[1024,256]{1,0:T(8,128)(2,1)} %param.21) | copy-start | bytes 1572868
  109.5 5.0 %copy-start.4 = (s32[10]{0:T(128)S(1)}, s32[10]{0:T(128)}, u32[]{:S(2)}) copy-start(s32[10]{0:T(128)} %param.14) | copy-start | bytes 124
  109.5 14.5 %all-to-all-start.5 = ((bf16[16,10,2,1024]{3,2,1,0:T(2,128)(2,1)}), bf16[16,10,2,1024]{3,2,1,0:T(2,128)(2,1)S(1)}, u32[]{:S(2)}, u32[]{:S(2)}) async-start(bf16[16,10,2,1024]{3,2,1,0:T(2,128)(2,1)} %copy.120), calls=%async_computation.5 | async-start | bytes 1310720 | tf_op jit(solution)/shard_map/all_to_all | solution.py:22
  114.5 10.2 %copy-start.2 = (bf16[16,2,1024]{2,1,0:T(2,128)(2,1)S(1)}, bf16[16,2,1024]{2,1,0:T(2,128)(2,1)}, u32[]{:S(2)}) copy-start(bf16[16,2,1024]{2,1,0:T(2,128)(2,1)} %param.12) | copy-start | bytes 196612

commit v17 on v16

--- a/solution.py
+++ b/solution.py
@@ -93,7 +93,7 @@
     out = jnp.einsum("bsjh,hd->bsjd", context_rows, w_out, preferred_element_type=jnp.bfloat16)
     attn_out = band_sum(out)
     state = (kept.astype(jnp.float32) + attn_out).astype(jnp.bfloat16)
-    mlp_in = band_gather(normed(state, mlp_gain))
+    mlp_in = normed(band_gather(state), mlp_gain)
     w_gate_up = jnp.concatenate([w_gate, w_up], axis=1)
     both = jnp.einsum("bsjd,df->bsjf", mlp_in, w_gate_up, preferred_element_type=jnp.float32)
     gate, upper = both[..., : w_gate.shape[1]], both[..., w_gate.shape[1] :]

time: 126 us -> 127 us (level)
  no operation moved by 1% of the time
where the time goes in v17:
time: 127 us; the launch traced here: 126 us
  blocking collectives  74.7 us (59%)
  waiting for transfers between devices  19.3 us (15%)
  starting transfers between devices  16.2 us (13%)
  local copies, waits for them, and re-layouts  8.98 us (7%)
  other arithmetic  3.53 us (3%)
  matrix products  2.67 us (2%)
    all_to_all x1, blocking collectives, shards(): lax.all_to_all(payload.reshape(n_z, spec_mine, -1), 'z', 0, 0, tiled=True)  28.7 us
    all_to_all x1, blocking collectives, band_sum(): got = lax.all_to_all(part, 'band', 0, 0, tiled=True)  15.9 us
    all_to_all x1, blocking collectives, shards(): context_rows = lax.all_to_all(context, 'z', 0, 0, tiled=True)  15.8 us
    all_to_all x1, blocking collectives, band_gather(): return lax.all_to_all(sent, 'band', 0, 0, tiled=True)  14.3 us
    all_to_all x1, waiting for transfers between devices, band_sum(): got = lax.all_to_all(part, 'band', 0, 0, tiled=True)  9.43 us
    all_to_all x1, starting transfers between devices, band_gather(): return lax.all_to_all(sent, 'band', 0, 0, tiled=True)  9.26 us
    all_to_all x1, waiting for transfers between devices, band_gather(): return lax.all_to_all(sent, 'band', 0, 0, tiled=True)  9.05 us
    all_to_all x1, starting transfers between devices, band_sum(): got = lax.all_to_all(part, 'band', 0, 0, tiled=True)  4.97 us
  transfers between devices with their start and end apart: 3, of which 3 were waited for; matrix products, arithmetic and copies ran while one was open for 1% of the time, Pallas kernels for 0%

profile of v17, /device:TPU:2, one launch (start us, length us, event | category | flops | bytes accessed | tf_op | source)
XLA Modules:
  0.0 126.4 jit_solution(3400493492765387082)
XLA Ops:
  0.0 0.7 pad_clamp_fusion
  0.7 1.5 %gather_fusion = bf16[10,2,1024]{2,1,0:T(2,128)(2,1)S(1)} fusion(bf16[16,2,1024]{2,1,0:T(2,128)(2,1)} %param.12, s32[1024]{0:T(1024)S(1)} %pad_clamp_fusion), kind=kCustom, calls=%fused_computation | custom fusion | bytes 81960 | tf_op jit(solution)/shard_map/jit(_take)/gather | solution.py:41
  2.2 1.2 broadcast_in_dim.68
  3.4 9.3 %all-to-all-start = ((bf16[16,10,2,1024]{3,2,1,0:T(2,128)(2,1)}), bf16[16,10,2,1024]{3,2,1,0:T(2,128)(2,1)S(1)}, u32[]{:S(2)}, u32[]{:S(2)}) async-start(bf16[16,10,2,1024]{3,2,1,0:T(2,128)(2,1)} %broadcast_in_dim.68), calls=%async_computation | async-start | bytes 1310720 | tf_op jit(solution)/shard_map/all_to_all | solution.py:18
  13.4 9.1 %all-to-all-done = bf16[16,10,2,1024]{3,2,1,0:T(2,128)(2,1)S(1)} async-done(((bf16[16,10,2,1024]{3,2,1,0:T(2,128)(2,1)}), bf16[16,10,2,1024]{3,2,1,0:T(2,128)(2,1)S(1)}, u32[]{:S(2)}, u32[]{:S(2)}) %all-to-all-start) | async-done | bytes 655392 | tf_op jit(solution)/shard_map/all_to_all | solution.py:18
  22.8 0.4 convolution_bitcast_fusion
  23.7 28.7 %all_to_all.30 = bf16[16,2,1984]{2,1,0:T(2,128)(2,1)S(1)} all-to-all(bf16[16,2,1984]{2,1,0:T(2,128)(2,1)S(1)} %copy.102), channel_id=1, replica_groups=mesh['band'=16,'z'=16,'c'=2] {'z'}, dimensions={0} | all-to-all | bytes 253952 | tf_op jit(solution)/shard_map/all_to_all | solution.py:60
  53.2 1.9 %collective-permute-start = (bf16[2,16,11,128]{3,2,1,0:T(8,128)(2,1)S(1)}, bf16[2,16,11,128]{3,2,1,0:T(8,128)(2,1)S(1)}, u32[]{:S(2)}, u32[]{:S(2)}) collective-permute-start(bf16[2,16,11,128]{3,2,1,0:T(8,128)(2,1)S(1)} %pad_maximum_fusion.2), channel_id=1, source_target_pairs={{0,1},{1,0},{2,3},{3,2},{4,5},{5,4},{6,7},{7,6},{8,9},{9,8},{10,11... | collective-permute-start | bytes 270344 | tf_op jit(solution)/shard_map/ppermute | solution.py:67
  55.7 0.8 collective-permute-done
  57.3 0.4 select_reduce_fusion
  58.1 0.4 fusion.9
  58.8 15.8 %all_to_all.31 = bf16[16,2,640]{2,1,0:T(2,128)(2,1)S(1)} all-to-all(bf16[16,2,640]{2,1,0:T(2,128)(2,1)S(1)} %copy.115), channel_id=1, replica_groups=mesh['band'=16,'z'=16,'c'=2] {'z'}, dimensions={0} | all-to-all | bytes 81920 | tf_op jit(solution)/shard_map/all_to_all | solution.py:90
  75.1 0.7 copy.118
  75.7 15.9 %all_to_all.32 = bf16[16,10,2,1024]{3,2,1,0:T(2,128)(2,1)S(1)} all-to-all(bf16[16,10,2,1024]{3,2,1,0:T(2,128)(2,1)S(1)} %copy.118), channel_id=1, replica_groups=mesh['band'=16,'z'=16,'c'=2] {'band'}, dimensions={0} | all-to-all | bytes 1310720 | tf_op jit(solution)/shard_map/all_to_all | solution.py:22
  91.6 0.6 convert_reduce_fusion.1
  92.6 14.3 %all_to_all.33 = bf16[16,10,2,1024]{3,2,1,0:T(2,128)(2,1)S(1)} all-to-all(bf16[16,10,2,1024]{3,2,1,0:T(2,128)(2,1)S(1)} %broadcast_in_dim.77), channel_id=1, replica_groups=mesh['band'=16,'z'=16,'c'=2] {'band'}, dimensions={0} | all-to-all | bytes 1310720 | tf_op jit(solution)/shard_map/all_to_all | solution.py:18
  107.2 0.7 copy-done.4
  107.9 0.5 fusion.10
  108.5 0.4 fusion.21
  108.9 1.5 %copy.120 = bf16[16,10,2,1024]{3,2,1,0:T(2,128)(2,1)} copy(bf16[16,10,2,1024]{3,0,2,1:T(8,128)(2,1)S(1)} %fusion.21) | data formatting | bytes 1310720 | tf_op jit(solution)/shard_map/bsjf,fd->bsjd/dot_general | solution.py:101
  110.4 5.0 %all-to-all-start.5 = ((bf16[16,10,2,1024]{3,2,1,0:T(2,128)(2,1)}), bf16[16,10,2,1024]{3,2,1,0:T(2,128)(2,1)S(1)}, u32[]{:S(2)}, u32[]{:S(2)}) async-start(bf16[16,10,2,1024]{3,2,1,0:T(2,128)(2,1)} %copy.120), calls=%async_computation.5 | async-start | bytes 1310720 | tf_op jit(solution)/shard_map/all_to_all | solution.py:22
  115.5 9.4 %all-to-all-done.5 = bf16[16,10,2,1024]{3,2,1,0:T(2,128)(2,1)S(1)} async-done(((bf16[16,10,2,1024]{3,2,1,0:T(2,128)(2,1)}), bf16[16,10,2,1024]{3,2,1,0:T(2,128)(2,1)S(1)}, u32[]{:S(2)}, u32[]{:S(2)}) %all-to-all-start.5) | async-done | bytes 655392 | tf_op jit(solution)/shard_map/all_to_all | solution.py:22
  124.9 0.6 convert_reduce_fusion
  125.7 0.7 copy.123
  (64 shorter events, 5.0 us)
Async XLA Ops:
  0.0 108.5 %copy-start = (bf16[256,1024]{1,0:T(8,128)(2,1)S(1)}, bf16[256,1024]{1,0:T(8,128)(2,1)}, u32[]{:S(2)}) copy-start(bf16[256,1024]{1,0:T(8,128)(2,1)} %param.23) | copy-start | bytes 1572868
  3.4 19.1 %all-to-all-start = ((bf16[16,10,2,1024]{3,2,1,0:T(2,128)(2,1)}), bf16[16,10,2,1024]{3,2,1,0:T(2,128)(2,1)S(1)}, u32[]{:S(2)}, u32[]{:S(2)}) async-start(bf16[16,10,2,1024]{3,2,1,0:T(2,128)(2,1)} %broadcast_in_dim.68), calls=%async_computation | async-start | bytes 1310720 | tf_op jit(solution)/shard_map/all_to_all | solution.py:18
  12.6 10.1 %copy-start.6 = (bf16[1024,64]{0,1:T(8,128)(2,1)S(1)}, bf16[1024,64]{0,1:T(8,128)(2,1)}, u32[]{:S(2)}) copy-start(bf16[1024,64]{0,1:T(8,128)(2,1)} %param.18) | copy-start | bytes 393220
  12.6 10.1 %copy-start.7 = (bf16[1024,64]{0,1:T(8,128)(2,1)S(1)}, bf16[1024,64]{0,1:T(8,128)(2,1)}, u32[]{:S(2)}) copy-start(bf16[1024,64]{0,1:T(8,128)(2,1)} %param.17) | copy-start | bytes 393220
  12.7 10.1 %copy-start.8 = (bf16[1024,64]{0,1:T(8,128)(2,1)S(1)}, bf16[1024,64]{0,1:T(8,128)(2,1)}, u32[]{:S(2)}) copy-start(bf16[1024,64]{0,1:T(8,128)(2,1)} %param.16) | copy-start | bytes 393220
  12.7 10.1 %copy-start.9 = (f32[1024]{0:T(1024)S(1)}, f32[1024]{0:T(1024)}, u32[]{:S(2)}) copy-start(f32[1024]{0:T(1024)} %param.15) | copy-start | bytes 12292
  53.2 3.2 %collective-permute-start = (bf16[2,16,11,128]{3,2,1,0:T(8,128)(2,1)S(1)}, bf16[2,16,11,128]{3,2,1,0:T(8,128)(2,1)S(1)}, u32[]{:S(2)}, u32[]{:S(2)}) collective-permute-start(bf16[2,16,11,128]{3,2,1,0:T(8,128)(2,1)S(1)} %pad_maximum_fusion.2), channel_id=1, source_target_pairs={{0,1},{1,0},{2,3},{3,2},{4,5},{5,4},{6,7},{7,6},{8,9},{9,8},{10,11... | collective-permute-start | bytes 270344 | tf_op jit(solution)/shard_map/ppermute | solution.py:67
  58.5 16.2 %copy-start.1 = (bf16[64,1024]{1,0:T(8,128)(2,1)S(1)}, bf16[64,1024]{1,0:T(8,128)(2,1)}, u32[]{:S(2)}) copy-start(bf16[64,1024]{1,0:T(8,128)(2,1)} %param.19) | copy-start | bytes 393220
  92.6 14.6 %copy-start.5 = (bf16[1024,256]{1,0:T(8,128)(2,1)S(1)}, bf16[1024,256]{1,0:T(8,128)(2,1)}, u32[]{:S(2)}) copy-start(bf16[1024,256]{1,0:T(8,128)(2,1)} %param.21) | copy-start | bytes 1572868
  106.9 1.0 copy-start.4
  106.9 1.0 copy-start.10
  110.4 5.0 %copy-start.3 = (s32[10]{0:T(128)S(1)}, s32[10]{0:T(128)}, u32[]{:S(2)}) copy-start(s32[10]{0:T(128)} %param.14) | copy-start | bytes 124
  110.4 14.5 %all-to-all-start.5 = ((bf16[16,10,2,1024]{3,2,1,0:T(2,128)(2,1)}), bf16[16,10,2,1024]{3,2,1,0:T(2,128)(2,1)S(1)}, u32[]{:S(2)}, u32[]{:S(2)}) async-start(bf16[16,10,2,1024]{3,2,1,0:T(2,128)(2,1)} %copy.120), calls=%async_computation.5 | async-start | bytes 1310720 | tf_op jit(solution)/shard_map/all_to_all | solution.py:22
  115.4 10.2 %copy-start.2 = (bf16[16,2,1024]{2,1,0:T(2,128)(2,1)S(1)}, bf16[16,2,1024]{2,1,0:T(2,128)(2,1)}, u32[]{:S(2)}) copy-start(bf16[16,2,1024]{2,1,0:T(2,128)(2,1)} %param.12) | copy-start | bytes 196612

commit v18 on v16

--- a/solution.py
+++ b/solution.py
@@ -104,10 +104,9 @@
     chosen = (
         jnp.arange(pixels.shape[0], dtype=jnp.int32)[:, None] == clear_index[None, :]
     ) & live_here[None, :]
-    placed = jnp.einsum(
-        "pc,csd->psd", chosen.astype(jnp.bfloat16), encoded, preferred_element_type=jnp.float32
-    ).astype(jnp.bfloat16)
+    source = jnp.argmax(chosen, axis=1).astype(jnp.int32)
     taken = jnp.any(chosen, axis=1)
+    placed = jnp.take(encoded, source, axis=0, mode="clip")
     return jnp.where(taken[:, None, None], placed, pixels)
 
 

time: 126 us -> 127 us (level)
  other arithmetic: 3.46 us -> 4.88 us
where the time goes in v18:
time: 127 us; the launch traced here: 126 us
  blocking collectives  74.7 us (59%)
  waiting for transfers between devices  18.6 us (15%)
  starting transfers between devices  16.2 us (13%)
  local copies, waits for them, and re-layouts  8.24 us (6%)
  other arithmetic  4.88 us (4%)
  matrix products  2.48 us (2%)
    all_to_all x1, blocking collectives, shards(): lax.all_to_all(payload.reshape(n_z, spec_mine, -1), 'z', 0, 0, tiled=True)  28.7 us
    all_to_all x1, blocking collectives, band_sum(): got = lax.all_to_all(part, 'band', 0, 0, tiled=True)  15.9 us
    all_to_all x1, blocking collectives, shards(): context_rows = lax.all_to_all(context, 'z', 0, 0, tiled=True)  15.8 us
    all_to_all x1, blocking collectives, band_gather(): return lax.all_to_all(sent, 'band', 0, 0, tiled=True)  14.3 us
    all_to_all x1, starting transfers between devices, band_gather(): return lax.all_to_all(sent, 'band', 0, 0, tiled=True)  9.26 us
    all_to_all x1, waiting for transfers between devices, band_gather(): return lax.all_to_all(sent, 'band', 0, 0, tiled=True)  9.05 us
    all_to_all x1, waiting for transfers between devices, band_sum(): got = lax.all_to_all(part, 'band', 0, 0, tiled=True)  8.79 us
    all_to_all x1, starting transfers between devices, band_sum(): got = lax.all_to_all(part, 'band', 0, 0, tiled=True)  4.98 us
  transfers between devices with their start and end apart: 3, of which 3 were waited for; matrix products, arithmetic and copies ran while one was open for 1% of the time, Pallas kernels for 0%

profile of v18, /device:TPU:2, one launch (start us, length us, event | category | flops | bytes accessed | tf_op | source)
XLA Modules:
  0.0 126.2 jit_solution(1696609658113028189)
XLA Ops:
  0.0 0.7 pad_clamp_fusion.1
  0.7 1.5 %gather_fusion = bf16[10,2,1024]{2,1,0:T(2,128)(2,1)S(1)} fusion(bf16[16,2,1024]{2,1,0:T(2,128)(2,1)} %param.12, s32[1024]{0:T(1024)S(1)} %pad_clamp_fusion.1), kind=kCustom, calls=%fused_computation | custom fusion | bytes 81960 | tf_op jit(solution)/shard_map/jit(_take)/gather | solution.py:41
  2.2 1.2 broadcast_in_dim.72
  3.4 9.3 %all-to-all-start = ((bf16[16,10,2,1024]{3,2,1,0:T(2,128)(2,1)}), bf16[16,10,2,1024]{3,2,1,0:T(2,128)(2,1)S(1)}, u32[]{:S(2)}, u32[]{:S(2)}) async-start(bf16[16,10,2,1024]{3,2,1,0:T(2,128)(2,1)} %broadcast_in_dim.72), calls=%async_computation | async-start | bytes 1310720 | tf_op jit(solution)/shard_map/all_to_all | solution.py:18
  13.4 9.1 %all-to-all-done = bf16[16,10,2,1024]{3,2,1,0:T(2,128)(2,1)S(1)} async-done(((bf16[16,10,2,1024]{3,2,1,0:T(2,128)(2,1)}), bf16[16,10,2,1024]{3,2,1,0:T(2,128)(2,1)S(1)}, u32[]{:S(2)}, u32[]{:S(2)}) %all-to-all-start) | async-done | bytes 655392 | tf_op jit(solution)/shard_map/all_to_all | solution.py:18
  22.8 0.4 convolution_bitcast_fusion
  23.7 28.7 %all_to_all.30 = bf16[16,2,1984]{2,1,0:T(2,128)(2,1)S(1)} all-to-all(bf16[16,2,1984]{2,1,0:T(2,128)(2,1)S(1)} %copy.89), channel_id=1, replica_groups=mesh['band'=16,'z'=16,'c'=2] {'z'}, dimensions={0} | all-to-all | bytes 253952 | tf_op jit(solution)/shard_map/all_to_all | solution.py:60
  53.2 1.9 %collective-permute-start = (bf16[2,16,11,128]{3,2,1,0:T(8,128)(2,1)S(1)}, bf16[2,16,11,128]{3,2,1,0:T(8,128)(2,1)S(1)}, u32[]{:S(2)}, u32[]{:S(2)}) collective-permute-start(bf16[2,16,11,128]{3,2,1,0:T(8,128)(2,1)S(1)} %pad_maximum_fusion.2), channel_id=1, source_target_pairs={{0,1},{1,0},{2,3},{3,2},{4,5},{5,4},{6,7},{7,6},{8,9},{9,8},{10,11... | collective-permute-start | bytes 270344 | tf_op jit(solution)/shard_map/ppermute | solution.py:67
  55.7 0.8 collective-permute-done
  57.3 0.4 select_reduce_fusion
  58.1 0.4 fusion.5
  58.8 15.8 %all_to_all.31 = bf16[16,2,640]{2,1,0:T(2,128)(2,1)S(1)} all-to-all(bf16[16,2,640]{2,1,0:T(2,128)(2,1)S(1)} %copy.102), channel_id=1, replica_groups=mesh['band'=16,'z'=16,'c'=2] {'z'}, dimensions={0} | all-to-all | bytes 81920 | tf_op jit(solution)/shard_map/all_to_all | solution.py:90
  75.1 0.7 copy.105
  75.7 15.9 %all_to_all.32 = bf16[16,10,2,1024]{3,2,1,0:T(2,128)(2,1)S(1)} all-to-all(bf16[16,10,2,1024]{3,2,1,0:T(2,128)(2,1)S(1)} %copy.105), channel_id=1, replica_groups=mesh['band'=16,'z'=16,'c'=2] {'band'}, dimensions={0} | all-to-all | bytes 1310720 | tf_op jit(solution)/shard_map/all_to_all | solution.py:22
  91.6 0.6 convert_reduce_fusion.1
  92.8 14.3 %all_to_all.33 = bf16[16,10,2,1024]{3,2,1,0:T(2,128)(2,1)S(1)} all-to-all(bf16[16,10,2,1024]{3,2,1,0:T(2,128)(2,1)S(1)} %broadcast_in_dim.81), channel_id=1, replica_groups=mesh['band'=16,'z'=16,'c'=2] {'band'}, dimensions={0} | all-to-all | bytes 1310720 | tf_op jit(solution)/shard_map/all_to_all | solution.py:18
  107.1 0.5 fusion.6
  108.0 1.5 %copy.107 = bf16[16,10,2,1024]{3,2,1,0:T(2,128)(2,1)} copy(bf16[16,10,2,1024]{3,0,2,1:T(8,128)(2,1)S(1)} %fusion.14) | data formatting | bytes 1310720 | tf_op jit(solution)/shard_map/bsjf,fd->bsjd/dot_general | solution.py:101
  109.5 5.0 %all-to-all-start.5 = ((bf16[16,10,2,1024]{3,2,1,0:T(2,128)(2,1)}), bf16[16,10,2,1024]{3,2,1,0:T(2,128)(2,1)S(1)}, u32[]{:S(2)}, u32[]{:S(2)}) async-start(bf16[16,10,2,1024]{3,2,1,0:T(2,128)(2,1)} %copy.107), calls=%async_computation.5 | async-start | bytes 1310720 | tf_op jit(solution)/shard_map/all_to_all | solution.py:22
  114.5 0.6 iota_reduce_fusion
  115.3 8.8 %all-to-all-done.5 = bf16[16,10,2,1024]{3,2,1,0:T(2,128)(2,1)S(1)} async-done(((bf16[16,10,2,1024]{3,2,1,0:T(2,128)(2,1)}), bf16[16,10,2,1024]{3,2,1,0:T(2,128)(2,1)S(1)}, u32[]{:S(2)}, u32[]{:S(2)}) %all-to-all-start.5) | async-done | bytes 655392 | tf_op jit(solution)/shard_map/all_to_all | solution.py:22
  124.1 0.6 convert_reduce_fusion
  124.7 0.7 gather_fusion.1
  125.4 0.8 broadcast_select_fusion
  (66 shorter events, 5.1 us)
Async XLA Ops:
  0.0 107.7 %copy-start = (bf16[256,1024]{1,0:T(8,128)(2,1)S(1)}, bf16[256,1024]{1,0:T(8,128)(2,1)}, u32[]{:S(2)}) copy-start(bf16[256,1024]{1,0:T(8,128)(2,1)} %param.23) | copy-start | bytes 1572868
  3.4 19.1 %all-to-all-start = ((bf16[16,10,2,1024]{3,2,1,0:T(2,128)(2,1)}), bf16[16,10,2,1024]{3,2,1,0:T(2,128)(2,1)S(1)}, u32[]{:S(2)}, u32[]{:S(2)}) async-start(bf16[16,10,2,1024]{3,2,1,0:T(2,128)(2,1)} %broadcast_in_dim.72), calls=%async_computation | async-start | bytes 1310720 | tf_op jit(solution)/shard_map/all_to_all | solution.py:18
  12.6 10.1 %copy-start.7 = (bf16[1024,64]{0,1:T(8,128)(2,1)S(1)}, bf16[1024,64]{0,1:T(8,128)(2,1)}, u32[]{:S(2)}) copy-start(bf16[1024,64]{0,1:T(8,128)(2,1)} %param.18) | copy-start | bytes 393220
  12.6 10.1 %copy-start.8 = (bf16[1024,64]{0,1:T(8,128)(2,1)S(1)}, bf16[1024,64]{0,1:T(8,128)(2,1)}, u32[]{:S(2)}) copy-start(bf16[1024,64]{0,1:T(8,128)(2,1)} %param.17) | copy-start | bytes 393220
  12.7 10.1 %copy-start.9 = (bf16[1024,64]{0,1:T(8,128)(2,1)S(1)}, bf16[1024,64]{0,1:T(8,128)(2,1)}, u32[]{:S(2)}) copy-start(bf16[1024,64]{0,1:T(8,128)(2,1)} %param.16) | copy-start | bytes 393220
  12.7 10.1 %copy-start.10 = (f32[1024]{0:T(1024)S(1)}, f32[1024]{0:T(1024)}, u32[]{:S(2)}) copy-start(f32[1024]{0:T(1024)} %param.15) | copy-start | bytes 12292
  53.2 3.2 %collective-permute-start = (bf16[2,16,11,128]{3,2,1,0:T(8,128)(2,1)S(1)}, bf16[2,16,11,128]{3,2,1,0:T(8,128)(2,1)S(1)}, u32[]{:S(2)}, u32[]{:S(2)}) collective-permute-start(bf16[2,16,11,128]{3,2,1,0:T(8,128)(2,1)S(1)} %pad_maximum_fusion.2), channel_id=1, source_target_pairs={{0,1},{1,0},{2,3},{3,2},{4,5},{5,4},{6,7},{7,6},{8,9},{9,8},{10,11... | collective-permute-start | bytes 270344 | tf_op jit(solution)/shard_map/ppermute | solution.py:67
  58.5 16.2 %copy-start.2 = (bf16[64,1024]{1,0:T(8,128)(2,1)S(1)}, bf16[64,1024]{1,0:T(8,128)(2,1)}, u32[]{:S(2)}) copy-start(bf16[64,1024]{1,0:T(8,128)(2,1)} %param.19) | copy-start | bytes 393220
  91.6 0.7 copy-start.3
  92.8 14.3 %copy-start.5 = (bf16[1024,256]{1,0:T(8,128)(2,1)S(1)}, bf16[1024,256]{1,0:T(8,128)(2,1)}, u32[]{:S(2)}) copy-start(bf16[1024,256]{1,0:T(8,128)(2,1)} %param.22) | copy-start | bytes 1572868
  92.8 14.3 %copy-start.6 = (bf16[1024,256]{1,0:T(8,128)(2,1)S(1)}, bf16[1024,256]{1,0:T(8,128)(2,1)}, u32[]{:S(2)}) copy-start(bf16[1024,256]{1,0:T(8,128)(2,1)} %param.21) | copy-start | bytes 1572868
  109.5 5.0 %copy-start.4 = (s32[10]{0:T(128)S(1)}, s32[10]{0:T(128)}, u32[]{:S(2)}) copy-start(s32[10]{0:T(128)} %param.14) | copy-start | bytes 124
  109.5 14.5 %all-to-all-start.5 = ((bf16[16,10,2,1024]{3,2,1,0:T(2,128)(2,1)}), bf16[16,10,2,1024]{3,2,1,0:T(2,128)(2,1)S(1)}, u32[]{:S(2)}, u32[]{:S(2)}) async-start(bf16[16,10,2,1024]{3,2,1,0:T(2,128)(2,1)} %copy.107), calls=%async_computation.5 | async-start | bytes 1310720 | tf_op jit(solution)/shard_map/all_to_all | solution.py:22
  114.5 10.9 %copy-start.1 = (bf16[16,2,1024]{2,1,0:T(2,128)(2,1)S(1)}, bf16[16,2,1024]{2,1,0:T(2,128)(2,1)}, u32[]{:S(2)}) copy-start(bf16[16,2,1024]{2,1,0:T(2,128)(2,1)} %param.12) | copy-start | bytes 196612

commit v19 on v16

--- a/solution.py
+++ b/solution.py
@@ -42,7 +42,9 @@
     slots_here, spec_here, width = kept.shape
     n_band = lax.axis_size("band")
     spec = n_band * spec_here
-    attn_in = normed(band_gather(kept), attn_gain)
+    sent = jnp.take(pixels, jnp.tile(clear_index, n_band), axis=0, mode="clip")
+    sent = sent.reshape((n_band,) + kept.shape)
+    attn_in = normed(lax.all_to_all(sent, "band", 0, 0, tiled=True), attn_gain)
     flat = attn_in.reshape(-1, width)
     heads_here = w_query.shape[1] // HD
 

time: 126 us -> 129 us (1.024)
  blocking collectives: 74.7 us -> 58.8 us
  waiting for transfers between devices: 19.3 us -> 29.1 us
  starting transfers between devices: 16.2 us -> 21.7 us
  local copies, waits for them, and re-layouts: 8.26 us -> 11.7 us
    all_to_all x1 -> x0, blocking collectives: 15.9 us -> none  [band_sum(): got = lax.all_to_all(part, 'band', 0, 0, tiled=True)]
    all_to_all x1 -> x2, waiting for transfers between devices: 9.43 us -> 19.3 us  [band_sum(): got = lax.all_to_all(part, 'band', 0, 0, tiled=True)]
    all_to_all x1 -> x2, starting transfers between devices: 4.98 us -> 10.5 us  [band_sum(): got = lax.all_to_all(part, 'band', 0, 0, tiled=True)]
    gather x0 -> x1, local copies, waits for them, and re-layouts: none -> 3.81 us  [shards(): sent = jnp.take(pixels, jnp.tile(clear_index, n_band), axis=0, mode='clip')]
  transfers between devices with their start and end apart: 3 -> 4, of which waited for: 3 -> 4; matrix products, arithmetic and copies ran while one was open for 1% -> 1% of each run, Pallas kernels for 0% -> 0%
where the time goes in v19:
time: 129 us; the launch traced here: 128 us
  blocking collectives  58.8 us (46%)
  waiting for transfers between devices  29.1 us (23%)
  starting transfers between devices  21.7 us (17%)
  local copies, waits for them, and re-layouts  11.7 us (9%)
  other arithmetic  2.75 us (2%)
  matrix products  2.63 us (2%)
    all_to_all x1, blocking collectives, shards(): lax.all_to_all(payload.reshape(n_z, spec_mine, -1), 'z', 0, 0, tiled=True)  28.7 us
    all_to_all x2, waiting for transfers between devices, band_sum(): got = lax.all_to_all(part, 'band', 0, 0, tiled=True)  19.3 us
    all_to_all x1, blocking collectives, shards(): context_rows = lax.all_to_all(context, 'z', 0, 0, tiled=True)  15.8 us
    all_to_all x1, blocking collectives, band_gather(): return lax.all_to_all(sent, 'band', 0, 0, tiled=True)  14.3 us
    all_to_all x2, starting transfers between devices, band_sum(): got = lax.all_to_all(part, 'band', 0, 0, tiled=True)  10.5 us
    all_to_all x1, starting transfers between devices, shards(): attn_in = normed(lax.all_to_all(sent, 'band', 0, 0, tiled=True), attn_gain)  9.26 us
    all_to_all x1, waiting for transfers between devices, shards(): attn_in = normed(lax.all_to_all(sent, 'band', 0, 0, tiled=True), attn_gain)  9.06 us
    gather x1, local copies, waits for them, and re-layouts, shards(): sent = jnp.take(pixels, jnp.tile(clear_index, n_band), axis=0, mode='clip')  3.81 us
  transfers between devices with their start and end apart: 4, of which 4 were waited for; matrix products, arithmetic and copies ran while one was open for 1% of the time, Pallas kernels for 0%

profile of v19, /device:TPU:2, one launch (start us, length us, event | category | flops | bytes accessed | tf_op | source)
XLA Modules:
  0.0 127.8 jit_solution(123953512401046331)
XLA Ops:
  0.0 0.7 eq.14
  0.8 3.8 %gather_fusion.1 = bf16[160,2,1024]{2,1,0:T(2,128)(2,1)} fusion(bf16[16,2,1024]{2,1,0:T(2,128)(2,1)} %param.12, s32[1024]{0:T(1024)S(1)} %pad_clamp_fusion), kind=kCustom, calls=%fused_computation.1 | custom fusion | bytes 1311360 | tf_op jit(solution)/shard_map/jit(_take)/gather | solution.py:45
  4.6 9.3 %all-to-all-start = ((bf16[16,10,2,1024]{3,2,1,0:T(2,128)(2,1)}), bf16[16,10,2,1024]{3,2,1,0:T(2,128)(2,1)S(1)}, u32[]{:S(2)}, u32[]{:S(2)}) async-start(bf16[16,10,2,1024]{3,2,1,0:T(2,128)(2,1)} %bitcast.2), calls=%async_computation | async-start | bytes 1310720 | tf_op jit(solution)/shard_map/all_to_all | solution.py:47
  14.7 9.1 %all-to-all-done = bf16[16,10,2,1024]{3,2,1,0:T(2,128)(2,1)S(1)} async-done(((bf16[16,10,2,1024]{3,2,1,0:T(2,128)(2,1)}), bf16[16,10,2,1024]{3,2,1,0:T(2,128)(2,1)S(1)}, u32[]{:S(2)}, u32[]{:S(2)}) %all-to-all-start) | async-done | bytes 655392 | tf_op jit(solution)/shard_map/all_to_all | solution.py:47
  24.1 0.4 convolution_bitcast_fusion
  25.0 28.7 %all_to_all.30 = bf16[16,2,1984]{2,1,0:T(2,128)(2,1)S(1)} all-to-all(bf16[16,2,1984]{2,1,0:T(2,128)(2,1)S(1)} %copy.104), channel_id=1, replica_groups=mesh['band'=16,'z'=16,'c'=2] {'z'}, dimensions={0} | all-to-all | bytes 253952 | tf_op jit(solution)/shard_map/all_to_all | solution.py:62
  54.5 1.9 %collective-permute-start = (bf16[2,16,11,128]{3,2,1,0:T(8,128)(2,1)S(1)}, bf16[2,16,11,128]{3,2,1,0:T(8,128)(2,1)S(1)}, u32[]{:S(2)}, u32[]{:S(2)}) collective-permute-start(bf16[2,16,11,128]{3,2,1,0:T(8,128)(2,1)S(1)} %pad_maximum_fusion.2), channel_id=1, source_target_pairs={{0,1},{1,0},{2,3},{3,2},{4,5},{5,4},{6,7},{7,6},{8,9},{9,8},{10,11... | collective-permute-start | bytes 270344 | tf_op jit(solution)/shard_map/ppermute | solution.py:69
  56.9 0.8 collective-permute-done
  58.5 0.4 select_reduce_fusion
  59.4 0.4 fusion.6
  60.1 15.8 %all_to_all.31 = bf16[16,2,640]{2,1,0:T(2,128)(2,1)S(1)} all-to-all(bf16[16,2,640]{2,1,0:T(2,128)(2,1)S(1)} %copy.117), channel_id=1, replica_groups=mesh['band'=16,'z'=16,'c'=2] {'z'}, dimensions={0} | all-to-all | bytes 81920 | tf_op jit(solution)/shard_map/all_to_all | solution.py:92
  76.3 1.5 %copy.120 = bf16[16,10,2,1024]{3,2,1,0:T(2,128)(2,1)} copy(bf16[16,10,2,1024]{3,0,2,1:T(8,128)(2,1)S(1)} %fusion.38) | data formatting | bytes 1310720 | tf_op jit(solution)/shard_map/bsjh,hd->bsjd/dot_general | solution.py:95
  77.8 5.7 %all-to-all-start.3 = ((bf16[16,10,2,1024]{3,2,1,0:T(2,128)(2,1)}), bf16[16,10,2,1024]{3,2,1,0:T(2,128)(2,1)S(1)}, u32[]{:S(2)}, u32[]{:S(2)}) async-start(bf16[16,10,2,1024]{3,2,1,0:T(2,128)(2,1)} %copy.120), calls=%async_computation.3 | async-start | bytes 1310720 | tf_op jit(solution)/shard_map/all_to_all | solution.py:22
  83.5 0.6 gather_fusion
  84.2 9.9 %all-to-all-done.3 = bf16[16,10,2,1024]{3,2,1,0:T(2,128)(2,1)S(1)} async-done(((bf16[16,10,2,1024]{3,2,1,0:T(2,128)(2,1)}), bf16[16,10,2,1024]{3,2,1,0:T(2,128)(2,1)S(1)}, u32[]{:S(2)}, u32[]{:S(2)}) %all-to-all-start.3) | async-done | bytes 655392 | tf_op jit(solution)/shard_map/all_to_all | solution.py:22
  94.1 0.6 convert_reduce_fusion.1
  95.3 14.3 %all_to_all.32 = bf16[16,10,2,1024]{3,2,1,0:T(2,128)(2,1)S(1)} all-to-all(bf16[16,10,2,1024]{3,2,1,0:T(2,128)(2,1)S(1)} %broadcast_in_dim.75), channel_id=1, replica_groups=mesh['band'=16,'z'=16,'c'=2] {'band'}, dimensions={0} | all-to-all | bytes 1310720 | tf_op jit(solution)/shard_map/all_to_all | solution.py:18
  109.6 0.5 fusion.7
  110.1 0.3 fusion.15
  110.5 1.5 %copy.122 = bf16[16,10,2,1024]{3,2,1,0:T(2,128)(2,1)} copy(bf16[16,10,2,1024]{3,0,2,1:T(8,128)(2,1)S(1)} %fusion.15) | data formatting | bytes 1310720 | tf_op jit(solution)/shard_map/bsjf,fd->bsjd/dot_general | solution.py:103
  112.0 4.8 %all-to-all-start.5 = ((bf16[16,10,2,1024]{3,2,1,0:T(2,128)(2,1)}), bf16[16,10,2,1024]{3,2,1,0:T(2,128)(2,1)S(1)}, u32[]{:S(2)}, u32[]{:S(2)}) async-start(bf16[16,10,2,1024]{3,2,1,0:T(2,128)(2,1)} %copy.122), calls=%async_computation.5 | async-start | bytes 1310720 | tf_op jit(solution)/shard_map/all_to_all | solution.py:22
  116.9 9.4 %all-to-all-done.5 = bf16[16,10,2,1024]{3,2,1,0:T(2,128)(2,1)S(1)} async-done(((bf16[16,10,2,1024]{3,2,1,0:T(2,128)(2,1)}), bf16[16,10,2,1024]{3,2,1,0:T(2,128)(2,1)S(1)}, u32[]{:S(2)}, u32[]{:S(2)}) %all-to-all-start.5) | async-done | bytes 655392 | tf_op jit(solution)/shard_map/all_to_all | solution.py:22
  126.4 0.6 convert_reduce_fusion
  127.1 0.7 copy.125
  (68 shorter events, 5.0 us)
Async XLA Ops:
  0.0 110.1 %copy-start = (bf16[256,1024]{1,0:T(8,128)(2,1)S(1)}, bf16[256,1024]{1,0:T(8,128)(2,1)}, u32[]{:S(2)}) copy-start(bf16[256,1024]{1,0:T(8,128)(2,1)} %param.23) | copy-start | bytes 1572868
  4.6 19.1 %all-to-all-start = ((bf16[16,10,2,1024]{3,2,1,0:T(2,128)(2,1)}), bf16[16,10,2,1024]{3,2,1,0:T(2,128)(2,1)S(1)}, u32[]{:S(2)}, u32[]{:S(2)}) async-start(bf16[16,10,2,1024]{3,2,1,0:T(2,128)(2,1)} %bitcast.2), calls=%async_computation | async-start | bytes 1310720 | tf_op jit(solution)/shard_map/all_to_all | solution.py:47
  13.9 10.1 %copy-start.7 = (bf16[1024,64]{0,1:T(8,128)(2,1)S(1)}, bf16[1024,64]{0,1:T(8,128)(2,1)}, u32[]{:S(2)}) copy-start(bf16[1024,64]{0,1:T(8,128)(2,1)} %param.18) | copy-start | bytes 393220
  13.9 10.1 %copy-start.8 = (bf16[1024,64]{0,1:T(8,128)(2,1)S(1)}, bf16[1024,64]{0,1:T(8,128)(2,1)}, u32[]{:S(2)}) copy-start(bf16[1024,64]{0,1:T(8,128)(2,1)} %param.17) | copy-start | bytes 393220
  13.9 10.1 %copy-start.9 = (bf16[1024,64]{0,1:T(8,128)(2,1)S(1)}, bf16[1024,64]{0,1:T(8,128)(2,1)}, u32[]{:S(2)}) copy-start(bf16[1024,64]{0,1:T(8,128)(2,1)} %param.16) | copy-start | bytes 393220
  13.9 10.1 %copy-start.10 = (f32[1024]{0:T(1024)S(1)}, f32[1024]{0:T(1024)}, u32[]{:S(2)}) copy-start(f32[1024]{0:T(1024)} %param.15) | copy-start | bytes 12292
  54.5 3.2 %collective-permute-start = (bf16[2,16,11,128]{3,2,1,0:T(8,128)(2,1)S(1)}, bf16[2,16,11,128]{3,2,1,0:T(8,128)(2,1)S(1)}, u32[]{:S(2)}, u32[]{:S(2)}) collective-permute-start(bf16[2,16,11,128]{3,2,1,0:T(8,128)(2,1)S(1)} %pad_maximum_fusion.2), channel_id=1, source_target_pairs={{0,1},{1,0},{2,3},{3,2},{4,5},{5,4},{6,7},{7,6},{8,9},{9,8},{10,11... | collective-permute-start | bytes 270344 | tf_op jit(solution)/shard_map/ppermute | solution.py:69
  59.8 16.2 %copy-start.2 = (bf16[64,1024]{1,0:T(8,128)(2,1)S(1)}, bf16[64,1024]{1,0:T(8,128)(2,1)}, u32[]{:S(2)}) copy-start(bf16[64,1024]{1,0:T(8,128)(2,1)} %param.19) | copy-start | bytes 393220
  77.8 5.7 %copy-start.4 = (s32[10]{0:T(128)S(1)}, s32[10]{0:T(128)}, u32[]{:S(2)}) copy-start(s32[10]{0:T(128)} %param.14) | copy-start | bytes 124
  77.8 5.7 %copy-start.1 = (bf16[16,2,1024]{2,1,0:T(2,128)(2,1)S(1)}, bf16[16,2,1024]{2,1,0:T(2,128)(2,1)}, u32[]{:S(2)}) copy-start(bf16[16,2,1024]{2,1,0:T(2,128)(2,1)} %param.12) | copy-start | bytes 196612
  77.8 16.2 %all-to-all-start.3 = ((bf16[16,10,2,1024]{3,2,1,0:T(2,128)(2,1)}), bf16[16,10,2,1024]{3,2,1,0:T(2,128)(2,1)S(1)}, u32[]{:S(2)}, u32[]{:S(2)}) async-start(bf16[16,10,2,1024]{3,2,1,0:T(2,128)(2,1)} %copy.120), calls=%async_computation.3 | async-start | bytes 1310720 | tf_op jit(solution)/shard_map/all_to_all | solution.py:22
  83.5 11.3 %copy-start.3 = (f32[1024]{0:T(1024)S(1)}, f32[1024]{0:T(1024)}, u32[]{:S(2)}) copy-start(f32[1024]{0:T(1024)} %param.20) | copy-start | bytes 12292
  95.3 14.3 %copy-start.5 = (bf16[1024,256]{1,0:T(8,128)(2,1)S(1)}, bf16[1024,256]{1,0:T(8,128)(2,1)}, u32[]{:S(2)}) copy-start(bf16[1024,256]{1,0:T(8,128)(2,1)} %param.22) | copy-start | bytes 1572868
  95.3 14.3 %copy-start.6 = (bf16[1024,256]{1,0:T(8,128)(2,1)S(1)}, bf16[1024,256]{1,0:T(8,128)(2,1)}, u32[]{:S(2)}) copy-start(bf16[1024,256]{1,0:T(8,128)(2,1)} %param.21) | copy-start | bytes 1572868
  112.0 14.4 %all-to-all-start.5 = ((bf16[16,10,2,1024]{3,2,1,0:T(2,128)(2,1)}), bf16[16,10,2,1024]{3,2,1,0:T(2,128)(2,1)S(1)}, u32[]{:S(2)}, u32[]{:S(2)}) async-start(bf16[16,10,2,1024]{3,2,1,0:T(2,128)(2,1)} %copy.122), calls=%async_computation.5 | async-start | bytes 1310720 | tf_op jit(solution)/shard_map/all_to_all | solution.py:22
